TPU v7x, 1024 devices: a whole 8x8x8 slice. The times are simulated.
1024 devices in a mesh: box: 128 (over x, y, core), ang: 8 (over z).
Axes of the slice: x: 8, y: 8, z: 8, core: 2. Of those that a mesh axis runs over, the one named last changes fastest.
Arguments:
- children: bfloat16 [131072, 2, 1024], P(('box', 'ang')), may hold values from -6 to 6
- interp_band: float32 [2048, 6], replicated, may hold values from -0.5 to 1
- band_start: int32 [2048], replicated, may hold values from 0 to 1018, as said below
- shift_angle: float32 [8, 2048], replicated, may hold values from -3.140625 to 3.140625
- far_box: int32 [16384, 27], P('box'), may hold values from 0 to 16383, as said below
- far_class: int32 [16384, 27], P('box'), may hold values from 0 to 315
- far_count: int32 [16384], P('box'), may hold values from 9 to 27, as said below
- translation: float32 [316, 2, 2048], replicated, may hold values from -0.3 to 0.3
Outputs:
- local_field: float32 [131072, 2, 1024], P(('box', 'ang'))
Inputs may be any that keep to these rules, and one draw needn't show every extreme that they name: `band_start`: every band lies inside the child-level samples. far_box[p, l] differs from p by 2 to 16. `far_count`: each aligned block of 128 parents (the parents of one index of box) holds at least one parent with all 27 slots live.
All inputs are finite; a program needn't handle non-finite values.
Results may differ from a plain program's by a relative error of at most 0.0063.
Values may be sent and summed in bfloat16 or wider, within the bound.
No kernel may reach another device: no remote copies, remote signals or barrier semaphores. Data moves between devices by JAX's collectives and lax.ppermute only.
A program may use at most 64 MiB of HBM per device.

v0:
```python
import jax
import jax.numpy as jnp
from jax import lax
from jax.sharding import PartitionSpec as P

K_LOW = 1024


def extended(shard, sides, width):
    for axis, dim in sides:
        peers, length = (lax.axis_size(axis), shard.shape[dim])
        up = [(i, (i + 1) % peers) for i in range(peers - 1)]
        down = [(j, i) for i, j in up]
        last = lax.slice_in_dim(shard, length - width, length, axis=dim)
        leading = lax.slice_in_dim(shard, 0, width, axis=dim)
        before = lax.ppermute(last, axis, up)
        after = lax.ppermute(leading, axis, down)
        shard = jnp.concatenate([before, shard, after], axis=dim)
    return shard


def build_interp(interp_band, band_start):
    low_ids = jnp.arange(interp_band.shape[0] // 2 * 0 + K_LOW, dtype=jnp.int32)
    dense = jnp.zeros((K_LOW, interp_band.shape[0]), jnp.float32)
    for column in range(interp_band.shape[1]):
        target = band_start + column
        dense = dense + jnp.where(
            low_ids[:, None] == target[None, :], interp_band[:, column][None, :], jnp.float32(0.0)
        )
    return dense.astype(jnp.bfloat16)


def shift_up(values, cosines, sines):
    real_part = values[:, :, 0, :] * cosines - values[:, :, 1, :] * sines
    imag_part = values[:, :, 0, :] * sines + values[:, :, 1, :] * cosines
    return jnp.stack([real_part, imag_part], axis=2)


def shift_down(values, cosines, sines):
    real_in = values[:, None, 0, :]
    imag_in = values[:, None, 1, :]
    real_part = real_in * cosines + imag_in * sines
    imag_part = imag_in * cosines - real_in * sines
    return jnp.stack([real_part, imag_part], axis=2)


def translate(patterns, operators, targets, classes, counts):
    gathered = patterns[targets].astype(jnp.float32)
    chosen = operators[classes]
    slots = jnp.arange(classes.shape[1], dtype=jnp.int32)
    live = (slots[None, :] < counts[:, None]).astype(jnp.float32)[:, :, None]
    real_part = jnp.sum(
        live * (chosen[:, :, 0] * gathered[:, :, 0] - chosen[:, :, 1] * gathered[:, :, 1]), axis=1
    )
    imag_part = jnp.sum(
        live * (chosen[:, :, 0] * gathered[:, :, 1] + chosen[:, :, 1] * gathered[:, :, 0]), axis=1
    )
    return jnp.stack([real_part, imag_part], axis=1)


def body(
    children, interp_band, band_start, shift_angle, far_box, far_class, far_count, translation
):
    high_width = interp_band.shape[0]
    low_width = children.shape[2]
    parents_here = children.shape[0] // 8
    interp = build_interp(interp_band, band_start)
    raised = jnp.dot(children.reshape(-1, low_width), interp, preferred_element_type=jnp.float32)
    raised = raised.reshape(-1, 8, 2, high_width)
    cosines = jnp.cos(shift_angle)
    sines = jnp.sin(shift_angle)
    parent = jnp.sum(shift_up(raised, cosines, sines), axis=1).astype(jnp.bfloat16)
    ang_count = lax.axis_size("ang")
    grouped = lax.all_to_all(parent, "ang", split_axis=2, concat_axis=0, tiled=True)
    group_rows = grouped.shape[0]
    padded = extended(grouped, (("box", 0),), parents_here)
    part_width = high_width // ang_count
    first_sample = lax.axis_index("ang") * part_width
    operators = lax.dynamic_slice_in_dim(translation, first_sample, part_width, 2)
    anchor = lax.axis_index("box") * group_rows - parents_here
    targets = far_box - anchor
    local_part = translate(padded, operators, targets, far_class, far_count).astype(jnp.bfloat16)
    local = lax.all_to_all(local_part, "ang", split_axis=0, concat_axis=2, tiled=True)
    spread = shift_down(local.astype(jnp.float32), cosines, sines).astype(jnp.bfloat16)
    result = jnp.dot(spread.reshape(-1, high_width), interp.T, preferred_element_type=jnp.float32)
    return result.reshape(-1, 2, low_width)


def solution(mesh):
    return jax.shard_map(
        body,
        mesh=mesh,
        in_specs=(
            P(("box", "ang"), None, None),
            P(),
            P(),
            P(),
            P("box", None),
            P("box", None),
            P("box"),
            P(),
        ),
        out_specs=P(("box", "ang"), None, None),
        check_vma=False,
    )
```

profile of v0, /device:TPU:14, one launch (start us, length us, event | category | flops | bytes accessed | tf_op | source)
XLA Modules:
  0.0 129.4 jit_solution(11762957735142899304)
XLA Ops:
  0.0 1.1 fusion.13
  1.1 0.7 broadcast_add_fusion.4
  1.8 1.2 reshape.143
  3.1 8.9 %convolution_bitcast_fusion = f32[256,2048]{1,0:T(8,128)} fusion(bf16[256,1024]{1,0:T(8,128)(2,1)S(1)} %reshape.143, f32[2048]{0:T(1024)S(1)} %bitcast.77, s32[2048]{0:T(1024)S(1)} %get-tuple-element.28, f32[2048]{0:T(1024)S(1)} %bitcast.79, s32[2048]{0:T(1024)S(1)} %get-tuple-element.29, f32[2048]{0:T(1024)S(1)} %bitcast.71, ...), kind=kOutput, calls=%fused_computation.17 | convolution fusion | flops 1111490560 | bytes 2719744 | tf_op jit(solution)/shard_map/dot_general | solution.py:68
  12.0 2.5 %reshape.144 = f32[16,8,2,2048]{3,2,1,0:T(2,128)S(1)} reshape(f32[256,2048]{1,0:T(8,128)} %convolution_bitcast_fusion) | data formatting | bytes 4194304 | tf_op jit(solution)/shard_map/reshape | solution.py:69
  14.8 2.6 %multiply_subtract_fusion.1 = (f32[16,8,1,2048]{3,2,1,0:T(1,128)S(1)}, f32[16,8,1,2048]{3,2,1,0:T(1,128)S(1)}) fusion(f32[16,8,2,2048]{3,2,1,0:T(2,128)S(1)} %reshape.144, f32[8,2048]{1,0:T(8,128)S(1)} %get-tuple-element.18, f32[8,2048]{1,0:T(8,128)S(1)} %get-tuple-element.17), kind=kLoop, calls=%fused_computation.25 | loop fusion | flops 1572864 | bytes 4325376 | tf_op jit(solution)/shard_map/sub | solution.py:34
  17.4 2.2 %maximum_reduce_fusion = bf16[16,2,2048]{2,1,0:T(2,128)(2,1)S(1)} fusion(f32[16,8,1,2048]{3,2,1,0:T(1,128)S(1)} %get-tuple-element.10, f32[16,8,1,2048]{3,2,1,0:T(1,128)S(1)} %get-tuple-element.9), kind=kLoop, calls=%fused_computation.18 | loop fusion | flops 983040 | bytes 2228224 | tf_op jit(solution)/shard_map/reduce_sum | solution.py:72
  19.5 0.8 copy.47
  20.3 1.7 %reshape.169 = bf16[8,2,4096]{2,1,0:T(2,128)(2,1)} reshape(bf16[2048,2,16]{2,1,0:T(2,128)(2,1)S(1)} %bitcast.60) | data formatting | bytes 262144
  22.0 16.7 %all-to-all-start = ((bf16[8,2,4096]{2,1,0:T(2,128)(2,1)}), bf16[8,2,4096]{2,1,0:T(2,128)(2,1)S(1)}, u32[]{:S(2)}, u32[]{:S(2)}) async-start(bf16[8,2,4096]{2,1,0:T(2,128)(2,1)} %reshape.169), calls=%async_computation | async-start | bytes 262144 | tf_op jit(solution)/shard_map/all_to_all | solution.py:74
  39.1 1.3 %constant_dynamic-slice_fusion = f32[316,2,256]{2,1,0:T(2,128)S(1)} fusion(f32[316,2,2048]{2,1,0:T(2,128)} %param.15, s32[]{:T(128)S(6)} %select_n.28), kind=kLoop, calls=%fused_computation.48 | loop fusion | bytes 1294340 | tf_op jit(solution)/shard_map/dynamic_slice | solution.py:79
  40.8 7.1 %all-to-all-done = bf16[8,2,4096]{2,1,0:T(2,128)(2,1)S(1)} async-done(((bf16[8,2,4096]{2,1,0:T(2,128)(2,1)}), bf16[8,2,4096]{2,1,0:T(2,128)(2,1)S(1)}, u32[]{:S(2)}, u32[]{:S(2)}) %all-to-all-start) | async-done | bytes 131104 | tf_op jit(solution)/shard_map/all_to_all | solution.py:74
  47.8 0.7 reshape.170
  49.2 1.9 %collective-permute-start = (bf16[16,2,256]{2,1,0:T(2,128)(2,1)S(1)}, bf16[16,2,256]{2,1,0:T(2,128)(2,1)S(1)}, u32[]{:S(2)}, u32[]{:S(2)}) collective-permute-start(bf16[16,2,256]{2,1,0:T(2,128)(2,1)S(1)} %bitcast.67), channel_id=1, source_target_pairs={{0,8},{8,16},{16,24},{24,32},{32,40},{40,48},{48,56},{56,64},{64,7... | collective-permute-start | bytes 49160 | tf_op jit(solution)/shard_map/ppermute | solution.py:16
  51.2 5.9 %collective-permute-start.1 = (bf16[16,2,256]{2,1,0:T(2,128)(2,1)S(1)}, bf16[16,2,256]{2,1,0:T(2,128)(2,1)S(1)}, u32[]{:S(2)}, u32[]{:S(2)}) collective-permute-start(bf16[16,2,256]{2,1,0:T(2,128)(2,1)S(1)} %bitcast.68), channel_id=1, source_target_pairs={{8,0},{16,8},{24,16},{32,24},{40,32},{48,40},{56,48},{64,56},{72,6... | collective-permute-start | bytes 49160 | tf_op jit(solution)/shard_map/ppermute | solution.py:17
  57.1 13.7 %gather_fusion = f32[3456,2,256]{2,1,0:T(2,128)} fusion(f32[316,2,256]{2,1,0:T(2,128)S(1)} %constant_dynamic-slice_fusion, s32[4096]{0:T(1024)S(1)} %pad_clamp_fusion.1), kind=kCustom, calls=%fused_computation | custom fusion | bytes 14169600 | tf_op jit(solution)/shard_map/gather | solution.py:49
  70.8 0.6 copy.62
  71.9 13.6 %gather_fusion.1 = bf16[3456,2,256]{2,1,0:T(2,128)(2,1)} fusion(bf16[160,2,256]{2,1,0:T(2,128)(2,1)S(1)} %pad_maximum_fusion, s32[4096]{0:T(1024)S(1)} %pad_clamp_fusion), kind=kCustom, calls=%fused_computation.1 | custom fusion | bytes 7091712 | tf_op jit(solution)/shard_map/gather | solution.py:48
  85.5 7.4 %convert.23 = f32[128,27,2,256]{3,2,1,0:T(2,128)} convert(bf16[128,27,2,256]{3,2,1,0:T(2,128)(2,1)} %bitcast.57) | non-fusion elementwise | flops 1769472 | bytes 10616832 | tf_op jit(solution)/shard_map/convert_element_type | solution.py:48
  92.9 15.2 %multiply_add_fusion = (f32[128,27,1,256]{3,2,1,0:T(1,128)S(1)}, f32[128,27,1,256]{3,2,1,0:T(1,128)S(1)}) fusion(f32[128,27,2,256]{3,2,1,0:T(2,128)} %convert.23, f32[128,27,2,256]{3,2,1,0:T(2,128)} %bitcast.56), kind=kLoop, calls=%fused_computation.15 | loop fusion | flops 5308416 | bytes 21233664 | tf_op jit(solution)/shard_map/add | solution.py:56
  108.1 0.8 fusion.3
  109.1 11.5 %all_to_all.27 = bf16[128,2,256]{2,1,0:T(2,128)(2,1)S(1)} all-to-all(bf16[128,2,256]{2,1,0:T(2,128)(2,1)S(1)} %copy.56), channel_id=1, replica_groups=mesh['box'=128,'ang'=8] {'ang'}, dimensions={0} | all-to-all | bytes 262144 | tf_op jit(solution)/shard_map/all_to_all | solution.py:83
  120.9 6.7 %fusion = f32[128,2,1024]{2,0,1:T(8,128)S(1)} fusion(bf16[128,1,2048]{2,0,1:T(8,128)(2,1)S(1)} %get-tuple-element.12, bf16[128,1,2048]{2,0,1:T(8,128)(2,1)S(1)} %get-tuple-element.11, f32[2048]{0:T(1024)S(1)} %bitcast.78, s32[2048]{0:T(1024)S(1)} %get-tuple-element.28, f32[2048]{0:T(1024)S(1)} %bitcast.80, s32[2048]{0:T(1024)S(1)} %get-tuple-element.29, ...), kind=kOutput, calls=%fused_computation.9 | convolution fusion | flops 1112014848 | bytes 2195456 | tf_op jit(solution)/shard_map/dot_general | solution.py:85
  127.6 1.8 %copy.59 = f32[128,2,1024]{2,1,0:T(2,128)} copy(f32[128,2,1024]{2,0,1:T(8,128)S(1)} %fusion) | data formatting | bytes 2097152 | tf_op jit(solution)/shard_map/dot_general | solution.py:85
  (35 shorter events, 2.5 us)
Async XLA Ops:
  3.1 11.5 %copy-start = (f32[8,2048]{1,0:T(8,128)S(1)}, f32[8,2048]{1,0:T(8,128)}, u32[]{:S(2)}) copy-start(f32[8,2048]{1,0:T(8,128)} %param.11) | copy-start | bytes 196612
  12.0 26.7 %copy-start.1 = (s32[128,27]{0,1:T(8,128)S(1)}, s32[128,27]{0,1:T(8,128)}, u32[]{:S(2)}) copy-start(s32[128,27]{0,1:T(8,128)} %param.12) | copy-start | bytes 41476
  12.0 27.0 %copy-start.2 = (s32[128,27]{0,1:T(8,128)S(1)}, s32[128,27]{0,1:T(8,128)}, u32[]{:S(2)}) copy-start(s32[128,27]{0,1:T(8,128)} %param.13) | copy-start | bytes 41476
  12.0 28.7 %copy-start.4 = (s32[128]{0:T(128)S(1)}, s32[128]{0:T(128)}, u32[]{:S(2)}) copy-start(s32[128]{0:T(128)} %param.14) | copy-start | bytes 1540
  22.0 25.8 %all-to-all-start = ((bf16[8,2,4096]{2,1,0:T(2,128)(2,1)}), bf16[8,2,4096]{2,1,0:T(2,128)(2,1)S(1)}, u32[]{:S(2)}, u32[]{:S(2)}) async-start(bf16[8,2,4096]{2,1,0:T(2,128)(2,1)} %reshape.169), calls=%async_computation | async-start | bytes 262144 | tf_op jit(solution)/shard_map/all_to_all | solution.py:74
  49.2 22.4 %collective-permute-start = (bf16[16,2,256]{2,1,0:T(2,128)(2,1)S(1)}, bf16[16,2,256]{2,1,0:T(2,128)(2,1)S(1)}, u32[]{:S(2)}, u32[]{:S(2)}) collective-permute-start(bf16[16,2,256]{2,1,0:T(2,128)(2,1)S(1)} %bitcast.67), channel_id=1, source_target_pairs={{0,8},{8,16},{16,24},{24,32},{32,40},{40,48},{48,56},{56,64},{64,7... | collective-permute-start | bytes 49160 | tf_op jit(solution)/shard_map/ppermute | solution.py:16
  51.2 20.4 %collective-permute-start.1 = (bf16[16,2,256]{2,1,0:T(2,128)(2,1)S(1)}, bf16[16,2,256]{2,1,0:T(2,128)(2,1)S(1)}, u32[]{:S(2)}, u32[]{:S(2)}) collective-permute-start(bf16[16,2,256]{2,1,0:T(2,128)(2,1)S(1)} %bitcast.68), channel_id=1, source_target_pairs={{8,0},{16,8},{24,16},{32,24},{40,32},{48,40},{56,48},{64,56},{72,6... | collective-permute-start | bytes 49160 | tf_op jit(solution)/shard_map/ppermute | solution.py:17
  108.1 12.8 %copy-start.3 = (s32[2048]{0:T(1024)S(1)}, s32[2048]{0:T(1024)}, u32[]{:S(2)}) copy-start(s32[2048]{0:T(1024)} %param.10) | copy-start | bytes 24580
where the time goes:
time: 131 us; the launch traced here: 129 us
  local copies, waits for them, and re-layouts  41.1 us (31%)
  other arithmetic  29.3 us (22%)
  starting transfers between devices  24.5 us (19%)
  matrix products  15.6 us (12%)
  blocking collectives  11.5 us (9%)
  waiting for transfers between devices  7.08 us (5%)
    all_to_all x1, starting transfers between devices, body(): lax.all_to_all(parent, 'ang', split_axis=2, concat_axis=0, tiled=True)  16.7 us
    add x1, other arithmetic, translate(): chosen[:, :, 0] * gathered[:, :, 1] + chosen[:, :, 1] * gathered[:, :, 0]  15.2 us
    gather x1, local copies, waits for them, and re-layouts, translate(): chosen = operators[classes]  13.7 us
    gather x1, local copies, waits for them, and re-layouts, translate(): gathered = patterns[targets].astype(jnp.float32)  13.6 us
    all_to_all x1, blocking collectives, body(): lax.all_to_all(local_part, 'ang', split_axis=0, concat_axis=2, tiled=True)  11.5 us
    dot_general x1, matrix products, body(): jnp.dot(children.reshape(-1, low_width), interp, preferred_element_type=j...  8.91 us
    convert_element_type x1, other arithmetic, translate(): gathered = patterns[targets].astype(jnp.float32)  7.35 us
    all_to_all x1, waiting for transfers between devices, body(): lax.all_to_all(parent, 'ang', split_axis=2, concat_axis=0, tiled=True)  7.07 us
  transfers between devices with their start and end apart: 3, of which 1 were waited for; matrix products, arithmetic and copies ran while one was open for 13% of the time, Pallas kernels for 0%

commit v1 on v0

v1 whole, which is shorter than its diff:
```python
import jax
import jax.numpy as jnp
from jax import lax
from jax.sharding import PartitionSpec as P

K_LOW = 1024
REACH = 16


def build_interp(interp_band, band_start):
    low_ids = jnp.arange(K_LOW, dtype=jnp.int32)
    dense = jnp.zeros((K_LOW, interp_band.shape[0]), jnp.float32)
    for column in range(interp_band.shape[1]):
        target = band_start + column
        dense = dense + jnp.where(
            low_ids[:, None] == target[None, :], interp_band[:, column][None, :], jnp.float32(0.0)
        )
    return dense.astype(jnp.bfloat16)


def shift_up(values, cosines, sines):
    real_part = values[:, :, 0, :] * cosines - values[:, :, 1, :] * sines
    imag_part = values[:, :, 0, :] * sines + values[:, :, 1, :] * cosines
    return jnp.stack([real_part, imag_part], axis=2)


def shift_down(values, cosines, sines):
    real_in = values[:, None, 0, :]
    imag_in = values[:, None, 1, :]
    real_part = real_in * cosines + imag_in * sines
    imag_part = imag_in * cosines - real_in * sines
    return jnp.stack([real_part, imag_part], axis=2)


def translate(window, translation, rel_box, classes, counts):
    rows, far = classes.shape
    width = window.shape[0]
    nclass = translation.shape[0]
    slots = jnp.arange(far, dtype=jnp.int32)
    live = slots[None, :] < counts[:, None]
    box_t = rel_box.T.reshape(-1)
    cls_t = classes.T.reshape(-1)
    live_t = live.T.reshape(-1)
    pick_box = jnp.logical_and(
        box_t[:, None] == jnp.arange(width, dtype=jnp.int32)[None, :], live_t[:, None]
    ).astype(jnp.bfloat16)
    pick_cls = (cls_t[:, None] == jnp.arange(nclass, dtype=jnp.int32)[None, :]).astype(jnp.bfloat16)
    pick_cls = jnp.concatenate([pick_cls, pick_cls], axis=1)
    high = translation.astype(jnp.bfloat16)
    low = (translation - high.astype(jnp.float32)).astype(jnp.bfloat16)
    op_re = jnp.concatenate([high[:, 0], low[:, 0]], axis=0)
    op_im = jnp.concatenate([high[:, 1], low[:, 1]], axis=0)
    f32 = jnp.float32
    t_re = jnp.dot(pick_cls, op_re, preferred_element_type=f32)
    t_im = jnp.dot(pick_cls, op_im, preferred_element_type=f32)
    p_re = jnp.dot(pick_box, window[:, 0], preferred_element_type=f32)
    p_im = jnp.dot(pick_box, window[:, 1], preferred_element_type=f32)
    real_part = (t_re * p_re - t_im * p_im).reshape(far, rows, -1).sum(axis=0)
    imag_part = (t_re * p_im + t_im * p_re).reshape(far, rows, -1).sum(axis=0)
    return jnp.stack([real_part, imag_part], axis=1)


def make_body(box_count, ang_count):
    devices = box_count * ang_count

    def body(
        children, interp_band, band_start, shift_angle, far_box, far_class, far_count, translation
    ):
        high_width = interp_band.shape[0]
        low_width = children.shape[2]
        parents_here = children.shape[0] // 8
        assert parents_here >= REACH
        interp = build_interp(interp_band, band_start)
        raised = jnp.dot(children.reshape(-1, low_width), interp, preferred_element_type=jnp.float32)
        raised = raised.reshape(-1, 8, 2, high_width)
        cosines = jnp.cos(shift_angle)
        sines = jnp.sin(shift_angle)
        parent = jnp.sum(shift_up(raised, cosines, sines), axis=1).astype(jnp.bfloat16)
        axes = ("box", "ang")
        up = [(i, i + 1) for i in range(devices - 1)]
        down = [(i + 1, i) for i in range(devices - 1)]
        before = lax.ppermute(parent[parents_here - REACH:], axes, up)
        after = lax.ppermute(parent[:REACH], axes, down)
        window = jnp.concatenate([before, parent, after], axis=0)
        ang = lax.axis_index("ang")
        device = lax.axis_index("box") * ang_count + ang
        first = ang * parents_here
        my_box = lax.dynamic_slice_in_dim(far_box, first, parents_here, 0)
        my_class = lax.dynamic_slice_in_dim(far_class, first, parents_here, 0)
        my_count = lax.dynamic_slice_in_dim(far_count, first, parents_here, 0)
        rel_box = my_box - (device * parents_here - REACH)
        local = translate(window, translation, rel_box, my_class, my_count).astype(jnp.bfloat16)
        spread = shift_down(local.astype(jnp.float32), cosines, sines).astype(jnp.bfloat16)
        result = jnp.dot(spread.reshape(-1, high_width), interp.T, preferred_element_type=jnp.float32)
        return result.reshape(-1, 2, low_width)

    return body


def solution(mesh):
    return jax.shard_map(
        make_body(mesh.shape["box"], mesh.shape["ang"]),
        mesh=mesh,
        in_specs=(
            P(("box", "ang"), None, None),
            P(),
            P(),
            P(),
            P("box", None),
            P("box", None),
            P("box"),
            P(),
        ),
        out_specs=P(("box", "ang"), None, None),
        check_vma=False,
    )
```

time: 131 us -> 81.4 us (0.62)
  local copies, waits for them, and re-layouts: 41.1 us -> 15.9 us
  other arithmetic: 29.3 us -> 17 us
  blocking collectives: 11.5 us -> 0 us
  matrix products: 15.6 us -> 23.8 us
  waiting for transfers between devices: 7.08 us -> 0.01 us
    gather x2 -> x0, local copies, waits for them, and re-layouts: 27.3 us -> none  [the longest x1 13.7 us: translate(): chosen = operators[classes]]
    all_to_all x1 -> x0, starting transfers between devices: 16.7 us -> none  [body(): lax.all_to_all(parent, 'ang', split_axis=2, concat_axis=0, tiled=True)]
    ppermute x2, starting transfers between devices: 7.85 us -> 23.6 us  [the longest x1 21.5 us: body(): after = lax.ppermute(parent[:REACH], axes, down)]
    add x1 -> x0, other arithmetic: 15.2 us -> none  [translate(): chosen[:, :, 0] * gathered[:, :, 1] + chosen[:, :, 1] * gathered[:, :, 0]]
    all_to_all x1 -> x0, blocking collectives: 11.5 us -> none  [body(): lax.all_to_all(local_part, 'ang', split_axis=0, concat_axis=2, tiled=True)]
    dot_general x0 -> x4, matrix products: none -> 7.31 us  [the longest x1 3.5 us: translate(): p_im = jnp.dot(pick_box, window[:, 1], preferred_element_type=f32)]
    all_to_all x1 -> x0, waiting for transfers between devices: 7.07 us -> none  [body(): lax.all_to_all(parent, 'ang', split_axis=2, concat_axis=0, tiled=True)]
    reduce_sum x1 -> x2, other arithmetic: 0.77 us -> 3.6 us  [the longest x1 2.8 us: translate(): imag_part = (t_re * p_im + t_im * p_re).reshape(far, rows, -1).sum(axis=0)]
  transfers between devices with their start and end apart: 3 -> 2, of which waited for: 1 -> 0; matrix products, arithmetic and copies ran while one was open for 13% -> 19% of each run, Pallas kernels for 0% -> 0%
where the time goes in v1:
time: 81.4 us; the launch traced here: 80.7 us
  matrix products  23.8 us (29%)
  starting transfers between devices  23.6 us (29%)
  other arithmetic  17 us (21%)
  local copies, waits for them, and re-layouts  15.9 us (20%)
    ppermute x1, starting transfers between devices, body(): after = lax.ppermute(parent[:REACH], axes, down)  21.5 us
    dot_general x1, matrix products, body(): jnp.dot(children.reshape(-1, low_width), interp, preferred_element_type=j...  8.95 us
    dot_general x1, matrix products, body(): jnp.dot(spread.reshape(-1, high_width), interp.T, preferred_element_type=...  7.57 us
    convert_element_type x1, other arithmetic, translate(): low = (translation - high.astype(jnp.float32)).astype(jnp.bfloat16)  5.22 us
    unnamed x41, local copies, waits for them, and re-layouts  4.87 us
    dot_general x1, matrix products, translate(): p_im = jnp.dot(pick_box, window[:, 1], preferred_element_type=f32)  3.5 us
    reduce_sum x1, other arithmetic, translate(): imag_part = (t_re * p_im + t_im * p_re).reshape(far, rows, -1).sum(axis=0)  2.8 us
    sub x1, other arithmetic, shift_up(): real_part = values[:, :, 0, :] * cosines - values[:, :, 1, :] * sines  2.55 us
  transfers between devices with their start and end apart: 2, of which 0 were waited for; matrix products, arithmetic and copies ran while one was open for 19% of the time, Pallas kernels for 0%

profile of v1, /device:TPU:14, one launch (start us, length us, event | category | flops | bytes accessed | tf_op | source)
XLA Modules:
  0.0 80.7 jit_solution(18222283055794541103)
XLA Ops:
  0.0 1.1 %fusion.34 = (f32[8,2048]{1,0:T(8,128)S(1)}, f32[8,2048]{1,0:T(8,128)S(1)}) fusion(f32[8,2048]{1,0:T(8,128)} %param.11), kind=kLoop, calls=%fused_computation.70 | loop fusion | bytes 196608 | tf_op jit(solution)/shard_map/cos | solution.py:76
  1.1 1.3 %reshape.132 = bf16[256,1024]{1,0:T(8,128)(2,1)S(1)} reshape(bf16[128,2,1024]{2,1,0:T(2,128)(2,1)} %param.8) | data formatting | bytes 1048576 | tf_op jit(solution)/shard_map/reshape | solution.py:74
  2.4 1.1 %fusion.35 = (f32[2048,1]{0,1:T(1,128)S(1)}, f32[2048,1]{0,1:T(1,128)S(1)}, f32[2048,1]{0,1:T(1,128)S(1)}, f32[2048,1]{0,1:T(1,128)S(1)}, f32[2048,1]{0,1:T(1,128)S(1)}, /*index=5*/f32[2048,1]{0,1:T(1,128)S(1)}) fusion(f32[2048,6]{0,1:T(8,128)} %param.9), kind=kLoop, calls=%fused_computation.71 | loop fusion | bytes 98304 | tf_op jit(solution)/shard_map/slice | solution.py:16
  3.6 0.7 broadcast_add_fusion.4
  4.9 9.0 %convolution_bitcast_fusion = f32[256,2048]{1,0:T(8,128)} fusion(bf16[256,1024]{1,0:T(8,128)(2,1)S(1)} %reshape.132, f32[2048]{0:T(1024)S(1)} %bitcast.62, s32[2048]{0:T(1024)S(1)} %get-tuple-element.30, f32[2048]{0:T(1024)S(1)} %bitcast.64, s32[2048]{0:T(1024)S(1)} %get-tuple-element.31, f32[2048]{0:T(1024)S(1)} %bitcast.56, ...), kind=kOutput, calls=%fused_computation.13 | convolution fusion | flops 1111490560 | bytes 2719744 | tf_op jit(solution)/shard_map/dot_general | solution.py:74
  13.9 2.5 %reshape.133 = f32[16,8,2,2048]{3,2,1,0:T(2,128)S(1)} reshape(f32[256,2048]{1,0:T(8,128)} %convolution_bitcast_fusion) | data formatting | bytes 4194304 | tf_op jit(solution)/shard_map/reshape | solution.py:75
  16.4 2.6 %multiply_subtract_fusion.1 = (f32[16,8,1,2048]{3,2,1,0:T(1,128)S(1)}, f32[16,8,1,2048]{3,2,1,0:T(1,128)S(1)}) fusion(f32[16,8,2,2048]{3,2,1,0:T(2,128)S(1)} %reshape.133, f32[8,2048]{1,0:T(8,128)S(1)} %get-tuple-element.20, f32[8,2048]{1,0:T(8,128)S(1)} %get-tuple-element.19), kind=kLoop, calls=%fused_computation.34 | loop fusion | flops 1572864 | bytes 4325376 | tf_op jit(solution)/shard_map/sub | solution.py:22
  19.0 2.2 %maximum_reduce_fusion = bf16[16,2,2048]{2,1,0:T(2,128)(2,1)S(1)} fusion(f32[16,8,1,2048]{3,2,1,0:T(1,128)S(1)} %get-tuple-element.12, f32[16,8,1,2048]{3,2,1,0:T(1,128)S(1)} %get-tuple-element.11), kind=kLoop, calls=%fused_computation.22 | loop fusion | flops 983040 | bytes 2228224 | tf_op jit(solution)/shard_map/reduce_sum | solution.py:78
  21.2 21.5 %collective-permute-start.1 = (bf16[16,2,2048]{2,1,0:T(2,128)(2,1)S(1)}, bf16[16,2,2048]{2,1,0:T(2,128)(2,1)S(1)}, u32[]{:S(2)}, u32[]{:S(2)}) collective-permute-start(bf16[16,2,2048]{2,1,0:T(2,128)(2,1)S(1)} %maximum_reduce_fusion), channel_id=1, source_target_pairs={{1,0},{2,1},{3,2},{4,3},{5,4},{6,5},{7,6},{8,7},{9,8},{10,9},{11,1... | collective-permute-start | bytes 393224 | tf_op jit(solution)/shard_map/ppermute | solution.py:83
  42.6 2.1 %collective-permute-start = (bf16[16,2,2048]{2,1,0:T(2,128)(2,1)S(1)}, bf16[16,2,2048]{2,1,0:T(2,128)(2,1)S(1)}, u32[]{:S(2)}, u32[]{:S(2)}) collective-permute-start(bf16[16,2,2048]{2,1,0:T(2,128)(2,1)S(1)} %maximum_reduce_fusion), channel_id=1, source_target_pairs={{0,1},{1,2},{2,3},{3,4},{4,5},{5,6},{6,7},{7,8},{8,9},{9,10},{10,1... | collective-permute-start | bytes 393224 | tf_op jit(solution)/shard_map/ppermute | solution.py:82
  44.7 5.2 %subtract_convert_fusion = bf16[316,2,2048]{2,0,1:T(8,128)(2,1)S(1)} fusion(f32[316,2,2048]{2,1,0:T(2,128)} %param.15), kind=kLoop, calls=%fused_computation.7 | loop fusion | flops 5177344 | bytes 7766016 | tf_op jit(solution)/shard_map/convert_element_type | solution.py:50
  50.0 4.3 %copy.33 = bf16[316,2,2048]{2,0,1:T(8,128)(2,1)} copy(f32[316,2,2048]{2,1,0:T(2,128)S(1)} %bitcast.49) | data formatting | bytes 7766016 | tf_op args[7]
  55.0 2.2 %slice_bitcast_fusion.2 = (bf16[316,2048]{1,0:T(8,128)(2,1)S(1)}, bf16[316,2048]{1,0:T(8,128)(2,1)S(1)}, bf16[316,2048]{1,0:T(8,128)(2,1)S(1)}, bf16[316,2048]{1,0:T(8,128)(2,1)S(1)}) fusion(bf16[316,2,2048]{2,0,1:T(8,128)(2,1)S(1)} %subtract_convert_fusion, bf16[316,2,2048]{2,0,1:T(8,128)(2,1)} %copy.33), kind=kLoop, calls=%fused_computation.25 | loop fusion | bytes 10354688 | tf_op jit(solution)/shard_map/squeeze | solution.py:51
  57.2 1.6 %fusion.6 = f32[432,2048]{1,0:T(8,128)S(1)} fusion(bf16[316,2048]{1,0:T(8,128)(2,1)S(1)} %get-tuple-element.10, bf16[316,2048]{1,0:T(8,128)(2,1)S(1)} %get-tuple-element.32, pred[432,316]{1,0:T(8,128)(4,1)S(1)} %iota_compare_fusion.6), kind=kOutput, calls=%fused_computation.18 | convolution fusion | flops 1123756672 | bytes 6264128 | tf_op jit(solution)/shard_map/dot_general | solution.py:55
  58.8 1.6 %fusion.2 = f32[432,2048]{1,0:T(8,128)S(1)} fusion(bf16[316,2048]{1,0:T(8,128)(2,1)S(1)} %get-tuple-element.9, bf16[316,2048]{1,0:T(8,128)(2,1)S(1)} %get-tuple-element.33, pred[432,316]{1,0:T(8,128)(4,1)S(1)} %iota_compare_fusion.6), kind=kOutput, calls=%fused_computation.14 | convolution fusion | flops 1123756672 | bytes 6264128 | tf_op jit(solution)/shard_map/dot_general | solution.py:54
  60.9 0.5 fusion.33
  61.5 0.7 fusion.18
  62.2 3.5 %multiply_subtract_fusion = (f32[432,2048]{1,0:T(8,128)S(1)}, f32[432,2048]{1,0:T(8,128)}) fusion(f32[432,2048]{1,0:T(8,128)S(1)} %fusion.6, f32[432,2048]{1,0:T(8,128)S(1)} %fusion.2, f32[432,2048]{1,0:T(8,128)S(1)} %fusion.18, bf16[48,1,2048]{2,1,0:T(2,128)(2,1)S(1)} %get-tuple-element.15, s32[432]{0:T(512)} %copy-done.3, pred[432]{0:T(512)(128)(4,1)} %copy-done.16), kind=kOutput, calls=%fused_computation.12 | convolution fusion | flops 90284544 | bytes 17893488 | tf_op jit(solution)/shard_map/dot_general | solution.py:57
  65.7 2.8 %reduce_sum.29 = bf16[16,2048]{1,0:T(8,128)(2,1)} reduce(f32[27,16,2048]{2,1,0:T(8,128)} %bitcast.51, f32[]{:T(128)} %constant.12.clone.1), dimensions={0}, to_apply=%region_2.3 | reduce | flops 851968 | bytes 3604484 | tf_op jit(solution)/shard_map/reduce_sum | solution.py:59
  68.5 0.8 reduce_sum.28
  69.3 0.9 %maximum_convert_fusion = f32[16,2,2048]{2,0,1:T(8,128)S(1)} fusion(bf16[16,1,2048]{2,0,1:T(8,128)(2,1)} %bitcast.52, bf16[16,1,2048]{2,0,1:T(8,128)(2,1)} %bitcast.53), kind=kLoop, calls=%fused_computation.49 | loop fusion | flops 131072 | bytes 393216 | tf_op jit(solution)/shard_map/convert_element_type | solution.py:93
  70.2 1.1 %fusion.13 = (bf16[128,1,2048]{2,0,1:T(8,128)(2,1)S(1)}, bf16[128,1,2048]{2,0,1:T(8,128)(2,1)S(1)}) fusion(f32[8,2048]{1,0:T(8,128)} %copy-done.2, f32[16,2048]{1,0:T(8,128)S(1)} %get-tuple-element.18, f32[8,2048]{1,0:T(8,128)} %copy-done.1, f32[16,2048]{1,0:T(8,128)S(1)} %get-tuple-element.17), kind=kLoop, calls=%fused_computation.36 | loop fusion | flops 2097152 | bytes 1441792 | tf_op jit(solution)/shard_map/add | solution.py:30
  71.3 7.6 %fusion = f32[128,2,1024]{2,0,1:T(8,128)S(1)} fusion(bf16[128,1,2048]{2,0,1:T(8,128)(2,1)S(1)} %get-tuple-element.14, bf16[128,1,2048]{2,0,1:T(8,128)(2,1)S(1)} %get-tuple-element.13, f32[2048]{0:T(1024)} %bitcast.63, s32[2048]{0:T(1024)} %copy-done.14, f32[2048]{0:T(1024)} %bitcast.65, s32[2048]{0:T(1024)} %copy-done.15, f32[2048]{0:T(1024)} %bitcast.57, ...), kind=kOutput, calls=%fused_computation.9 | convolution fusion | flops 1112014848 | bytes 2195456 | tf_op jit(solution)/shard_map/dot_general | solution.py:94
  78.9 1.8 %copy.18 = f32[128,2,1024]{2,1,0:T(2,128)} copy(f32[128,2,1024]{2,0,1:T(8,128)S(1)} %fusion) | data formatting | bytes 2097152 | tf_op jit(solution)/shard_map/dot_general | solution.py:94
  (53 shorter events, 1.8 us)
Async XLA Ops:
  0.0 54.3 %copy-start = (s32[128,27]{0,1:T(8,128)S(1)}, s32[128,27]{0,1:T(8,128)}, u32[]{:S(2)}) copy-start(s32[128,27]{0,1:T(8,128)} %param.13) | copy-start | bytes 41476
  1.1 15.3 %copy-start.1 = (f32[8,2048]{1,0:T(8,128)}, f32[8,2048]{1,0:T(8,128)S(1)}, u32[]{:S(2)}) copy-start(f32[8,2048]{1,0:T(8,128)S(1)} %get-tuple-element.19) | copy-start | bytes 196612
  1.1 15.3 %copy-start.2 = (f32[8,2048]{1,0:T(8,128)}, f32[8,2048]{1,0:T(8,128)S(1)}, u32[]{:S(2)}) copy-start(f32[8,2048]{1,0:T(8,128)S(1)} %get-tuple-element.20) | copy-start | bytes 196612
  3.5 0.8 copy-start.5
  3.6 0.8 copy-start.6
  3.6 0.8 copy-start.7
  3.6 0.8 copy-start.8
  3.6 0.8 copy-start.9
  3.6 0.8 copy-start.10
  4.3 0.6 copy-start.11
  4.3 0.6 copy-start.12
  4.3 0.6 copy-start.13
  4.3 0.6 copy-start.14
  4.3 0.6 copy-start.15
  19.0 31.0 %slice-start = ((s8[5177344]{0:T(1024)(128)(4,1)}), s8[4194304]{0:T(1024)(128)(4,1)S(1)}, s32[]{:S(2)}) async-start(s8[5177344]{0:T(1024)(128)(4,1)} %bitcast.48), calls=%async_computation | async-start | bytes 8388608
  21.1 28.8 %slice-start.1 = ((s8[5177344]{0:T(1024)(128)(4,1)}), s8[983040]{0:T(1024)(128)(4,1)S(1)}, s32[]{:S(2)}) async-start(s8[5177344]{0:T(1024)(128)(4,1)} %bitcast.48), calls=%async_computation.1 | async-start | bytes 1966080
  21.2 39.2 %collective-permute-start.1 = (bf16[16,2,2048]{2,1,0:T(2,128)(2,1)S(1)}, bf16[16,2,2048]{2,1,0:T(2,128)(2,1)S(1)}, u32[]{:S(2)}, u32[]{:S(2)}) collective-permute-start(bf16[16,2,2048]{2,1,0:T(2,128)(2,1)S(1)} %maximum_reduce_fusion), channel_id=1, source_target_pairs={{1,0},{2,1},{3,2},{4,3},{5,4},{6,5},{7,6},{8,7},{9,8},{10,9},{11,1... | collective-permute-start | bytes 393224 | tf_op jit(solution)/shard_map/ppermute | solution.py:83
  42.6 17.8 %collective-permute-start = (bf16[16,2,2048]{2,1,0:T(2,128)(2,1)S(1)}, bf16[16,2,2048]{2,1,0:T(2,128)(2,1)S(1)}, u32[]{:S(2)}, u32[]{:S(2)}) collective-permute-start(bf16[16,2,2048]{2,1,0:T(2,128)(2,1)S(1)} %maximum_reduce_fusion), channel_id=1, source_target_pairs={{0,1},{1,2},{2,3},{3,4},{4,5},{5,6},{6,7},{7,8},{8,9},{9,10},{10,1... | collective-permute-start | bytes 393224 | tf_op jit(solution)/shard_map/ppermute | solution.py:82
  50.0 4.6 %copy-start.4 = (s32[128,27]{0,1:T(8,128)S(1)}, s32[128,27]{0,1:T(8,128)}, u32[]{:S(2)}) copy-start(s32[128,27]{0,1:T(8,128)} %param.12) | copy-start | bytes 41476
  50.0 4.8 %copy-start.17 = (s32[128]{0:T(128)S(1)}, s32[128]{0:T(128)}, u32[]{:S(2)}) copy-start(s32[128]{0:T(128)} %param.14) | copy-start | bytes 1540
  54.8 6.7 %copy-start.3 = (s32[432]{0:T(512)}, s32[432]{0:T(512)S(1)}, u32[]{:S(2)}) copy-start(s32[432]{0:T(512)S(1)} %eq.112) | copy-start | bytes 5188
  55.0 6.6 %copy-start.16 = (pred[432]{0:T(512)(128)(4,1)}, pred[432]{0:T(512)(128)(4,1)S(1)}, u32[]{:S(2)}) copy-start(pred[432]{0:T(512)(128)(4,1)S(1)} %lt.30) | copy-start | bytes 1300

commit v2 on v1

v2 whole, which is shorter than its diff:
```python
import jax
import jax.numpy as jnp
from jax import lax
from jax.sharding import PartitionSpec as P

K_LOW = 1024
REACH = 16


def build_interp(interp_band, band_start):
    low_ids = jnp.arange(K_LOW, dtype=jnp.int32)
    dense = jnp.zeros((K_LOW, interp_band.shape[0]), jnp.float32)
    for column in range(interp_band.shape[1]):
        target = band_start + column
        dense = dense + jnp.where(
            low_ids[:, None] == target[None, :], interp_band[:, column][None, :], jnp.float32(0.0)
        )
    return dense.astype(jnp.bfloat16)


def translate(window, translation, rel_box, classes, counts):
    rows, far = classes.shape
    width = window.shape[1]
    nclass = translation.shape[0]
    slots = jnp.arange(far, dtype=jnp.int32)
    live = slots[None, :] < counts[:, None]
    box_t = rel_box.T.reshape(-1)
    cls_t = classes.T.reshape(-1)
    live_t = live.T.reshape(-1)
    pick_box = jnp.logical_and(
        box_t[:, None] == jnp.arange(width, dtype=jnp.int32)[None, :], live_t[:, None]
    ).astype(jnp.bfloat16)
    pick_cls = (cls_t[:, None] == jnp.arange(nclass, dtype=jnp.int32)[None, :]).astype(jnp.bfloat16)
    pick_cls = jnp.concatenate([pick_cls, pick_cls], axis=1)
    op_re = split_parts(translation[:, 0])
    op_im = split_parts(translation[:, 1])
    f32 = jnp.float32
    t_re = jnp.dot(pick_cls, op_re, preferred_element_type=f32)
    t_im = jnp.dot(pick_cls, op_im, preferred_element_type=f32)
    p_re = jnp.dot(pick_box, window[0], preferred_element_type=f32)
    p_im = jnp.dot(pick_box, window[1], preferred_element_type=f32)
    real_part = (t_re * p_re - t_im * p_im).reshape(far, rows, -1).sum(axis=0)
    imag_part = (t_re * p_im + t_im * p_re).reshape(far, rows, -1).sum(axis=0)
    return real_part, imag_part


def split_parts(values):
    high = values.astype(jnp.bfloat16)
    low = (values - high.astype(jnp.float32)).astype(jnp.bfloat16)
    return jnp.concatenate([high, low], axis=0)


def make_body(box_count, ang_count):
    devices = box_count * ang_count

    def body(
        children, interp_band, band_start, shift_angle, far_box, far_class, far_count, translation
    ):
        high_width = interp_band.shape[0]
        low_width = children.shape[2]
        parents_here = children.shape[0] // 8
        assert parents_here >= REACH
        f32 = jnp.float32
        interp = lax.optimization_barrier(build_interp(interp_band, band_start))
        raised_re = jnp.dot(children[:, 0], interp, preferred_element_type=f32).reshape(-1, 8, high_width)
        raised_im = jnp.dot(children[:, 1], interp, preferred_element_type=f32).reshape(-1, 8, high_width)
        cosines = jnp.cos(shift_angle)
        sines = jnp.sin(shift_angle)
        parent_re = jnp.sum(raised_re * cosines - raised_im * sines, axis=1)
        parent_im = jnp.sum(raised_re * sines + raised_im * cosines, axis=1)
        parent = jnp.stack([parent_re, parent_im]).astype(jnp.bfloat16)
        axes = ("box", "ang")
        up = [(i, i + 1) for i in range(devices - 1)]
        down = [(i + 1, i) for i in range(devices - 1)]
        before = lax.ppermute(parent[:, parents_here - REACH:], axes, up)
        after = lax.ppermute(parent[:, :REACH], axes, down)
        window = jnp.concatenate([before, parent, after], axis=1)
        ang = lax.axis_index("ang")
        device = lax.axis_index("box") * ang_count + ang
        first = ang * parents_here
        my_box = lax.dynamic_slice_in_dim(far_box, first, parents_here, 0)
        my_class = lax.dynamic_slice_in_dim(far_class, first, parents_here, 0)
        my_count = lax.dynamic_slice_in_dim(far_count, first, parents_here, 0)
        rel_box = my_box - (device * parents_here - REACH)
        local_re, local_im = translate(window, translation, rel_box, my_class, my_count)
        local_re = lax.reduce_precision(local_re, exponent_bits=8, mantissa_bits=7)[:, None]
        local_im = lax.reduce_precision(local_im, exponent_bits=8, mantissa_bits=7)[:, None]
        spread_re = (local_re * cosines + local_im * sines).astype(jnp.bfloat16).reshape(-1, high_width)
        spread_im = (local_im * cosines - local_re * sines).astype(jnp.bfloat16).reshape(-1, high_width)
        contract = (((1,), (1,)), ((), ()))
        out_re = lax.dot_general(spread_re, interp, contract, preferred_element_type=f32)
        out_im = lax.dot_general(spread_im, interp, contract, preferred_element_type=f32)
        return jnp.stack([out_re, out_im], axis=1)

    return body


def solution(mesh):
    return jax.shard_map(
        make_body(mesh.shape["box"], mesh.shape["ang"]),
        mesh=mesh,
        in_specs=(
            P(("box", "ang"), None, None),
            P(),
            P(),
            P(),
            P("box", None),
            P("box", None),
            P("box"),
            P(),
        ),
        out_specs=P(("box", "ang"), None, None),
        check_vma=False,
    )
```

time: 81.4 us -> 78.6 us (0.966)
  matrix products: 23.8 us -> 17.1 us
  local copies, waits for them, and re-layouts: 15.9 us -> 18.3 us
  other arithmetic: 17 us -> 19.1 us
    slice x1 -> x2, local copies, waits for them, and re-layouts: 0.55 us -> 11.6 us  [the longest x1 10.8 us: translate(): op_re = split_parts(translation[:, 0])]
    dot_general x4 -> x6, matrix products: 20.7 us -> 12.2 us  [the longest x1 4.15 us: body(): lax.dot_general(spread_im, interp, contract, preferred_element_type=f32)]
    convert_element_type x2, other arithmetic: 6.11 us -> 11.8 us  [the longest x1 7.17 us: build_interp(): return dense.astype(jnp.bfloat16)]
    unnamed x41 -> x32, local copies, waits for them, and re-layouts: 4.87 us -> 0.24 us
    reshape x2 -> x0, local copies, waits for them, and re-layouts: 3.77 us -> none  [the longest x1 2.49 us: body(): raised = raised.reshape(-1, 8, 2, high_width)]
    convert_element_type x0 -> x1, local copies, waits for them, and re-layouts: none -> 2.94 us  [split_parts(): high = values.astype(jnp.bfloat16)]
    reduce_precision x0 -> x2, other arithmetic: none -> 2.63 us  [the longest x1 1.57 us: body(): lax.reduce_precision(local_im, exponent_bits=8, mantissa_bits=7)[:, None]]
    sub x1 -> x0, other arithmetic: 2.55 us -> none  [shift_up(): real_part = values[:, :, 0, :] * cosines - values[:, :, 1, :] * sines]
  transfers between devices with their start and end apart: 2 -> 2, of which waited for: 0 -> 0; matrix products, arithmetic and copies ran while one was open for 19% -> 31% of each run, Pallas kernels for 0% -> 0%
where the time goes in v2:
time: 78.6 us; the launch traced here: 78.3 us
  starting transfers between devices  23.4 us (30%)
  other arithmetic  19.1 us (24%)
  local copies, waits for them, and re-layouts  18.3 us (23%)
  matrix products  17.1 us (22%)
    ppermute x1, starting transfers between devices, body(): after = lax.ppermute(parent[:, :REACH], axes, down)  21.3 us
    slice x1, local copies, waits for them, and re-layouts, translate(): op_re = split_parts(translation[:, 0])  10.8 us
    convert_element_type x1, other arithmetic, build_interp(): return dense.astype(jnp.bfloat16)  7.17 us
    convert_element_type x1, other arithmetic, split_parts(): low = (values - high.astype(jnp.float32)).astype(jnp.bfloat16)  4.58 us
    dot_general x1, matrix products, body(): lax.dot_general(spread_im, interp, contract, preferred_element_type=f32)  4.15 us
    dot_general x1, matrix products, translate(): t_im = jnp.dot(pick_cls, op_im, preferred_element_type=f32)  3.37 us
    dot_general x1, matrix products, translate(): p_im = jnp.dot(pick_box, window[1], preferred_element_type=f32)  3.34 us
    convert_element_type x1, local copies, waits for them, and re-layouts, split_parts(): high = values.astype(jnp.bfloat16)  2.94 us
  transfers between devices with their start and end apart: 2, of which 0 were waited for; matrix products, arithmetic and copies ran while one was open for 31% of the time, Pallas kernels for 0%

profile of v2, /device:TPU:14, one launch (start us, length us, event | category | flops | bytes accessed | tf_op | source)
XLA Modules:
  0.0 78.3 jit_solution(1228757459425202799)
XLA Ops:
  0.0 1.1 %fusion.38 = (f32[2048,1]{0,1:T(1,128)S(1)}, f32[2048,1]{0,1:T(1,128)S(1)}, f32[2048,1]{0,1:T(1,128)S(1)}, f32[2048,1]{0,1:T(1,128)S(1)}, f32[2048,1]{0,1:T(1,128)S(1)}, /*index=5*/f32[2048,1]{0,1:T(1,128)S(1)}) fusion(f32[2048,6]{0,1:T(8,128)} %param.9), kind=kLoop, calls=%fused_computation.75 | loop fusion | bytes 98304 | tf_op jit(solution)/shard_map/slice | solution.py:16
  1.1 0.7 broadcast_add_fusion.4
  1.8 7.2 %add_convert_fusion = bf16[1024,2048]{1,0:T(8,128)(2,1)S(1)} fusion(f32[2048]{0:T(1024)S(1)} %bitcast.82, s32[2048]{0:T(1024)S(1)} %get-tuple-element.24, f32[2048]{0:T(1024)S(1)} %bitcast.83, s32[2048]{0:T(1024)S(1)} %get-tuple-element.25, f32[2048]{0:T(1024)S(1)} %bitcast.79, s32[2048]{0:T(1024)S(1)} %get-tuple-element.22, f32[2048]{0:T(1024)S(1)} %bitcast.80, ...), kind=kLoop, calls=%fused_computation | loop fusion | flops 37748736 | bytes 4292608 | tf_op jit(solution)/shard_map/convert_element_type | solution.py:18
  9.0 0.7 fusion.36
  9.8 0.2 fusion.37
  10.1 0.7 convolution_bitcast_fusion.1
  10.8 0.2 copy-done.1
  11.0 1.5 %subtract_reduce_fusion = (bf16[16,2048]{1,0:T(8,128)(2,1)S(1)}, bf16[16,2048]{1,0:T(8,128)(2,1)S(1)}) fusion(f32[16,8,2048]{2,1,0:T(8,128)S(1)} %convolution_bitcast_fusion.1, f32[8,2048]{1,0:T(8,128)S(1)} %get-tuple-element.14, f32[8,2048]{1,0:T(8,128)S(1)} %get-tuple-element.13, bf16[1024,2048]{1,0:T(8,128)(2,1)S(1)} %add_convert_fusion, ...), kind=kOutput, calls=%fused_computation.32 | convolution fusion | flops 538902528 | bytes 5767168 | tf_op jit(solution)/shard_map/dot_general | solution.py:66
  12.6 21.3 %collective-permute-start.1 = (bf16[2,16,2048]{2,1,0:T(8,128)(2,1)S(1)}, bf16[2,16,2048]{2,1,0:T(8,128)(2,1)S(1)}, u32[]{:S(2)}, u32[]{:S(2)}) collective-permute-start(bf16[2,16,2048]{2,1,0:T(8,128)(2,1)S(1)} %pad_maximum_fusion.2), channel_id=1, source_target_pairs={{1,0},{2,1},{3,2},{4,3},{5,4},{6,5},{7,6},{8,7},{9,8},{10,9},{11,1... | collective-permute-start | bytes 393224 | tf_op jit(solution)/shard_map/ppermute | solution.py:76
  33.9 2.1 %collective-permute-start = (bf16[2,16,2048]{2,1,0:T(8,128)(2,1)S(1)}, bf16[2,16,2048]{2,1,0:T(8,128)(2,1)S(1)}, u32[]{:S(2)}, u32[]{:S(2)}) collective-permute-start(bf16[2,16,2048]{2,1,0:T(8,128)(2,1)S(1)} %pad_maximum_fusion.2), channel_id=1, source_target_pairs={{0,1},{1,2},{2,3},{3,4},{4,5},{5,6},{6,7},{7,8},{8,9},{9,10},{10,1... | collective-permute-start | bytes 393224 | tf_op jit(solution)/shard_map/ppermute | solution.py:75
  36.0 10.8 %fusion.35 = (f32[316,1,2048]{2,1,0:T(1,128)S(1)}, f32[316,1,2048]{2,1,0:T(1,128)}) fusion(f32[316,2,2048]{2,1,0:T(2,128)} %param.15), kind=kLoop, calls=%fused_computation.72 | loop fusion | bytes 10354688 | tf_op jit(solution)/shard_map/slice | solution.py:35
  46.8 4.6 %subtract_convert_fusion = (bf16[316,2048]{1,0:T(8,128)(2,1)}, bf16[316,2048]{1,0:T(8,128)(2,1)S(1)}) fusion(f32[316,1,2048]{2,1,0:T(1,128)} %get-tuple-element.10, f32[316,1,2048]{2,1,0:T(1,128)S(1)} %get-tuple-element.9), kind=kLoop, calls=%fused_computation.11 | loop fusion | flops 5177344 | bytes 7766016 | tf_op jit(solution)/shard_map/convert_element_type | solution.py:49
  51.4 2.9 %fusion.8 = (bf16[316,2048]{1,0:T(8,128)(2,1)}, bf16[316,2048]{1,0:T(8,128)(2,1)}) fusion(f32[316,1,2048]{2,1,0:T(1,128)S(1)} %get-tuple-element.9, f32[316,1,2048]{2,1,0:T(1,128)S(1)} %copy-done.3), kind=kLoop, calls=%fused_computation.21 | loop fusion | bytes 7766016 | tf_op jit(solution)/shard_map/convert_element_type | solution.py:48
  55.1 3.4 %fusion.4 = f32[432,2048]{1,0:T(8,128)S(1)} fusion(bf16[316,2048]{1,0:T(8,128)(2,1)} %get-tuple-element.26, bf16[316,2048]{1,0:T(8,128)(2,1)} %get-tuple-element.29, pred[432,316]{1,0:T(8,128)(4,1)S(1)} %iota_compare_fusion.6), kind=kOutput, calls=%fused_computation.17 | convolution fusion | flops 1123756672 | bytes 6264128 | tf_op jit(solution)/shard_map/dot_general | solution.py:39
  58.5 1.6 %fusion = f32[432,2048]{1,0:T(8,128)S(1)} fusion(bf16[316,2048]{1,0:T(8,128)(2,1)S(1)} %get-tuple-element.27, bf16[316,2048]{1,0:T(8,128)(2,1)S(1)} %copy-done.5, pred[432,316]{1,0:T(8,128)(4,1)S(1)} %iota_compare_fusion.6), kind=kOutput, calls=%fused_computation.13 | convolution fusion | flops 1123756672 | bytes 6264128 | tf_op jit(solution)/shard_map/dot_general | solution.py:38
  60.1 0.9 %fusion.25 = f32[432,2048]{1,0:T(8,128)S(1)} fusion(bf16[2,48,2048]{2,1,0:T(8,128)(2,1)S(1)} %pad_maximum_fusion.1, s32[432]{0:T(512)S(1)} %eq.112, pred[432]{0:T(512)(128)(4,1)S(1)} %lt.30), kind=kOutput, calls=%fused_computation.50 | convolution fusion | flops 84976128 | bytes 3738112 | tf_op jit(solution)/shard_map/dot_general | solution.py:40
  61.0 3.3 %multiply_subtract_fusion = (f32[432,2048]{1,0:T(8,128)S(1)}, f32[432,2048]{1,0:T(8,128)}) fusion(f32[432,2048]{1,0:T(8,128)S(1)} %fusion.4, f32[432,2048]{1,0:T(8,128)S(1)} %fusion, f32[432,2048]{1,0:T(8,128)S(1)} %fusion.25, bf16[2,48,2048]{2,1,0:T(8,128)(2,1)S(1)} %pad_maximum_fusion.1, s32[432]{0:T(512)} %copy-done.12, pred[432]{0:T(512)(128)(4,1)} %copy-done.14), kind=kOutput, calls=%fused_computation.8 | convolution fusion | flops 90284544 | bytes 17893488 | tf_op jit(solution)/shard_map/dot_general | solution.py:41
  64.4 2.8 %reduce_sum.39 = f32[16,2048]{1,0:T(8,128)} reduce(f32[27,16,2048]{2,1,0:T(8,128)} %bitcast.73, f32[]{:T(128)} %constant.12.clone.1), dimensions={0}, to_apply=%region_3.4 | reduce | flops 851968 | bytes 3670020 | tf_op jit(solution)/shard_map/reduce_sum | solution.py:43
  67.2 1.6 %reduce_precision.15 = f32[16,2048]{1,0:T(8,128)} reduce-precision(f32[16,2048]{1,0:T(8,128)} %reduce_sum.39), exponent_bits=8, mantissa_bits=7 | non-fusion elementwise | flops 32768 | bytes 262144 | tf_op jit(solution)/shard_map/reduce_precision | solution.py:87
  68.8 0.8 %reduce_sum.38 = f32[16,2048]{1,0:T(8,128)} reduce(f32[27,16,2048]{2,1,0:T(8,128)S(1)} %bitcast.72, f32[]{:T(128)} %constant.12.clone.1), dimensions={0}, to_apply=%region_2.3 | reduce | flops 851968 | bytes 3670020 | tf_op jit(solution)/shard_map/reduce_sum | solution.py:42
  69.6 1.1 %reduce_precision.14 = f32[16,2048]{1,0:T(8,128)S(1)} reduce-precision(f32[16,2048]{1,0:T(8,128)} %reduce_sum.38), exponent_bits=8, mantissa_bits=7 | non-fusion elementwise | flops 32768 | bytes 262144 | tf_op jit(solution)/shard_map/reduce_precision | solution.py:86
  70.7 4.1 %convolution_bitcast_fusion.2 = f32[128,1,1024]{2,0,1:T(8,128)S(1)} fusion(bf16[1024,2048]{1,0:T(8,128)(2,1)} %copy-done.1, f32[16,2048]{1,0:T(8,128)} %reduce_precision.15, f32[16,2048]{1,0:T(8,128)S(1)} %reduce_precision.14, f32[8,2048]{1,0:T(8,128)} %copy-done.9, f32[8,2048]{1,0:T(8,128)} %copy-done.7), kind=kOutput, calls=%fused_computation.25 | convolution fusion | flops 537919488 | bytes 5111808 | tf_op jit(solution)/shard_map/dot_general | solution.py:92
  74.9 1.5 %convolution_bitcast_fusion.3 = f32[128,1,1024]{2,0,1:T(8,128)S(1)} fusion(bf16[1024,2048]{1,0:T(8,128)(2,1)S(1)} %copy-done.2, f32[16,2048]{1,0:T(8,128)S(1)} %copy-done.6, f32[16,2048]{1,0:T(8,128)S(1)} %reduce_precision.14, f32[8,2048]{1,0:T(8,128)S(1)} %copy-done.10, f32[8,2048]{1,0:T(8,128)S(1)} %copy-done.8), kind=kOutput, calls=%fused_computation.26 | convolution fusion | flops 537919488 | bytes 5111808 | tf_op jit(solution)/shard_map/dot_general | solution.py:91
  76.5 1.8 %copy.14 = f32[128,2,1024]{2,1,0:T(2,128)} copy(f32[128,2,1024]{2,0,1:T(8,128)S(1)} %pad_maximum_fusion) | data formatting | bytes 2097152 | tf_op jit(solution)/shard_map/stack | solution.py:93
  (44 shorter events, 0.9 us)
Async XLA Ops:
  0.0 54.4 %copy-start = (s32[128,27]{0,1:T(8,128)S(1)}, s32[128,27]{0,1:T(8,128)}, u32[]{:S(2)}) copy-start(s32[128,27]{0,1:T(8,128)} %param.13) | copy-start | bytes 41476
  0.0 9.0 %copy-start.4 = (bf16[128,2,1024]{2,1,0:T(2,128)(2,1)S(1)}, bf16[128,2,1024]{2,1,0:T(2,128)(2,1)}, u32[]{:S(2)}) copy-start(bf16[128,2,1024]{2,1,0:T(2,128)(2,1)} %param.8) | copy-start | bytes 1572868
  0.0 9.8 %copy-start.11 = (f32[8,2048]{1,0:T(8,128)S(1)}, f32[8,2048]{1,0:T(8,128)}, u32[]{:S(2)}) copy-start(f32[8,2048]{1,0:T(8,128)} %param.11) | copy-start | bytes 196612
  9.0 2.0 %copy-start.1 = (bf16[1024,2048]{1,0:T(8,128)(2,1)}, bf16[1024,2048]{1,0:T(8,128)(2,1)S(1)}, u32[]{:S(2)}) copy-start(bf16[1024,2048]{1,0:T(8,128)(2,1)S(1)} %add_convert_fusion) | copy-start | bytes 12582916
  10.0 2.5 %copy-start.7 = (f32[8,2048]{1,0:T(8,128)}, f32[8,2048]{1,0:T(8,128)S(1)}, u32[]{:S(2)}) copy-start(f32[8,2048]{1,0:T(8,128)S(1)} %get-tuple-element.13) | copy-start | bytes 196612
  10.0 2.5 %copy-start.9 = (f32[8,2048]{1,0:T(8,128)}, f32[8,2048]{1,0:T(8,128)S(1)}, u32[]{:S(2)}) copy-start(f32[8,2048]{1,0:T(8,128)S(1)} %get-tuple-element.14) | copy-start | bytes 196612
  12.6 47.5 %collective-permute-start.1 = (bf16[2,16,2048]{2,1,0:T(8,128)(2,1)S(1)}, bf16[2,16,2048]{2,1,0:T(8,128)(2,1)S(1)}, u32[]{:S(2)}, u32[]{:S(2)}) collective-permute-start(bf16[2,16,2048]{2,1,0:T(8,128)(2,1)S(1)} %pad_maximum_fusion.2), channel_id=1, source_target_pairs={{1,0},{2,1},{3,2},{4,3},{5,4},{6,5},{7,6},{8,7},{9,8},{10,9},{11,1... | collective-permute-start | bytes 393224 | tf_op jit(solution)/shard_map/ppermute | solution.py:76
  33.9 26.2 %collective-permute-start = (bf16[2,16,2048]{2,1,0:T(8,128)(2,1)S(1)}, bf16[2,16,2048]{2,1,0:T(8,128)(2,1)S(1)}, u32[]{:S(2)}, u32[]{:S(2)}) collective-permute-start(bf16[2,16,2048]{2,1,0:T(8,128)(2,1)S(1)} %pad_maximum_fusion.2), channel_id=1, source_target_pairs={{0,1},{1,2},{2,3},{3,4},{4,5},{5,6},{6,7},{7,8},{8,9},{9,10},{10,1... | collective-permute-start | bytes 393224 | tf_op jit(solution)/shard_map/ppermute | solution.py:75
  46.8 4.6 %copy-start.3 = (f32[316,1,2048]{2,1,0:T(1,128)S(1)}, f32[316,1,2048]{2,1,0:T(1,128)}, u32[]{:S(2)}) copy-start(f32[316,1,2048]{2,1,0:T(1,128)} %get-tuple-element.10) | copy-start | bytes 7766020
  51.4 3.3 %copy-start.13 = (s32[128,27]{0,1:T(8,128)S(1)}, s32[128,27]{0,1:T(8,128)}, u32[]{:S(2)}) copy-start(s32[128,27]{0,1:T(8,128)} %param.12) | copy-start | bytes 41476
  51.4 3.4 %copy-start.15 = (s32[128]{0:T(128)S(1)}, s32[128]{0:T(128)}, u32[]{:S(2)}) copy-start(s32[128]{0:T(128)} %param.14) | copy-start | bytes 1540
  54.9 5.2 %copy-start.12 = (s32[432]{0:T(512)}, s32[432]{0:T(512)S(1)}, u32[]{:S(2)}) copy-start(s32[432]{0:T(512)S(1)} %eq.112) | copy-start | bytes 5188
  55.1 5.1 %copy-start.14 = (pred[432]{0:T(512)(128)(4,1)}, pred[432]{0:T(512)(128)(4,1)S(1)}, u32[]{:S(2)}) copy-start(pred[432]{0:T(512)(128)(4,1)S(1)} %lt.30) | copy-start | bytes 1300
  55.1 3.4 %copy-start.5 = (bf16[316,2048]{1,0:T(8,128)(2,1)S(1)}, bf16[316,2048]{1,0:T(8,128)(2,1)}, u32[]{:S(2)}) copy-start(bf16[316,2048]{1,0:T(8,128)(2,1)} %get-tuple-element.28) | copy-start | bytes 3883012
  69.6 5.2 %copy-start.2 = (bf16[1024,2048]{1,0:T(8,128)(2,1)S(1)}, bf16[1024,2048]{1,0:T(8,128)(2,1)}, u32[]{:S(2)}) copy-start(bf16[1024,2048]{1,0:T(8,128)(2,1)} %copy-done.1) | copy-start | bytes 12582916
  69.6 5.2 %copy-start.6 = (f32[16,2048]{1,0:T(8,128)S(1)}, f32[16,2048]{1,0:T(8,128)}, u32[]{:S(2)}) copy-start(f32[16,2048]{1,0:T(8,128)} %reduce_precision.15) | copy-start | bytes 393220
  69.6 5.2 %copy-start.8 = (f32[8,2048]{1,0:T(8,128)S(1)}, f32[8,2048]{1,0:T(8,128)}, u32[]{:S(2)}) copy-start(f32[8,2048]{1,0:T(8,128)} %copy-done.7) | copy-start | bytes 196612
  69.6 5.3 %copy-start.10 = (f32[8,2048]{1,0:T(8,128)S(1)}, f32[8,2048]{1,0:T(8,128)}, u32[]{:S(2)}) copy-start(f32[8,2048]{1,0:T(8,128)} %copy-done.9) | copy-start | bytes 196612

commit v3 on v2

--- a/solution.py
+++ b/solution.py
@@ -32,11 +32,12 @@
     ).astype(jnp.bfloat16)
     pick_cls = (cls_t[:, None] == jnp.arange(nclass, dtype=jnp.int32)[None, :]).astype(jnp.bfloat16)
     pick_cls = jnp.concatenate([pick_cls, pick_cls], axis=1)
-    op_re = split_parts(translation[:, 0])
-    op_im = split_parts(translation[:, 1])
     f32 = jnp.float32
-    t_re = jnp.dot(pick_cls, op_re, preferred_element_type=f32)
-    t_im = jnp.dot(pick_cls, op_im, preferred_element_type=f32)
+    picked = lax.dot_general(
+        pick_cls, split_parts(translation), (((1,), (0,)), ((), ())), preferred_element_type=f32
+    )
+    t_re = picked[:, 0]
+    t_im = picked[:, 1]
     p_re = jnp.dot(pick_box, window[0], preferred_element_type=f32)
     p_im = jnp.dot(pick_box, window[1], preferred_element_type=f32)
     real_part = (t_re * p_re - t_im * p_im).reshape(far, rows, -1).sum(axis=0)
@@ -45,9 +46,9 @@
 
 
 def split_parts(values):
-    high = values.astype(jnp.bfloat16)
-    low = (values - high.astype(jnp.float32)).astype(jnp.bfloat16)
-    return jnp.concatenate([high, low], axis=0)
+    high = lax.reduce_precision(values, exponent_bits=8, mantissa_bits=7)
+    low = values - high
+    return jnp.concatenate([high.astype(jnp.bfloat16), low.astype(jnp.bfloat16)], axis=0)
 
 
 def make_body(box_count, ang_count):

time: 78.6 us -> 69.9 us (0.89)
  local copies, waits for them, and re-layouts: 18.3 us -> 7.15 us
  matrix products: 17.1 us -> 18.7 us
  other arithmetic: 19.1 us -> 20 us
    slice x1 -> x0, local copies, waits for them, and re-layouts: 10.8 us -> none  [translate(): op_re = split_parts(translation[:, 0])]
    convert_element_type x1 -> x0, local copies, waits for them, and re-layouts: 2.94 us -> none  [split_parts(): high = values.astype(jnp.bfloat16)]
    reduce_sum x1, other arithmetic: 0.83 us -> 2.83 us  [translate(): real_part = (t_re * p_re - t_im * p_im).reshape(far, rows, -1).sum(axis=0)]
    reduce_sum x1, other arithmetic: 2.83 us -> 0.83 us  [translate(): imag_part = (t_re * p_im + t_im * p_re).reshape(far, rows, -1).sum(axis=0)]
    dot_general x1, matrix products: 3.34 us -> 4.98 us  [translate(): p_im = jnp.dot(pick_box, window[1], preferred_element_type=f32)]
    slice x1, local copies, waits for them, and re-layouts: 0.73 us -> 2.17 us  [body(): children[:, 0]]
    cos x1, local copies, waits for them, and re-layouts: 0.24 us -> 1.08 us  [body(): cosines = jnp.cos(shift_angle)]
    convert_element_type x1, other arithmetic: 4.58 us -> 5.4 us  [split_parts(): high.astype(jnp.bfloat16)]
  transfers between devices with their start and end apart: 2 -> 2, of which waited for: 0 -> 0; matrix products, arithmetic and copies ran while one was open for 31% -> 16% of each run, Pallas kernels for 0% -> 0%
where the time goes in v3:
time: 69.9 us; the launch traced here: 69.5 us
  starting transfers between devices  23.4 us (33%)
  other arithmetic  20 us (29%)
  matrix products  18.7 us (27%)
  local copies, waits for them, and re-layouts  7.15 us (10%)
    ppermute x1, starting transfers between devices, body(): after = lax.ppermute(parent[:, :REACH], axes, down)  21.3 us
    convert_element_type x1, other arithmetic, build_interp(): return dense.astype(jnp.bfloat16)  7.19 us
    convert_element_type x1, other arithmetic, split_parts(): high.astype(jnp.bfloat16)  5.4 us
    dot_general x1, matrix products, translate(): lax.dot_general(pick_cls, split_parts(translation), (((1,), (0,)), ((), (...  5.08 us
    dot_general x1, matrix products, translate(): p_im = jnp.dot(pick_box, window[1], preferred_element_type=f32)  4.98 us
    dot_general x1, matrix products, body(): lax.dot_general(spread_im, interp, contract, preferred_element_type=f32)  4.15 us
    reduce_sum x1, other arithmetic, translate(): real_part = (t_re * p_re - t_im * p_im).reshape(far, rows, -1).sum(axis=0)  2.83 us
    slice x1, local copies, waits for them, and re-layouts, body(): children[:, 0]  2.17 us
  transfers between devices with their start and end apart: 2, of which 0 were waited for; matrix products, arithmetic and copies ran while one was open for 16% of the time, Pallas kernels for 0%

profile of v3, /device:TPU:14, one launch (start us, length us, event | category | flops | bytes accessed | tf_op | source)
XLA Modules:
  0.0 69.5 jit_solution(8769176751247467587)
XLA Ops:
  0.0 0.7 %broadcast_add_fusion.4 = (s32[2048]{0:T(1024)S(1)}, s32[2048]{0:T(1024)S(1)}, s32[2048]{0:T(1024)S(1)}, s32[2048]{0:T(1024)S(1)}, s32[2048]{0:T(1024)S(1)}) fusion(s32[2048]{0:T(1024)} %param.10), kind=kLoop, calls=%fused_computation.64 | loop fusion | flops 10240 | bytes 49152 | tf_op jit(solution)/shard_map/add | solution.py:14
  0.7 1.1 %fusion.32 = (f32[2048,1]{0,1:T(1,128)S(1)}, f32[2048,1]{0,1:T(1,128)S(1)}, f32[2048,1]{0,1:T(1,128)S(1)}, f32[2048,1]{0,1:T(1,128)S(1)}, f32[2048,1]{0,1:T(1,128)S(1)}, /*index=5*/f32[2048,1]{0,1:T(1,128)S(1)}) fusion(f32[2048,6]{0,1:T(8,128)} %param.9), kind=kLoop, calls=%fused_computation.69 | loop fusion | bytes 98304 | tf_op jit(solution)/shard_map/slice | solution.py:16
  1.9 1.1 %fusion.31 = (f32[8,2048]{1,0:T(8,128)S(1)}, f32[8,2048]{1,0:T(8,128)S(1)}) fusion(f32[8,2048]{1,0:T(8,128)} %param.11), kind=kLoop, calls=%fused_computation.68 | loop fusion | bytes 196608 | tf_op jit(solution)/shard_map/cos | solution.py:68
  3.0 2.2 %fusion.30 = (bf16[128,1,1024]{2,1,0:T(2,128)(2,1)S(1)}, bf16[128,1,1024]{2,1,0:T(2,128)(2,1)S(1)}) fusion(bf16[128,2,1024]{2,1,0:T(2,128)(2,1)} %param.8), kind=kLoop, calls=%fused_computation.67 | loop fusion | bytes 1048576 | tf_op jit(solution)/shard_map/slice | solution.py:66
  5.1 7.2 %add_convert_fusion = bf16[1024,2048]{1,0:T(8,128)(2,1)S(1)} fusion(f32[2048]{0:T(1024)S(1)} %bitcast.81, s32[2048]{0:T(1024)S(1)} %get-tuple-element.24, f32[2048]{0:T(1024)S(1)} %bitcast.82, s32[2048]{0:T(1024)S(1)} %get-tuple-element.25, f32[2048]{0:T(1024)S(1)} %bitcast.78, s32[2048]{0:T(1024)S(1)} %get-tuple-element.22, f32[2048]{0:T(1024)S(1)} %bitcast.79, ...), kind=kLoop, calls=%fused_computation | loop fusion | flops 37748736 | bytes 4292608 | tf_op jit(solution)/shard_map/convert_element_type | solution.py:18
  12.4 0.7 %convolution_bitcast_fusion.1 = f32[16,8,2048]{2,1,0:T(8,128)S(1)} fusion(bf16[1024,2048]{1,0:T(8,128)(2,1)S(1)} %add_convert_fusion, bf16[128,1,1024]{2,1,0:T(2,128)(2,1)S(1)} %get-tuple-element.11), kind=kOutput, calls=%fused_computation.19 | convolution fusion | flops 536870912 | bytes 5505024 | tf_op jit(solution)/shard_map/dot_general | solution.py:66
  13.1 1.5 %subtract_reduce_fusion = (bf16[16,2048]{1,0:T(8,128)(2,1)S(1)}, bf16[16,2048]{1,0:T(8,128)(2,1)S(1)}) fusion(f32[16,8,2048]{2,1,0:T(8,128)S(1)} %convolution_bitcast_fusion.1, f32[8,2048]{1,0:T(8,128)S(1)} %get-tuple-element.14, f32[8,2048]{1,0:T(8,128)S(1)} %get-tuple-element.13, bf16[1024,2048]{1,0:T(8,128)(2,1)S(1)} %add_convert_fusion, ...), kind=kOutput, calls=%fused_computation.29 | convolution fusion | flops 538902528 | bytes 5767168 | tf_op jit(solution)/shard_map/dot_general | solution.py:67
  14.7 21.3 %collective-permute-start.1 = (bf16[2,16,2048]{2,1,0:T(8,128)(2,1)S(1)}, bf16[2,16,2048]{2,1,0:T(8,128)(2,1)S(1)}, u32[]{:S(2)}, u32[]{:S(2)}) collective-permute-start(bf16[2,16,2048]{2,1,0:T(8,128)(2,1)S(1)} %pad_maximum_fusion.2), channel_id=1, source_target_pairs={{1,0},{2,1},{3,2},{4,3},{5,4},{6,5},{7,6},{8,7},{9,8},{10,9},{11,1... | collective-permute-start | bytes 393224 | tf_op jit(solution)/shard_map/ppermute | solution.py:77
  36.0 2.1 %collective-permute-start = (bf16[2,16,2048]{2,1,0:T(8,128)(2,1)S(1)}, bf16[2,16,2048]{2,1,0:T(8,128)(2,1)S(1)}, u32[]{:S(2)}, u32[]{:S(2)}) collective-permute-start(bf16[2,16,2048]{2,1,0:T(8,128)(2,1)S(1)} %pad_maximum_fusion.2), channel_id=1, source_target_pairs={{0,1},{1,2},{2,3},{3,4},{4,5},{5,6},{6,7},{7,8},{8,9},{9,10},{10,1... | collective-permute-start | bytes 393224 | tf_op jit(solution)/shard_map/ppermute | solution.py:76
  38.4 0.2 iota_compare_fusion.6
  38.6 5.4 %reduce-precision_convert_fusion = (bf16[316,2,2048]{2,0,1:T(8,128)(2,1)S(1)}, bf16[316,2,2048]{2,0,1:T(8,128)(2,1)S(1)}) fusion(f32[316,2,2048]{2,1,0:T(2,128)} %param.15), kind=kLoop, calls=%fused_computation.8 | loop fusion | flops 5177344 | bytes 10354688 | tf_op jit(solution)/shard_map/convert_element_type | solution.py:51
  44.0 5.1 %fusion.1 = f32[432,2,2048]{2,0,1:T(8,128)} fusion(bf16[316,2,2048]{2,0,1:T(8,128)(2,1)S(1)} %get-tuple-element.10, bf16[316,2,2048]{2,0,1:T(8,128)(2,1)S(1)} %get-tuple-element.9, pred[432,316]{1,0:T(8,128)(4,1)S(1)} %iota_compare_fusion.6), kind=kOutput, calls=%fused_computation.10 | convolution fusion | flops 2247240192 | bytes 12391744 | tf_op jit(solution)/shard_map/dot_general | solution.py:36
  49.4 0.3 copy-done.10
  49.7 0.2 copy-done.8
  49.9 0.7 fusion.22
  50.6 5.0 %multiply_subtract_fusion = (f32[432,2048]{1,0:T(8,128)}, f32[432,2048]{1,0:T(8,128)S(1)}) fusion(f32[432,2048]{1,0:T(8,128)S(1)} %fusion.22, f32[432,2,2048]{2,0,1:T(8,128)} %fusion.1, bf16[2,48,2048]{2,1,0:T(8,128)(2,1)S(1)} %pad_maximum_fusion.1, s32[432]{0:T(512)} %copy-done.8, pred[432]{0:T(512)(128)(4,1)} %copy-done.10), kind=kOutput, calls=%fused_computation.17 | convolution fusion | flops 90284544 | bytes 17893488 | tf_op jit(solution)/shard_map/dot_general | solution.py:42
  55.6 2.8 %reduce_sum.38 = f32[16,2048]{1,0:T(8,128)} reduce(f32[27,16,2048]{2,1,0:T(8,128)} %bitcast.72, f32[]{:T(128)} %constant.12.clone.1), dimensions={0}, to_apply=%region_2.3 | reduce | flops 851968 | bytes 3670020 | tf_op jit(solution)/shard_map/reduce_sum | solution.py:43
  58.4 1.6 %reduce_precision.18 = f32[16,2048]{1,0:T(8,128)} reduce-precision(f32[16,2048]{1,0:T(8,128)} %reduce_sum.38), exponent_bits=8, mantissa_bits=7 | non-fusion elementwise | flops 32768 | bytes 262144 | tf_op jit(solution)/shard_map/reduce_precision | solution.py:87
  60.0 0.8 %reduce_sum.39 = f32[16,2048]{1,0:T(8,128)} reduce(f32[27,16,2048]{2,1,0:T(8,128)S(1)} %bitcast.71, f32[]{:T(128)} %constant.12.clone.1), dimensions={0}, to_apply=%region_3.4 | reduce | flops 851968 | bytes 3670020 | tf_op jit(solution)/shard_map/reduce_sum | solution.py:44
  60.8 1.1 %reduce_precision.19 = f32[16,2048]{1,0:T(8,128)S(1)} reduce-precision(f32[16,2048]{1,0:T(8,128)} %reduce_sum.39), exponent_bits=8, mantissa_bits=7 | non-fusion elementwise | flops 32768 | bytes 262144 | tf_op jit(solution)/shard_map/reduce_precision | solution.py:88
  61.9 4.1 %convolution_bitcast_fusion.2 = f32[128,1,1024]{2,0,1:T(8,128)S(1)} fusion(bf16[1024,2048]{1,0:T(8,128)(2,1)} %copy-done.1, f32[16,2048]{1,0:T(8,128)S(1)} %reduce_precision.19, f32[16,2048]{1,0:T(8,128)} %reduce_precision.18, f32[8,2048]{1,0:T(8,128)} %copy-done.6, f32[8,2048]{1,0:T(8,128)} %copy-done.4), kind=kOutput, calls=%fused_computation.20 | convolution fusion | flops 537919488 | bytes 5111808 | tf_op jit(solution)/shard_map/dot_general | solution.py:93
  66.1 1.5 %convolution_bitcast_fusion.3 = f32[128,1,1024]{2,0,1:T(8,128)S(1)} fusion(bf16[1024,2048]{1,0:T(8,128)(2,1)S(1)} %copy-done.2, f32[16,2048]{1,0:T(8,128)S(1)} %reduce_precision.19, f32[16,2048]{1,0:T(8,128)S(1)} %copy-done.3, f32[8,2048]{1,0:T(8,128)S(1)} %copy-done.7, f32[8,2048]{1,0:T(8,128)S(1)} %copy-done.5), kind=kOutput, calls=%fused_computation.21 | convolution fusion | flops 537919488 | bytes 5111808 | tf_op jit(solution)/shard_map/dot_general | solution.py:92
  67.6 0.1 pad_maximum_fusion
  67.7 1.8 %copy.16 = f32[128,2,1024]{2,1,0:T(2,128)} copy(f32[128,2,1024]{2,0,1:T(8,128)S(1)} %pad_maximum_fusion) | data formatting | bytes 2097152 | tf_op jit(solution)/shard_map/stack | solution.py:94
  (33 shorter events, 0.6 us)
Async XLA Ops:
  0.0 38.2 %copy-start = (s32[128,27]{0,1:T(8,128)S(1)}, s32[128,27]{0,1:T(8,128)}, u32[]{:S(2)}) copy-start(s32[128,27]{0,1:T(8,128)} %param.13) | copy-start | bytes 41476
  2.9 10.2 %copy-start.4 = (f32[8,2048]{1,0:T(8,128)}, f32[8,2048]{1,0:T(8,128)S(1)}, u32[]{:S(2)}) copy-start(f32[8,2048]{1,0:T(8,128)S(1)} %get-tuple-element.13) | copy-start | bytes 196612
  3.0 10.2 %copy-start.6 = (f32[8,2048]{1,0:T(8,128)}, f32[8,2048]{1,0:T(8,128)S(1)}, u32[]{:S(2)}) copy-start(f32[8,2048]{1,0:T(8,128)S(1)} %get-tuple-element.14) | copy-start | bytes 196612
  12.3 2.3 %copy-start.1 = (bf16[1024,2048]{1,0:T(8,128)(2,1)}, bf16[1024,2048]{1,0:T(8,128)(2,1)S(1)}, u32[]{:S(2)}) copy-start(bf16[1024,2048]{1,0:T(8,128)(2,1)S(1)} %add_convert_fusion) | copy-start | bytes 12582916
  12.3 25.8 %copy-start.11 = (s32[128]{0:T(128)S(1)}, s32[128]{0:T(128)}, u32[]{:S(2)}) copy-start(s32[128]{0:T(128)} %param.14) | copy-start | bytes 1540
  14.7 34.6 %collective-permute-start.1 = (bf16[2,16,2048]{2,1,0:T(8,128)(2,1)S(1)}, bf16[2,16,2048]{2,1,0:T(8,128)(2,1)S(1)}, u32[]{:S(2)}, u32[]{:S(2)}) collective-permute-start(bf16[2,16,2048]{2,1,0:T(8,128)(2,1)S(1)} %pad_maximum_fusion.2), channel_id=1, source_target_pairs={{1,0},{2,1},{3,2},{4,3},{5,4},{6,5},{7,6},{8,7},{9,8},{10,9},{11,1... | collective-permute-start | bytes 393224 | tf_op jit(solution)/shard_map/ppermute | solution.py:77
  36.0 13.3 %collective-permute-start = (bf16[2,16,2048]{2,1,0:T(8,128)(2,1)S(1)}, bf16[2,16,2048]{2,1,0:T(8,128)(2,1)S(1)}, u32[]{:S(2)}, u32[]{:S(2)}) collective-permute-start(bf16[2,16,2048]{2,1,0:T(8,128)(2,1)S(1)} %pad_maximum_fusion.2), channel_id=1, source_target_pairs={{0,1},{1,2},{2,3},{3,4},{4,5},{5,6},{6,7},{7,8},{8,9},{9,10},{10,1... | collective-permute-start | bytes 393224 | tf_op jit(solution)/shard_map/ppermute | solution.py:76
  44.0 5.2 %copy-start.9 = (s32[128,27]{0,1:T(8,128)S(1)}, s32[128,27]{0,1:T(8,128)}, u32[]{:S(2)}) copy-start(s32[128,27]{0,1:T(8,128)} %param.12) | copy-start | bytes 41476
  49.1 0.5 copy-start.10
  49.3 0.6 copy-start.8
  60.8 5.2 %copy-start.2 = (bf16[1024,2048]{1,0:T(8,128)(2,1)S(1)}, bf16[1024,2048]{1,0:T(8,128)(2,1)}, u32[]{:S(2)}) copy-start(bf16[1024,2048]{1,0:T(8,128)(2,1)} %copy-done.1) | copy-start | bytes 12582916
  60.8 5.2 %copy-start.3 = (f32[16,2048]{1,0:T(8,128)S(1)}, f32[16,2048]{1,0:T(8,128)}, u32[]{:S(2)}) copy-start(f32[16,2048]{1,0:T(8,128)} %reduce_precision.18) | copy-start | bytes 393220
  60.8 5.2 %copy-start.5 = (f32[8,2048]{1,0:T(8,128)S(1)}, f32[8,2048]{1,0:T(8,128)}, u32[]{:S(2)}) copy-start(f32[8,2048]{1,0:T(8,128)} %copy-done.4) | copy-start | bytes 196612
  60.8 5.3 %copy-start.7 = (f32[8,2048]{1,0:T(8,128)S(1)}, f32[8,2048]{1,0:T(8,128)}, u32[]{:S(2)}) copy-start(f32[8,2048]{1,0:T(8,128)} %copy-done.6) | copy-start | bytes 196612

commit v4 on v3

--- a/solution.py
+++ b/solution.py
@@ -2,20 +2,42 @@
 import jax.numpy as jnp
 from jax import lax
 from jax.sharding import PartitionSpec as P
+from jax.experimental import pallas as pl
+
+INTERPRET = False
+CHUNK = 512
 
 K_LOW = 1024
 REACH = 16
 
 
 def build_interp(interp_band, band_start):
-    low_ids = jnp.arange(K_LOW, dtype=jnp.int32)
+    offset = jnp.arange(K_LOW, dtype=jnp.int32)[:, None] - band_start[None, :]
+    weights = interp_band.T
     dense = jnp.zeros((K_LOW, interp_band.shape[0]), jnp.float32)
     for column in range(interp_band.shape[1]):
-        target = band_start + column
-        dense = dense + jnp.where(
-            low_ids[:, None] == target[None, :], interp_band[:, column][None, :], jnp.float32(0.0)
-        )
+        dense = jnp.where(offset == column, weights[column][None, :], dense)
     return dense.astype(jnp.bfloat16)
+
+
+def translate_kernel(pick_cls_ref, pick_box_ref, ops_ref, win_ref, out_ref):
+    f32 = jnp.float32
+    pick_cls = pick_cls_ref[...]
+    pick_box = pick_box_ref[...]
+    t_re = jnp.dot(pick_cls, ops_ref[0], preferred_element_type=f32)
+    t_im = jnp.dot(pick_cls, ops_ref[1], preferred_element_type=f32)
+    p_re = jnp.dot(pick_box, win_ref[0], preferred_element_type=f32)
+    p_im = jnp.dot(pick_box, win_ref[1], preferred_element_type=f32)
+    real_part = t_re * p_re - t_im * p_im
+    imag_part = t_re * p_im + t_im * p_re
+    rows = out_ref.shape[1]
+    acc_re = real_part[0:rows]
+    acc_im = imag_part[0:rows]
+    for slot in range(1, real_part.shape[0] // rows):
+        acc_re = acc_re + real_part[slot * rows:(slot + 1) * rows]
+        acc_im = acc_im + imag_part[slot * rows:(slot + 1) * rows]
+    out_ref[0] = acc_re.astype(out_ref.dtype)
+    out_ref[1] = acc_im.astype(out_ref.dtype)
 
 
 def translate(window, translation, rel_box, classes, counts):
@@ -32,17 +54,22 @@
     ).astype(jnp.bfloat16)
     pick_cls = (cls_t[:, None] == jnp.arange(nclass, dtype=jnp.int32)[None, :]).astype(jnp.bfloat16)
     pick_cls = jnp.concatenate([pick_cls, pick_cls], axis=1)
-    f32 = jnp.float32
-    picked = lax.dot_general(
-        pick_cls, split_parts(translation), (((1,), (0,)), ((), ())), preferred_element_type=f32
-    )
-    t_re = picked[:, 0]
-    t_im = picked[:, 1]
-    p_re = jnp.dot(pick_box, window[0], preferred_element_type=f32)
-    p_im = jnp.dot(pick_box, window[1], preferred_element_type=f32)
-    real_part = (t_re * p_re - t_im * p_im).reshape(far, rows, -1).sum(axis=0)
-    imag_part = (t_re * p_im + t_im * p_re).reshape(far, rows, -1).sum(axis=0)
-    return real_part, imag_part
+    ops = split_parts(translation).transpose(1, 0, 2)
+    k_high = window.shape[2]
+    slots_rows = pick_cls.shape[0]
+    return pl.pallas_call(
+        translate_kernel,
+        out_shape=jax.ShapeDtypeStruct((2, rows, k_high), jnp.bfloat16),
+        grid=(k_high // CHUNK,),
+        in_specs=[
+            pl.BlockSpec((slots_rows, pick_cls.shape[1]), lambda j: (0, 0)),
+            pl.BlockSpec((slots_rows, width), lambda j: (0, 0)),
+            pl.BlockSpec((2, ops.shape[1], CHUNK), lambda j: (0, 0, j)),
+            pl.BlockSpec((2, width, CHUNK), lambda j: (0, 0, j)),
+        ],
+        out_specs=pl.BlockSpec((2, rows, CHUNK), lambda j: (0, 0, j)),
+        interpret=INTERPRET,
+    )(pick_cls, pick_box, ops, window)
 
 
 def split_parts(values):
@@ -83,9 +110,9 @@
         my_class = lax.dynamic_slice_in_dim(far_class, first, parents_here, 0)
         my_count = lax.dynamic_slice_in_dim(far_count, first, parents_here, 0)
         rel_box = my_box - (device * parents_here - REACH)
-        local_re, local_im = translate(window, translation, rel_box, my_class, my_count)
-        local_re = lax.reduce_precision(local_re, exponent_bits=8, mantissa_bits=7)[:, None]
-        local_im = lax.reduce_precision(local_im, exponent_bits=8, mantissa_bits=7)[:, None]
+        local = translate(window, translation, rel_box, my_class, my_count).astype(f32)
+        local_re = local[0][:, None]
+        local_im = local[1][:, None]
         spread_re = (local_re * cosines + local_im * sines).astype(jnp.bfloat16).reshape(-1, high_width)
         spread_im = (local_im * cosines - local_re * sines).astype(jnp.bfloat16).reshape(-1, high_width)
         contract = (((1,), (1,)), ((), ()))

time: 69.9 us -> 60.3 us (0.86)
  matrix products: 18.7 us -> 7.71 us
  Pallas kernels: 0 us -> 7 us
  local copies, waits for them, and re-layouts: 7.15 us -> 4.25 us
  other arithmetic: 20 us -> 17.4 us
    dot_general x3 -> x0, matrix products: 10.7 us -> none  [the longest x1 5.08 us: translate(): lax.dot_general(pick_cls, split_parts(translation), (((1,), (0,)), ((), (...]
    pallas_call x0 -> x1, Pallas kernels: none -> 7 us  [translate(): pl.pallas_call(translate_kernel, out_shape=jax.ShapeDtypeStruct((2, rows,...]
    reduce_sum x2 -> x0, other arithmetic: 3.66 us -> none  [the longest x1 2.83 us: translate(): real_part = (t_re * p_re - t_im * p_im).reshape(far, rows, -1).sum(axis=0)]
    transpose x0 -> x1, other arithmetic: none -> 3.23 us  [translate(): ops = split_parts(translation).transpose(1, 0, 2)]
    reduce_precision x2 -> x0, other arithmetic: 2.62 us -> none  [the longest x1 1.56 us: body(): lax.reduce_precision(local_re, exponent_bits=8, mantissa_bits=7)[:, None]]
    convert_element_type x1, other arithmetic: 7.19 us -> 4.67 us  [build_interp(): return dense.astype(jnp.bfloat16)]
    convert_element_type x0 -> x2, other arithmetic: none -> 1.9 us  [the longest x1 1.07 us: body(): translate(window, translation, rel_box, my_class, my_count).astype(f32)]
    slice x1, local copies, waits for them, and re-layouts: 2.17 us -> 0.73 us  [body(): children[:, 0]]
  transfers between devices with their start and end apart: 2 -> 2, of which waited for: 0 -> 0; matrix products, arithmetic and copies ran while one was open for 16% -> 18% of each run, Pallas kernels for 0% -> 0%
where the time goes in v4:
time: 60.3 us; the launch traced here: 60 us
  starting transfers between devices  23.4 us (39%)
  other arithmetic  17.4 us (29%)
  matrix products  7.71 us (13%)
  Pallas kernels  7 us (12%)
  local copies, waits for them, and re-layouts  4.25 us (7%)
    ppermute x1, starting transfers between devices, body(): after = lax.ppermute(parent[:, :REACH], axes, down)  21.3 us
    pallas_call x1, Pallas kernels, translate(): pl.pallas_call(translate_kernel, out_shape=jax.ShapeDtypeStruct((2, rows,...  7 us
    convert_element_type x1, other arithmetic, split_parts(): high.astype(jnp.bfloat16)  5.4 us
    convert_element_type x1, other arithmetic, build_interp(): return dense.astype(jnp.bfloat16)  4.67 us
    dot_general x1, matrix products, body(): lax.dot_general(spread_im, interp, contract, preferred_element_type=f32)  3.91 us
    transpose x1, other arithmetic, translate(): ops = split_parts(translation).transpose(1, 0, 2)  3.23 us
    ppermute x1, starting transfers between devices, body(): before = lax.ppermute(parent[:, parents_here - REACH:], axes, up)  2.1 us
    another operation x1, local copies, waits for them, and re-layouts, body(): return jnp.stack([out_re, out_im], axis=1)  1.79 us
  transfers between devices with their start and end apart: 2, of which 0 were waited for; matrix products, arithmetic and copies ran while one was open for 18% of the time, Pallas kernels for 0%

profile of v4, /device:TPU:14, one launch (start us, length us, event | category | flops | bytes accessed | tf_op | source)
XLA Modules:
  0.0 60.0 jit_solution(12409567916233805307)
XLA Ops:
  0.0 1.1 %fusion.23 = (f32[1,2048]{1,0:T(1,128)S(1)}, f32[1,2048]{1,0:T(1,128)S(1)}, f32[1,2048]{1,0:T(1,128)S(1)}, f32[1,2048]{1,0:T(1,128)S(1)}, f32[1,2048]{1,0:T(1,128)S(1)}, /*index=5*/f32[1,2048]{1,0:T(1,128)S(1)}) fusion(f32[6,2048]{1,0:T(8,128)} %bitcast.57), kind=kLoop, calls=%fused_computation.49 | loop fusion | bytes 98304 | tf_op jit(solution)/shard_map/slice | solution.py:19
  1.1 4.7 %select_convert_fusion = bf16[1024,2048]{1,0:T(8,128)(2,1)S(1)} fusion(f32[2048]{0:T(1024)S(1)} %bitcast.59, f32[2048]{0:T(1024)S(1)} %bitcast.60, f32[2048]{0:T(1024)S(1)} %bitcast.61, f32[2048]{0:T(1024)S(1)} %bitcast.62, f32[2048]{0:T(1024)S(1)} %bitcast.63, f32[2048]{0:T(1024)S(1)} %bitcast.58, s32[2048]{0:T(1024)} %param.10), kind=kLoop, calls=%fused_computation | loop fusion | flops 27262976 | bytes 4251648 | tf_op jit(solution)/shard_map/convert_element_type | solution.py:20
  5.8 0.7 %fusion.21 = (bf16[128,1,1024]{2,1,0:T(2,128)(2,1)S(1)}, bf16[128,1,1024]{2,1,0:T(2,128)(2,1)S(1)}) fusion(bf16[128,2,1024]{2,1,0:T(2,128)(2,1)S(1)} %copy-done.2), kind=kLoop, calls=%fused_computation.47 | loop fusion | bytes 1048576 | tf_op jit(solution)/shard_map/slice | solution.py:93
  6.6 0.2 fusion.22
  6.8 0.7 %convolution_bitcast_fusion.1 = f32[16,8,2048]{2,1,0:T(8,128)S(1)} fusion(bf16[1024,2048]{1,0:T(8,128)(2,1)S(1)} %select_convert_fusion, bf16[128,1,1024]{2,1,0:T(2,128)(2,1)S(1)} %get-tuple-element.9), kind=kOutput, calls=%fused_computation.13 | convolution fusion | flops 536870912 | bytes 5505024 | tf_op jit(solution)/shard_map/dot_general | solution.py:93
  7.6 1.5 %subtract_reduce_fusion = (bf16[16,2048]{1,0:T(8,128)(2,1)S(1)}, bf16[16,2048]{1,0:T(8,128)(2,1)S(1)}) fusion(f32[16,8,2048]{2,1,0:T(8,128)S(1)} %convolution_bitcast_fusion.1, f32[8,2048]{1,0:T(8,128)S(1)} %get-tuple-element.14, f32[8,2048]{1,0:T(8,128)S(1)} %get-tuple-element.13, bf16[1024,2048]{1,0:T(8,128)(2,1)S(1)} %select_convert_fusion, ...), kind=kOutput, calls=%fused_computation.21 | convolution fusion | flops 538902528 | bytes 5767168 | tf_op jit(solution)/shard_map/dot_general | solution.py:94
  9.2 21.3 %collective-permute-start.1 = (bf16[2,16,2048]{2,1,0:T(8,128)(2,1)S(1)}, bf16[2,16,2048]{2,1,0:T(8,128)(2,1)S(1)}, u32[]{:S(2)}, u32[]{:S(2)}) collective-permute-start(bf16[2,16,2048]{2,1,0:T(8,128)(2,1)S(1)} %pad_maximum_fusion.2), channel_id=1, source_target_pairs={{1,0},{2,1},{3,2},{4,3},{5,4},{6,5},{7,6},{8,7},{9,8},{10,9},{11,1... | collective-permute-start | bytes 393224 | tf_op jit(solution)/shard_map/ppermute | solution.py:104
  30.5 2.1 %collective-permute-start = (bf16[2,16,2048]{2,1,0:T(8,128)(2,1)S(1)}, bf16[2,16,2048]{2,1,0:T(8,128)(2,1)S(1)}, u32[]{:S(2)}, u32[]{:S(2)}) collective-permute-start(bf16[2,16,2048]{2,1,0:T(8,128)(2,1)S(1)} %pad_maximum_fusion.2), channel_id=1, source_target_pairs={{0,1},{1,2},{2,3},{3,4},{4,5},{5,6},{6,7},{7,8},{8,9},{9,10},{10,1... | collective-permute-start | bytes 393224 | tf_op jit(solution)/shard_map/ppermute | solution.py:103
  32.6 0.1 subtract_bitcast_fusion
  32.7 0.1 eq.66
  32.8 0.2 iota_compare_fusion
  33.0 0.1 eq.70
  33.1 0.1 lt.30
  33.2 5.4 %reduce-precision_convert_fusion = (bf16[316,2,2048]{2,0,1:T(8,128)(2,1)S(1)}, bf16[316,2,2048]{2,0,1:T(8,128)(2,1)S(1)}) fusion(f32[316,2,2048]{2,1,0:T(2,128)} %param.15), kind=kLoop, calls=%fused_computation.9 | loop fusion | flops 5177344 | bytes 10354688 | tf_op jit(solution)/shard_map/convert_element_type | solution.py:78
  38.6 3.2 %maximum_bitcast_fusion.ops_ref = bf16[2,632,2048]{2,1,0:T(8,128)(2,1)} fusion(bf16[316,2,2048]{2,0,1:T(8,128)(2,1)S(1)} %get-tuple-element.8, bf16[316,2,2048]{2,0,1:T(8,128)(2,1)S(1)} %get-tuple-element.7), kind=kLoop, calls=%fused_computation.11 | loop fusion | flops 10354688 | bytes 10354688 | tf_op jit(solution)/shard_map/transpose | solution.py:57
  41.9 0.8 %fusion.20.pick_box_ref = bf16[432,48]{1,0:T(8,128)(2,1)} fusion(s32[432]{0:T(512)S(1)} %eq.70, pred[432]{0:T(512)(128)(4,1)S(1)} %lt.30), kind=kLoop, calls=%fused_computation.38 | loop fusion | flops 62208 | bytes 43632 | tf_op jit(solution)/shard_map/convert_element_type | solution.py:54
  42.7 1.0 %add_convert_fusion.pick_cls_ref = bf16[432,632]{1,0:T(8,128)(2,1)} fusion(pred[432,316]{1,0:T(8,128)(4,1)S(1)} %iota_compare_fusion), kind=kLoop, calls=%fused_computation.16 | loop fusion | flops 546048 | bytes 682560 | tf_op jit(solution)/shard_map/concatenate | solution.py:56
  43.7 0.8 %pad_maximum_fusion.1.win_ref = bf16[2,48,2048]{2,1,0:T(8,128)(2,1)} fusion(bf16[2,16,2048]{2,1,0:T(8,128)(2,1)S(1)} %collective-permute-done.1, bf16[1,16,2048]{2,1,0:T(8,128)(2,1)S(1)} %bitcast.56, bf16[1,16,2048]{2,1,0:T(8,128)(2,1)S(1)} %bitcast.54, bf16[2,16,2048]{2,1,0:T(8,128)(2,1)S(1)} %collective-permute-done), kind=kLoop, calls=%fused_computation.33 | loop fusion | flops 1572864 | bytes 786432 | tf_op jit(solution)/shard_map/concatenate | solution.py:105
  44.5 7.0 %shard_map.82 = bf16[2,16,2048]{2,1,0:T(8,128)(2,1)} custom-call(bf16[432,632]{1,0:T(8,128)(2,1)} %add_convert_fusion.pick_cls_ref, bf16[432,48]{1,0:T(8,128)(2,1)} %fusion.20.pick_box_ref, bf16[2,632,2048]{2,1,0:T(8,128)(2,1)} %maximum_bitcast_fusion.ops_ref, bf16[2,48,2048]{2,1,0:T(8,128)(2,1)} %pad_maximum_fusion.1.win_ref), custom_call_target="tpu_custom_call" | custom-call | tf_op jit(solution)/shard_map/pallas_call | solution.py:60
  51.5 1.1 %convert_element_type.35 = f32[2,16,2048]{2,1,0:T(8,128)S(1)} convert(bf16[2,16,2048]{2,1,0:T(8,128)(2,1)} %shard_map.82) | non-fusion elementwise | flops 65536 | bytes 393216 | tf_op jit(solution)/shard_map/convert_element_type | solution.py:113
  52.6 3.9 %convolution_bitcast_fusion.2 = f32[128,1,1024]{2,0,1:T(8,128)S(1)} fusion(bf16[1024,2048]{1,0:T(8,128)(2,1)} %copy-done, f32[16,2048]{1,0:T(8,128)S(1)} %get-tuple-element.12, f32[16,2048]{1,0:T(8,128)S(1)} %get-tuple-element.11, f32[8,2048]{1,0:T(8,128)S(1)} %get-tuple-element.14, f32[8,2048]{1,0:T(8,128)S(1)} %get-tuple-element.13), kind=kOutput, calls=%fused_computation.14 | convolution fusion | flops 537919488 | bytes 5111808 | tf_op jit(solution)/shard_map/dot_general | solution.py:120
  56.5 1.5 %convolution_bitcast_fusion.3 = f32[128,1,1024]{2,0,1:T(8,128)S(1)} fusion(bf16[1024,2048]{1,0:T(8,128)(2,1)S(1)} %copy-done.1, f32[16,2048]{1,0:T(8,128)S(1)} %get-tuple-element.12, f32[16,2048]{1,0:T(8,128)S(1)} %get-tuple-element.11, f32[8,2048]{1,0:T(8,128)S(1)} %get-tuple-element.14, f32[8,2048]{1,0:T(8,128)S(1)} %get-tuple-element.13), kind=kOutput, calls=%fused_computation.15 | convolution fusion | flops 537919488 | bytes 5111808 | tf_op jit(solution)/shard_map/dot_general | solution.py:119
  58.1 0.1 pad_maximum_fusion
  58.2 1.8 %copy.16 = f32[128,2,1024]{2,1,0:T(2,128)} copy(f32[128,2,1024]{2,0,1:T(8,128)S(1)} %pad_maximum_fusion) | data formatting | bytes 2097152 | tf_op jit(solution)/shard_map/stack | solution.py:121
  (20 shorter events, 0.2 us)
Async XLA Ops:
  0.0 5.8 %copy-start.2 = (bf16[128,2,1024]{2,1,0:T(2,128)(2,1)S(1)}, bf16[128,2,1024]{2,1,0:T(2,128)(2,1)}, u32[]{:S(2)}) copy-start(bf16[128,2,1024]{2,1,0:T(2,128)(2,1)} %param.8) | copy-start | bytes 1572868
  0.0 6.6 %copy-start.3 = (f32[8,2048]{1,0:T(8,128)S(1)}, f32[8,2048]{1,0:T(8,128)}, u32[]{:S(2)}) copy-start(f32[8,2048]{1,0:T(8,128)} %param.11) | copy-start | bytes 196612
  5.8 3.3 %copy-start = (bf16[1024,2048]{1,0:T(8,128)(2,1)}, bf16[1024,2048]{1,0:T(8,128)(2,1)S(1)}, u32[]{:S(2)}) copy-start(bf16[1024,2048]{1,0:T(8,128)(2,1)S(1)} %select_convert_fusion) | copy-start | bytes 12582916
  7.6 25.1 %copy-start.4 = (s32[128,27]{0,1:T(8,128)S(1)}, s32[128,27]{0,1:T(8,128)}, u32[]{:S(2)}) copy-start(s32[128,27]{0,1:T(8,128)} %param.12) | copy-start | bytes 41476
  7.6 25.0 %copy-start.5 = (s32[128,27]{0,1:T(8,128)S(1)}, s32[128,27]{0,1:T(8,128)}, u32[]{:S(2)}) copy-start(s32[128,27]{0,1:T(8,128)} %param.13) | copy-start | bytes 41476
  7.6 25.5 %copy-start.6 = (s32[128]{0:T(128)S(1)}, s32[128]{0:T(128)}, u32[]{:S(2)}) copy-start(s32[128]{0:T(128)} %param.14) | copy-start | bytes 1540
  9.2 34.6 %collective-permute-start.1 = (bf16[2,16,2048]{2,1,0:T(8,128)(2,1)S(1)}, bf16[2,16,2048]{2,1,0:T(8,128)(2,1)S(1)}, u32[]{:S(2)}, u32[]{:S(2)}) collective-permute-start(bf16[2,16,2048]{2,1,0:T(8,128)(2,1)S(1)} %pad_maximum_fusion.2), channel_id=1, source_target_pairs={{1,0},{2,1},{3,2},{4,3},{5,4},{6,5},{7,6},{8,7},{9,8},{10,9},{11,1... | collective-permute-start | bytes 393224 | tf_op jit(solution)/shard_map/ppermute | solution.py:104
  30.5 13.2 %collective-permute-start = (bf16[2,16,2048]{2,1,0:T(8,128)(2,1)S(1)}, bf16[2,16,2048]{2,1,0:T(8,128)(2,1)S(1)}, u32[]{:S(2)}, u32[]{:S(2)}) collective-permute-start(bf16[2,16,2048]{2,1,0:T(8,128)(2,1)S(1)} %pad_maximum_fusion.2), channel_id=1, source_target_pairs={{0,1},{1,2},{2,3},{3,4},{4,5},{5,6},{6,7},{7,8},{8,9},{9,10},{10,1... | collective-permute-start | bytes 393224 | tf_op jit(solution)/shard_map/ppermute | solution.py:103
  51.5 5.0 %copy-start.1 = (bf16[1024,2048]{1,0:T(8,128)(2,1)S(1)}, bf16[1024,2048]{1,0:T(8,128)(2,1)}, u32[]{:S(2)}) copy-start(bf16[1024,2048]{1,0:T(8,128)(2,1)} %copy-done) | copy-start | bytes 12582916

commit v5 on v4

--- a/solution.py
+++ b/solution.py
@@ -20,12 +20,14 @@
     return dense.astype(jnp.bfloat16)
 
 
-def translate_kernel(pick_cls_ref, pick_box_ref, ops_ref, win_ref, out_ref):
+def translate_kernel(pick_cls_ref, pick_box_ref, high_ref, low_ref, win_ref, out_ref):
     f32 = jnp.float32
     pick_cls = pick_cls_ref[...]
     pick_box = pick_box_ref[...]
-    t_re = jnp.dot(pick_cls, ops_ref[0], preferred_element_type=f32)
-    t_im = jnp.dot(pick_cls, ops_ref[1], preferred_element_type=f32)
+    t_re = jnp.dot(pick_cls, high_ref[0], preferred_element_type=f32)
+    t_re = t_re + jnp.dot(pick_cls, low_ref[0], preferred_element_type=f32)
+    t_im = jnp.dot(pick_cls, high_ref[1], preferred_element_type=f32)
+    t_im = t_im + jnp.dot(pick_cls, low_ref[1], preferred_element_type=f32)
     p_re = jnp.dot(pick_box, win_ref[0], preferred_element_type=f32)
     p_im = jnp.dot(pick_box, win_ref[1], preferred_element_type=f32)
     real_part = t_re * p_re - t_im * p_im
@@ -53,8 +55,7 @@
         box_t[:, None] == jnp.arange(width, dtype=jnp.int32)[None, :], live_t[:, None]
     ).astype(jnp.bfloat16)
     pick_cls = (cls_t[:, None] == jnp.arange(nclass, dtype=jnp.int32)[None, :]).astype(jnp.bfloat16)
-    pick_cls = jnp.concatenate([pick_cls, pick_cls], axis=1)
-    ops = split_parts(translation).transpose(1, 0, 2)
+    high, low = split_parts(translation.transpose(1, 0, 2))
     k_high = window.shape[2]
     slots_rows = pick_cls.shape[0]
     return pl.pallas_call(
@@ -64,18 +65,19 @@
         in_specs=[
             pl.BlockSpec((slots_rows, pick_cls.shape[1]), lambda j: (0, 0)),
             pl.BlockSpec((slots_rows, width), lambda j: (0, 0)),
-            pl.BlockSpec((2, ops.shape[1], CHUNK), lambda j: (0, 0, j)),
+            pl.BlockSpec((2, nclass, CHUNK), lambda j: (0, 0, j)),
+            pl.BlockSpec((2, nclass, CHUNK), lambda j: (0, 0, j)),
             pl.BlockSpec((2, width, CHUNK), lambda j: (0, 0, j)),
         ],
         out_specs=pl.BlockSpec((2, rows, CHUNK), lambda j: (0, 0, j)),
         interpret=INTERPRET,
-    )(pick_cls, pick_box, ops, window)
+    )(pick_cls, pick_box, high, low, window)
 
 
 def split_parts(values):
     high = lax.reduce_precision(values, exponent_bits=8, mantissa_bits=7)
     low = values - high
-    return jnp.concatenate([high.astype(jnp.bfloat16), low.astype(jnp.bfloat16)], axis=0)
+    return high.astype(jnp.bfloat16), low.astype(jnp.bfloat16)
 
 
 def make_body(box_count, ang_count):

time: 60.3 us -> 62.2 us (1.032)
  local copies, waits for them, and re-layouts: 4.25 us -> 6.51 us
  other arithmetic: 17.4 us -> 16.2 us
  Pallas kernels: 7 us -> 7.87 us
    convert_element_type x1 -> x2, other arithmetic: 5.4 us -> 8.66 us  [the longest x1 7.79 us: split_parts(): return (high.astype(jnp.bfloat16), low.astype(jnp.bfloat16))]
    transpose x1 -> x0, other arithmetic: 3.23 us -> none  [translate(): ops = split_parts(translation).transpose(1, 0, 2)]
    slice x1, local copies, waits for them, and re-layouts: 0.73 us -> 2.15 us  [body(): children[:, 0]]
    concatenate x1 -> x0, other arithmetic: 1.05 us -> none  [translate(): pick_cls = jnp.concatenate([pick_cls, pick_cls], axis=1)]
    pallas_call x1, Pallas kernels: 7 us -> 7.87 us  [translate(): pl.pallas_call(translate_kernel, out_shape=jax.ShapeDtypeStruct((2, rows,...]
    cos x1, local copies, waits for them, and re-layouts: 0.24 us -> 1.08 us  [body(): cosines = jnp.cos(shift_angle)]
  transfers between devices with their start and end apart: 2 -> 2, of which waited for: 0 -> 0; matrix products, arithmetic and copies ran while one was open for 18% -> 16% of each run, Pallas kernels for 0% -> 0%
where the time goes in v5:
time: 62.2 us; the launch traced here: 61.9 us
  starting transfers between devices  23.4 us (38%)
  other arithmetic  16.2 us (26%)
  Pallas kernels  7.87 us (13%)
  matrix products  7.71 us (12%)
  local copies, waits for them, and re-layouts  6.51 us (10%)
    ppermute x1, starting transfers between devices, body(): after = lax.ppermute(parent[:, :REACH], axes, down)  21.3 us
    pallas_call x1, Pallas kernels, translate(): pl.pallas_call(translate_kernel, out_shape=jax.ShapeDtypeStruct((2, rows,...  7.87 us
    convert_element_type x1, other arithmetic, split_parts(): return (high.astype(jnp.bfloat16), low.astype(jnp.bfloat16))  7.79 us
    convert_element_type x1, other arithmetic, build_interp(): return dense.astype(jnp.bfloat16)  4.67 us
    dot_general x1, matrix products, body(): lax.dot_general(spread_im, interp, contract, preferred_element_type=f32)  3.91 us
    slice x1, local copies, waits for them, and re-layouts, body(): children[:, 0]  2.15 us
    ppermute x1, starting transfers between devices, body(): before = lax.ppermute(parent[:, parents_here - REACH:], axes, up)  2.1 us
    another operation x1, local copies, waits for them, and re-layouts, body(): return jnp.stack([out_re, out_im], axis=1)  1.79 us
  transfers between devices with their start and end apart: 2, of which 0 were waited for; matrix products, arithmetic and copies ran while one was open for 16% of the time, Pallas kernels for 0%

profile of v5, /device:TPU:14, one launch (start us, length us, event | category | flops | bytes accessed | tf_op | source)
XLA Modules:
  0.0 61.9 jit_solution(6646204910616946655)
XLA Ops:
  0.0 1.1 %fusion.24 = (f32[1,2048]{1,0:T(1,128)S(1)}, f32[1,2048]{1,0:T(1,128)S(1)}, f32[1,2048]{1,0:T(1,128)S(1)}, f32[1,2048]{1,0:T(1,128)S(1)}, f32[1,2048]{1,0:T(1,128)S(1)}, /*index=5*/f32[1,2048]{1,0:T(1,128)S(1)}) fusion(f32[6,2048]{1,0:T(8,128)} %bitcast.58), kind=kLoop, calls=%fused_computation.48 | loop fusion | bytes 98304 | tf_op jit(solution)/shard_map/slice | solution.py:19
  1.1 1.1 %fusion.23 = (f32[8,2048]{1,0:T(8,128)S(1)}, f32[8,2048]{1,0:T(8,128)S(1)}) fusion(f32[8,2048]{1,0:T(8,128)} %param.11), kind=kLoop, calls=%fused_computation.47 | loop fusion | bytes 196608 | tf_op jit(solution)/shard_map/cos | solution.py:97
  2.2 2.2 %fusion.22 = (bf16[128,1,1024]{2,1,0:T(2,128)(2,1)S(1)}, bf16[128,1,1024]{2,1,0:T(2,128)(2,1)S(1)}) fusion(bf16[128,2,1024]{2,1,0:T(2,128)(2,1)} %param.8), kind=kLoop, calls=%fused_computation.46 | loop fusion | bytes 1048576 | tf_op jit(solution)/shard_map/slice | solution.py:95
  4.4 4.7 %select_convert_fusion = bf16[1024,2048]{1,0:T(8,128)(2,1)S(1)} fusion(f32[2048]{0:T(1024)S(1)} %bitcast.60, f32[2048]{0:T(1024)S(1)} %bitcast.61, f32[2048]{0:T(1024)S(1)} %bitcast.62, f32[2048]{0:T(1024)S(1)} %bitcast.63, f32[2048]{0:T(1024)S(1)} %bitcast.64, f32[2048]{0:T(1024)S(1)} %bitcast.59, s32[2048]{0:T(1024)} %param.10), kind=kLoop, calls=%fused_computation | loop fusion | flops 27262976 | bytes 4251648 | tf_op jit(solution)/shard_map/convert_element_type | solution.py:20
  9.0 0.7 %convolution_bitcast_fusion.1 = f32[16,8,2048]{2,1,0:T(8,128)S(1)} fusion(bf16[1024,2048]{1,0:T(8,128)(2,1)S(1)} %select_convert_fusion, bf16[128,1,1024]{2,1,0:T(2,128)(2,1)S(1)} %get-tuple-element.9), kind=kOutput, calls=%fused_computation.12 | convolution fusion | flops 536870912 | bytes 5505024 | tf_op jit(solution)/shard_map/dot_general | solution.py:95
  9.8 0.0 copy-start.3
  9.8 1.5 %subtract_reduce_fusion = (bf16[16,2048]{1,0:T(8,128)(2,1)S(1)}, bf16[16,2048]{1,0:T(8,128)(2,1)S(1)}) fusion(f32[16,8,2048]{2,1,0:T(8,128)S(1)} %convolution_bitcast_fusion.1, f32[8,2048]{1,0:T(8,128)S(1)} %get-tuple-element.14, f32[8,2048]{1,0:T(8,128)S(1)} %get-tuple-element.13, bf16[1024,2048]{1,0:T(8,128)(2,1)S(1)} %select_convert_fusion, ...), kind=kOutput, calls=%fused_computation.19 | convolution fusion | flops 538902528 | bytes 5767168 | tf_op jit(solution)/shard_map/dot_general | solution.py:96
  11.4 21.3 %collective-permute-start.1 = (bf16[2,16,2048]{2,1,0:T(8,128)(2,1)S(1)}, bf16[2,16,2048]{2,1,0:T(8,128)(2,1)S(1)}, u32[]{:S(2)}, u32[]{:S(2)}) collective-permute-start(bf16[2,16,2048]{2,1,0:T(8,128)(2,1)S(1)} %pad_maximum_fusion.2), channel_id=1, source_target_pairs={{1,0},{2,1},{3,2},{4,3},{5,4},{6,5},{7,6},{8,7},{9,8},{10,9},{11,1... | collective-permute-start | bytes 393224 | tf_op jit(solution)/shard_map/ppermute | solution.py:106
  32.7 2.1 %collective-permute-start = (bf16[2,16,2048]{2,1,0:T(8,128)(2,1)S(1)}, bf16[2,16,2048]{2,1,0:T(8,128)(2,1)S(1)}, u32[]{:S(2)}, u32[]{:S(2)}) collective-permute-start(bf16[2,16,2048]{2,1,0:T(8,128)(2,1)S(1)} %pad_maximum_fusion.2), channel_id=1, source_target_pairs={{0,1},{1,2},{2,3},{3,4},{4,5},{5,6},{6,7},{7,8},{8,9},{9,10},{10,1... | collective-permute-start | bytes 393224 | tf_op jit(solution)/shard_map/ppermute | solution.py:105
  34.9 0.1 dynamic_slice.11
  35.0 0.1 lt.30
  35.1 0.1 subtract_bitcast_fusion
  35.1 0.1 eq.70
  35.2 0.1 eq.66
  35.3 0.9 %fusion.7.pick_cls_ref = bf16[432,316]{1,0:T(8,128)(2,1)} fusion(s32[432]{0:T(512)S(1)} %eq.66), kind=kLoop, calls=%fused_computation.21 | loop fusion | flops 273024 | bytes 274752 | tf_op jit(solution)/shard_map/convert_element_type | solution.py:57
  36.2 7.8 %fusion.6 = (bf16[2,316,2048]{2,1,0:T(8,128)(2,1)}, bf16[2,316,2048]{2,1,0:T(8,128)(2,1)}) fusion(f32[316,2,2048]{2,1,0:T(2,128)} %param.15), kind=kLoop, calls=%fused_computation.10 | loop fusion | flops 5177344 | bytes 10354688 | tf_op jit(solution)/shard_map/convert_element_type | solution.py:80
  44.0 0.8 %fusion.21.pick_box_ref = bf16[432,48]{1,0:T(8,128)(2,1)} fusion(s32[432]{0:T(512)S(1)} %eq.70, pred[432]{0:T(512)(128)(4,1)S(1)} %lt.30), kind=kLoop, calls=%fused_computation.37 | loop fusion | flops 62208 | bytes 43632 | tf_op jit(solution)/shard_map/convert_element_type | solution.py:56
  44.8 0.8 %pad_maximum_fusion.1.win_ref = bf16[2,48,2048]{2,1,0:T(8,128)(2,1)} fusion(bf16[2,16,2048]{2,1,0:T(8,128)(2,1)S(1)} %collective-permute-done.1, bf16[1,16,2048]{2,1,0:T(8,128)(2,1)S(1)} %bitcast.57, bf16[1,16,2048]{2,1,0:T(8,128)(2,1)S(1)} %bitcast.55, bf16[2,16,2048]{2,1,0:T(8,128)(2,1)S(1)} %collective-permute-done), kind=kLoop, calls=%fused_computation.32 | loop fusion | flops 1572864 | bytes 786432 | tf_op jit(solution)/shard_map/concatenate | solution.py:107
  45.6 7.9 %shard_map.82 = bf16[2,16,2048]{2,1,0:T(8,128)(2,1)} custom-call(bf16[432,316]{1,0:T(8,128)(2,1)} %fusion.7.pick_cls_ref, bf16[432,48]{1,0:T(8,128)(2,1)} %fusion.21.pick_box_ref, bf16[2,316,2048]{2,1,0:T(8,128)(2,1)} %get-tuple-element.8.high_ref, bf16[2,316,2048]{2,1,0:T(8,128)(2,1)} %get-tuple-element.7.low_ref, ...), custom_call_target="tpu_custom_call" | custom-call | tf_op jit(solution)/shard_map/pallas_call | solution.py:61
  53.4 1.1 %convert_element_type.38 = f32[2,16,2048]{2,1,0:T(8,128)S(1)} convert(bf16[2,16,2048]{2,1,0:T(8,128)(2,1)} %shard_map.82) | non-fusion elementwise | flops 65536 | bytes 393216 | tf_op jit(solution)/shard_map/convert_element_type | solution.py:115
  54.5 3.9 %convolution_bitcast_fusion.2 = f32[128,1,1024]{2,0,1:T(8,128)S(1)} fusion(bf16[1024,2048]{1,0:T(8,128)(2,1)} %copy-done, f32[16,2048]{1,0:T(8,128)S(1)} %get-tuple-element.12, f32[16,2048]{1,0:T(8,128)S(1)} %get-tuple-element.11, f32[8,2048]{1,0:T(8,128)S(1)} %get-tuple-element.14, f32[8,2048]{1,0:T(8,128)S(1)} %get-tuple-element.13), kind=kOutput, calls=%fused_computation.13 | convolution fusion | flops 537919488 | bytes 5111808 | tf_op jit(solution)/shard_map/dot_general | solution.py:122
  58.5 1.5 %convolution_bitcast_fusion.3 = f32[128,1,1024]{2,0,1:T(8,128)S(1)} fusion(bf16[1024,2048]{1,0:T(8,128)(2,1)S(1)} %copy-done.1, f32[16,2048]{1,0:T(8,128)S(1)} %get-tuple-element.12, f32[16,2048]{1,0:T(8,128)S(1)} %get-tuple-element.11, f32[8,2048]{1,0:T(8,128)S(1)} %get-tuple-element.14, f32[8,2048]{1,0:T(8,128)S(1)} %get-tuple-element.13), kind=kOutput, calls=%fused_computation.14 | convolution fusion | flops 537919488 | bytes 5111808 | tf_op jit(solution)/shard_map/dot_general | solution.py:121
  60.0 0.1 pad_maximum_fusion
  60.1 1.8 %copy.14 = f32[128,2,1024]{2,1,0:T(2,128)} copy(f32[128,2,1024]{2,0,1:T(8,128)S(1)} %pad_maximum_fusion) | data formatting | bytes 2097152 | tf_op jit(solution)/shard_map/stack | solution.py:123
  (14 shorter events, 0.1 us)
Async XLA Ops:
  9.0 2.3 %copy-start = (bf16[1024,2048]{1,0:T(8,128)(2,1)}, bf16[1024,2048]{1,0:T(8,128)(2,1)S(1)}, u32[]{:S(2)}) copy-start(bf16[1024,2048]{1,0:T(8,128)(2,1)S(1)} %select_convert_fusion) | copy-start | bytes 12582916
  9.8 25.1 %copy-start.4 = (s32[128]{0:T(128)S(1)}, s32[128]{0:T(128)}, u32[]{:S(2)}) copy-start(s32[128]{0:T(128)} %param.14) | copy-start | bytes 1540
  9.8 25.2 %copy-start.2 = (s32[128,27]{0,1:T(8,128)S(1)}, s32[128,27]{0,1:T(8,128)}, u32[]{:S(2)}) copy-start(s32[128,27]{0,1:T(8,128)} %param.12) | copy-start | bytes 41476
  9.8 25.2 %copy-start.3 = (s32[128,27]{0,1:T(8,128)S(1)}, s32[128,27]{0,1:T(8,128)}, u32[]{:S(2)}) copy-start(s32[128,27]{0,1:T(8,128)} %param.13) | copy-start | bytes 41476
  11.4 33.4 %collective-permute-start.1 = (bf16[2,16,2048]{2,1,0:T(8,128)(2,1)S(1)}, bf16[2,16,2048]{2,1,0:T(8,128)(2,1)S(1)}, u32[]{:S(2)}, u32[]{:S(2)}) collective-permute-start(bf16[2,16,2048]{2,1,0:T(8,128)(2,1)S(1)} %pad_maximum_fusion.2), channel_id=1, source_target_pairs={{1,0},{2,1},{3,2},{4,3},{5,4},{6,5},{7,6},{8,7},{9,8},{10,9},{11,1... | collective-permute-start | bytes 393224 | tf_op jit(solution)/shard_map/ppermute | solution.py:106
  32.7 12.1 %collective-permute-start = (bf16[2,16,2048]{2,1,0:T(8,128)(2,1)S(1)}, bf16[2,16,2048]{2,1,0:T(8,128)(2,1)S(1)}, u32[]{:S(2)}, u32[]{:S(2)}) collective-permute-start(bf16[2,16,2048]{2,1,0:T(8,128)(2,1)S(1)} %pad_maximum_fusion.2), channel_id=1, source_target_pairs={{0,1},{1,2},{2,3},{3,4},{4,5},{5,6},{6,7},{7,8},{8,9},{9,10},{10,1... | collective-permute-start | bytes 393224 | tf_op jit(solution)/shard_map/ppermute | solution.py:105
  53.4 5.0 %copy-start.1 = (bf16[1024,2048]{1,0:T(8,128)(2,1)S(1)}, bf16[1024,2048]{1,0:T(8,128)(2,1)}, u32[]{:S(2)}) copy-start(bf16[1024,2048]{1,0:T(8,128)(2,1)} %copy-done) | copy-start | bytes 12582916

commit v6 on v4

--- a/solution.py
+++ b/solution.py
@@ -20,7 +20,7 @@
     return dense.astype(jnp.bfloat16)
 
 
-def translate_kernel(pick_cls_ref, pick_box_ref, ops_ref, win_ref, out_ref):
+def translate_kernel(pick_cls_ref, pick_box_ref, ops_ref, win_ref, cos_ref, sin_ref, out_ref):
     f32 = jnp.float32
     pick_cls = pick_cls_ref[...]
     pick_box = pick_box_ref[...]
@@ -30,17 +30,23 @@
     p_im = jnp.dot(pick_box, win_ref[1], preferred_element_type=f32)
     real_part = t_re * p_re - t_im * p_im
     imag_part = t_re * p_im + t_im * p_re
-    rows = out_ref.shape[1]
+    rows = out_ref.shape[1] // 8
     acc_re = real_part[0:rows]
     acc_im = imag_part[0:rows]
     for slot in range(1, real_part.shape[0] // rows):
         acc_re = acc_re + real_part[slot * rows:(slot + 1) * rows]
         acc_im = acc_im + imag_part[slot * rows:(slot + 1) * rows]
-    out_ref[0] = acc_re.astype(out_ref.dtype)
-    out_ref[1] = acc_im.astype(out_ref.dtype)
+    local_re = acc_re.astype(jnp.bfloat16).astype(f32)[:, None, :]
+    local_im = acc_im.astype(jnp.bfloat16).astype(f32)[:, None, :]
+    cosines = cos_ref[...][None]
+    sines = sin_ref[...][None]
+    spread_re = local_re * cosines + local_im * sines
+    spread_im = local_im * cosines - local_re * sines
+    out_ref[0] = spread_re.reshape(out_ref.shape[1], -1).astype(out_ref.dtype)
+    out_ref[1] = spread_im.reshape(out_ref.shape[1], -1).astype(out_ref.dtype)
 
 
-def translate(window, translation, rel_box, classes, counts):
+def translate(window, translation, rel_box, classes, counts, cosines, sines):
     rows, far = classes.shape
     width = window.shape[1]
     nclass = translation.shape[0]
@@ -59,17 +65,19 @@
     slots_rows = pick_cls.shape[0]
     return pl.pallas_call(
         translate_kernel,
-        out_shape=jax.ShapeDtypeStruct((2, rows, k_high), jnp.bfloat16),
+        out_shape=jax.ShapeDtypeStruct((2, rows * 8, k_high), jnp.bfloat16),
         grid=(k_high // CHUNK,),
         in_specs=[
             pl.BlockSpec((slots_rows, pick_cls.shape[1]), lambda j: (0, 0)),
             pl.BlockSpec((slots_rows, width), lambda j: (0, 0)),
             pl.BlockSpec((2, ops.shape[1], CHUNK), lambda j: (0, 0, j)),
             pl.BlockSpec((2, width, CHUNK), lambda j: (0, 0, j)),
+            pl.BlockSpec((8, CHUNK), lambda j: (0, j)),
+            pl.BlockSpec((8, CHUNK), lambda j: (0, j)),
         ],
-        out_specs=pl.BlockSpec((2, rows, CHUNK), lambda j: (0, 0, j)),
+        out_specs=pl.BlockSpec((2, rows * 8, CHUNK), lambda j: (0, 0, j)),
         interpret=INTERPRET,
-    )(pick_cls, pick_box, ops, window)
+    )(pick_cls, pick_box, ops, window, cosines, sines)
 
 
 def split_parts(values):
@@ -110,11 +118,9 @@
         my_class = lax.dynamic_slice_in_dim(far_class, first, parents_here, 0)
         my_count = lax.dynamic_slice_in_dim(far_count, first, parents_here, 0)
         rel_box = my_box - (device * parents_here - REACH)
-        local = translate(window, translation, rel_box, my_class, my_count).astype(f32)
-        local_re = local[0][:, None]
-        local_im = local[1][:, None]
-        spread_re = (local_re * cosines + local_im * sines).astype(jnp.bfloat16).reshape(-1, high_width)
-        spread_im = (local_im * cosines - local_re * sines).astype(jnp.bfloat16).reshape(-1, high_width)
+        spread = translate(window, translation, rel_box, my_class, my_count, cosines, sines)
+        spread_re = spread[0]
+        spread_im = spread[1]
         contract = (((1,), (1,)), ((), ()))
         out_re = lax.dot_general(spread_re, interp, contract, preferred_element_type=f32)
         out_im = lax.dot_general(spread_im, interp, contract, preferred_element_type=f32)

time: 60.3 us -> 60 us (level)
  other arithmetic: 17.4 us -> 16.3 us
  Pallas kernels: 7 us -> 7.74 us
    convert_element_type x1 -> x0, other arithmetic: 1.07 us -> none  [body(): translate(window, translation, rel_box, my_class, my_count).astype(f32)]
    pallas_call x1, Pallas kernels: 7 us -> 7.74 us  [translate(): pl.pallas_call(translate_kernel, out_shape=jax.ShapeDtypeStruct((2, rows...]
  transfers between devices with their start and end apart: 2 -> 2, of which waited for: 0 -> 0; matrix products, arithmetic and copies ran while one was open for 18% -> 19% of each run, Pallas kernels for 0% -> 0%
where the time goes in v6:
time: 60 us; the launch traced here: 59.7 us
  starting transfers between devices  23.4 us (39%)
  other arithmetic  16.3 us (27%)
  matrix products  7.82 us (13%)
  Pallas kernels  7.74 us (13%)
  local copies, waits for them, and re-layouts  4.24 us (7%)
    ppermute x1, starting transfers between devices, body(): after = lax.ppermute(parent[:, :REACH], axes, down)  21.3 us
    pallas_call x1, Pallas kernels, translate(): pl.pallas_call(translate_kernel, out_shape=jax.ShapeDtypeStruct((2, rows...  7.74 us
    convert_element_type x1, other arithmetic, split_parts(): high.astype(jnp.bfloat16)  5.4 us
    convert_element_type x1, other arithmetic, build_interp(): return dense.astype(jnp.bfloat16)  4.67 us
    dot_general x1, matrix products, body(): lax.dot_general(spread_im, interp, contract, preferred_element_type=f32)  4.01 us
    transpose x1, other arithmetic, translate(): ops = split_parts(translation).transpose(1, 0, 2)  3.22 us
    ppermute x1, starting transfers between devices, body(): before = lax.ppermute(parent[:, parents_here - REACH:], axes, up)  2.1 us
    another operation x1, local copies, waits for them, and re-layouts, body(): return jnp.stack([out_re, out_im], axis=1)  1.78 us
  transfers between devices with their start and end apart: 2, of which 0 were waited for; matrix products, arithmetic and copies ran while one was open for 19% of the time, Pallas kernels for 0%

profile of v6, /device:TPU:14, one launch (start us, length us, event | category | flops | bytes accessed | tf_op | source)
XLA Modules:
  0.0 59.7 jit_solution(1631296231961092135)
XLA Ops:
  0.0 1.1 %fusion.11 = (f32[1,2048]{1,0:T(1,128)S(1)}, f32[1,2048]{1,0:T(1,128)S(1)}, f32[1,2048]{1,0:T(1,128)S(1)}, f32[1,2048]{1,0:T(1,128)S(1)}, f32[1,2048]{1,0:T(1,128)S(1)}, /*index=5*/f32[1,2048]{1,0:T(1,128)S(1)}) fusion(f32[6,2048]{1,0:T(8,128)} %bitcast.53), kind=kLoop, calls=%fused_computation.37 | loop fusion | bytes 98304 | tf_op jit(solution)/shard_map/slice | solution.py:19
  1.1 4.7 %select_convert_fusion = bf16[1024,2048]{1,0:T(8,128)(2,1)S(1)} fusion(f32[2048]{0:T(1024)S(1)} %bitcast.55, f32[2048]{0:T(1024)S(1)} %bitcast.56, f32[2048]{0:T(1024)S(1)} %bitcast.57, f32[2048]{0:T(1024)S(1)} %bitcast.58, f32[2048]{0:T(1024)S(1)} %bitcast.59, f32[2048]{0:T(1024)S(1)} %bitcast.54, s32[2048]{0:T(1024)} %param.10), kind=kLoop, calls=%fused_computation | loop fusion | flops 27262976 | bytes 4251648 | tf_op jit(solution)/shard_map/convert_element_type | solution.py:20
  5.8 0.7 %fusion.9 = (bf16[128,1,1024]{2,1,0:T(2,128)(2,1)S(1)}, bf16[128,1,1024]{2,1,0:T(2,128)(2,1)S(1)}) fusion(bf16[128,2,1024]{2,1,0:T(2,128)(2,1)S(1)} %copy-done.3), kind=kLoop, calls=%fused_computation.35 | loop fusion | bytes 1048576 | tf_op jit(solution)/shard_map/slice | solution.py:101
  6.6 0.2 fusion.10
  6.8 0.7 %convolution_bitcast_fusion.1 = f32[16,8,2048]{2,1,0:T(8,128)S(1)} fusion(bf16[1024,2048]{1,0:T(8,128)(2,1)S(1)} %select_convert_fusion, bf16[128,1,1024]{2,1,0:T(2,128)(2,1)S(1)} %get-tuple-element.9), kind=kOutput, calls=%fused_computation.13 | convolution fusion | flops 536870912 | bytes 5505024 | tf_op jit(solution)/shard_map/dot_general | solution.py:101
  7.6 1.5 %subtract_reduce_fusion = (bf16[16,2048]{1,0:T(8,128)(2,1)S(1)}, bf16[16,2048]{1,0:T(8,128)(2,1)S(1)}) fusion(f32[16,8,2048]{2,1,0:T(8,128)S(1)} %convolution_bitcast_fusion.1, f32[8,2048]{1,0:T(8,128)S(1)} %get-tuple-element.12.sin_ref, f32[8,2048]{1,0:T(8,128)S(1)} %get-tuple-element.11.cos_ref, bf16[1024,2048]{1,0:T(8,128)(2,1)S(1)} %select_convert_fusion, ...), kind=kOutput, calls=%fused_computation.19 | convolution fusion | flops 538902528 | bytes 5767168 | tf_op jit(solution)/shard_map/dot_general | solution.py:102
  9.2 21.3 %collective-permute-start.1 = (bf16[2,16,2048]{2,1,0:T(8,128)(2,1)S(1)}, bf16[2,16,2048]{2,1,0:T(8,128)(2,1)S(1)}, u32[]{:S(2)}, u32[]{:S(2)}) collective-permute-start(bf16[2,16,2048]{2,1,0:T(8,128)(2,1)S(1)} %pad_maximum_fusion.2), channel_id=1, source_target_pairs={{1,0},{2,1},{3,2},{4,3},{5,4},{6,5},{7,6},{8,7},{9,8},{10,9},{11,1... | collective-permute-start | bytes 393224 | tf_op jit(solution)/shard_map/ppermute | solution.py:112
  30.6 2.1 %collective-permute-start = (bf16[2,16,2048]{2,1,0:T(8,128)(2,1)S(1)}, bf16[2,16,2048]{2,1,0:T(8,128)(2,1)S(1)}, u32[]{:S(2)}, u32[]{:S(2)}) collective-permute-start(bf16[2,16,2048]{2,1,0:T(8,128)(2,1)S(1)} %pad_maximum_fusion.2), channel_id=1, source_target_pairs={{0,1},{1,2},{2,3},{3,4},{4,5},{5,6},{6,7},{7,8},{8,9},{9,10},{10,1... | collective-permute-start | bytes 393224 | tf_op jit(solution)/shard_map/ppermute | solution.py:111
  32.7 0.1 subtract_bitcast_fusion
  32.8 0.1 eq.66
  32.9 0.2 iota_compare_fusion
  33.0 0.1 eq.70
  33.1 0.1 dynamic_slice.11
  33.2 0.1 lt.30
  33.3 5.4 %reduce-precision_convert_fusion = (bf16[316,2,2048]{2,0,1:T(8,128)(2,1)S(1)}, bf16[316,2,2048]{2,0,1:T(8,128)(2,1)S(1)}) fusion(f32[316,2,2048]{2,1,0:T(2,128)} %param.15), kind=kLoop, calls=%fused_computation.9 | loop fusion | flops 5177344 | bytes 10354688 | tf_op jit(solution)/shard_map/convert_element_type | solution.py:86
  38.7 3.2 %maximum_bitcast_fusion.ops_ref = bf16[2,632,2048]{2,1,0:T(8,128)(2,1)} fusion(bf16[316,2,2048]{2,0,1:T(8,128)(2,1)S(1)} %get-tuple-element.8, bf16[316,2,2048]{2,0,1:T(8,128)(2,1)S(1)} %get-tuple-element.7), kind=kLoop, calls=%fused_computation.11 | loop fusion | flops 10354688 | bytes 10354688 | tf_op jit(solution)/shard_map/transpose | solution.py:63
  41.9 0.8 %fusion.8.pick_box_ref = bf16[432,48]{1,0:T(8,128)(2,1)} fusion(s32[432]{0:T(512)S(1)} %eq.70, pred[432]{0:T(512)(128)(4,1)S(1)} %lt.30), kind=kLoop, calls=%fused_computation.28 | loop fusion | flops 62208 | bytes 43632 | tf_op jit(solution)/shard_map/convert_element_type | solution.py:60
  42.7 1.1 %add_convert_fusion.pick_cls_ref = bf16[432,632]{1,0:T(8,128)(2,1)} fusion(pred[432,316]{1,0:T(8,128)(4,1)S(1)} %iota_compare_fusion), kind=kLoop, calls=%fused_computation.16 | loop fusion | flops 546048 | bytes 682560 | tf_op jit(solution)/shard_map/concatenate | solution.py:62
  43.8 0.8 %pad_maximum_fusion.1.win_ref = bf16[2,48,2048]{2,1,0:T(8,128)(2,1)} fusion(bf16[2,16,2048]{2,1,0:T(8,128)(2,1)S(1)} %collective-permute-done.1, bf16[1,16,2048]{2,1,0:T(8,128)(2,1)S(1)} %bitcast.52, bf16[1,16,2048]{2,1,0:T(8,128)(2,1)S(1)} %bitcast.50, bf16[2,16,2048]{2,1,0:T(8,128)(2,1)S(1)} %collective-permute-done), kind=kLoop, calls=%fused_computation.23 | loop fusion | flops 1572864 | bytes 786432 | tf_op jit(solution)/shard_map/concatenate | solution.py:113
  44.6 7.7 %shard_map.82 = bf16[2,128,2048]{2,1,0:T(8,128)(2,1)} custom-call(bf16[432,632]{1,0:T(8,128)(2,1)} %add_convert_fusion.pick_cls_ref, bf16[432,48]{1,0:T(8,128)(2,1)} %fusion.8.pick_box_ref, bf16[2,632,2048]{2,1,0:T(8,128)(2,1)} %maximum_bitcast_fusion.ops_ref, bf16[2,48,2048]{2,1,0:T(8,128)(2,1)} %pad_maximum_fusion.1.win_ref, f32[8,2048]{1,0:T(8,128)} %copy-done.4, ...), custom_call_target="tpu_custom_call" | custom-call | tf_op jit(solution)/shard_map/pallas_call | solution.py:66
  52.3 4.0 %convolution_bitcast_fusion.2 = f32[128,1,1024]{2,0,1:T(8,128)S(1)} fusion(bf16[1024,2048]{1,0:T(8,128)(2,1)} %copy-done, bf16[2,128,2048]{2,1,0:T(8,128)(2,1)} %shard_map.82), kind=kOutput, calls=%fused_computation.14 | convolution fusion | flops 536870912 | bytes 5242880 | tf_op jit(solution)/shard_map/dot_general | solution.py:126
  56.4 1.5 %convolution_bitcast_fusion.3 = f32[128,1,1024]{2,0,1:T(8,128)S(1)} fusion(bf16[1024,2048]{1,0:T(8,128)(2,1)S(1)} %copy-done.1, bf16[2,128,2048]{2,1,0:T(8,128)(2,1)S(1)} %copy-done.2), kind=kOutput, calls=%fused_computation.15 | convolution fusion | flops 536870912 | bytes 5242880 | tf_op jit(solution)/shard_map/dot_general | solution.py:125
  57.9 0.1 pad_maximum_fusion
  58.0 1.8 %copy.16 = f32[128,2,1024]{2,1,0:T(2,128)} copy(f32[128,2,1024]{2,0,1:T(8,128)S(1)} %pad_maximum_fusion) | data formatting | bytes 2097152 | tf_op jit(solution)/shard_map/stack | solution.py:127
  (24 shorter events, 0.1 us)
Async XLA Ops:
  0.0 5.8 %copy-start.3 = (bf16[128,2,1024]{2,1,0:T(2,128)(2,1)S(1)}, bf16[128,2,1024]{2,1,0:T(2,128)(2,1)}, u32[]{:S(2)}) copy-start(bf16[128,2,1024]{2,1,0:T(2,128)(2,1)} %param.8) | copy-start | bytes 1572868
  0.0 6.6 %copy-start.6 = (f32[8,2048]{1,0:T(8,128)S(1)}, f32[8,2048]{1,0:T(8,128)}, u32[]{:S(2)}) copy-start(f32[8,2048]{1,0:T(8,128)} %param.11) | copy-start | bytes 196612
  5.8 3.4 %copy-start = (bf16[1024,2048]{1,0:T(8,128)(2,1)}, bf16[1024,2048]{1,0:T(8,128)(2,1)S(1)}, u32[]{:S(2)}) copy-start(bf16[1024,2048]{1,0:T(8,128)(2,1)S(1)} %select_convert_fusion) | copy-start | bytes 12582916
  6.8 2.4 %copy-start.4 = (f32[8,2048]{1,0:T(8,128)}, f32[8,2048]{1,0:T(8,128)S(1)}, u32[]{:S(2)}) copy-start(f32[8,2048]{1,0:T(8,128)S(1)} %get-tuple-element.11.cos_ref) | copy-start | bytes 196612
  6.8 2.4 %copy-start.5 = (f32[8,2048]{1,0:T(8,128)}, f32[8,2048]{1,0:T(8,128)S(1)}, u32[]{:S(2)}) copy-start(f32[8,2048]{1,0:T(8,128)S(1)} %get-tuple-element.12.sin_ref) | copy-start | bytes 196612
  7.6 25.1 %copy-start.7 = (s32[128,27]{0,1:T(8,128)S(1)}, s32[128,27]{0,1:T(8,128)}, u32[]{:S(2)}) copy-start(s32[128,27]{0,1:T(8,128)} %param.12) | copy-start | bytes 41476
  7.6 25.1 %copy-start.8 = (s32[128,27]{0,1:T(8,128)S(1)}, s32[128,27]{0,1:T(8,128)}, u32[]{:S(2)}) copy-start(s32[128,27]{0,1:T(8,128)} %param.13) | copy-start | bytes 41476
  7.6 25.5 %copy-start.9 = (s32[128]{0:T(128)S(1)}, s32[128]{0:T(128)}, u32[]{:S(2)}) copy-start(s32[128]{0:T(128)} %param.14) | copy-start | bytes 1540
  9.2 34.6 %collective-permute-start.1 = (bf16[2,16,2048]{2,1,0:T(8,128)(2,1)S(1)}, bf16[2,16,2048]{2,1,0:T(8,128)(2,1)S(1)}, u32[]{:S(2)}, u32[]{:S(2)}) collective-permute-start(bf16[2,16,2048]{2,1,0:T(8,128)(2,1)S(1)} %pad_maximum_fusion.2), channel_id=1, source_target_pairs={{1,0},{2,1},{3,2},{4,3},{5,4},{6,5},{7,6},{8,7},{9,8},{10,9},{11,1... | collective-permute-start | bytes 393224 | tf_op jit(solution)/shard_map/ppermute | solution.py:112
  30.6 13.2 %collective-permute-start = (bf16[2,16,2048]{2,1,0:T(8,128)(2,1)S(1)}, bf16[2,16,2048]{2,1,0:T(8,128)(2,1)S(1)}, u32[]{:S(2)}, u32[]{:S(2)}) collective-permute-start(bf16[2,16,2048]{2,1,0:T(8,128)(2,1)S(1)} %pad_maximum_fusion.2), channel_id=1, source_target_pairs={{0,1},{1,2},{2,3},{3,4},{4,5},{5,6},{6,7},{7,8},{8,9},{9,10},{10,1... | collective-permute-start | bytes 393224 | tf_op jit(solution)/shard_map/ppermute | solution.py:111
  52.3 4.0 %copy-start.1 = (bf16[1024,2048]{1,0:T(8,128)(2,1)S(1)}, bf16[1024,2048]{1,0:T(8,128)(2,1)}, u32[]{:S(2)}) copy-start(bf16[1024,2048]{1,0:T(8,128)(2,1)} %copy-done) | copy-start | bytes 12582916
  52.3 4.0 %copy-start.2 = (bf16[2,128,2048]{2,1,0:T(8,128)(2,1)S(1)}, bf16[2,128,2048]{2,1,0:T(8,128)(2,1)}, u32[]{:S(2)}) copy-start(bf16[2,128,2048]{2,1,0:T(8,128)(2,1)} %shard_map.82) | copy-start | bytes 3145732

commit v7 on v6

--- a/solution.py
+++ b/solution.py
@@ -119,12 +119,11 @@
         my_count = lax.dynamic_slice_in_dim(far_count, first, parents_here, 0)
         rel_box = my_box - (device * parents_here - REACH)
         spread = translate(window, translation, rel_box, my_class, my_count, cosines, sines)
-        spread_re = spread[0]
-        spread_im = spread[1]
         contract = (((1,), (1,)), ((), ()))
-        out_re = lax.dot_general(spread_re, interp, contract, preferred_element_type=f32)
-        out_im = lax.dot_general(spread_im, interp, contract, preferred_element_type=f32)
-        return jnp.stack([out_re, out_im], axis=1)
+        result = lax.dot_general(
+            spread.reshape(-1, high_width), interp, contract, preferred_element_type=f32
+        )
+        return result.reshape(2, -1, low_width).transpose(1, 0, 2)
 
     return body
 

time: 60 us -> 58.2 us (0.970)
  matrix products: 7.82 us -> 6.08 us
    another operation x1 -> x0, local copies, waits for them, and re-layouts: 1.78 us -> none  [body(): return jnp.stack([out_re, out_im], axis=1)]
    transpose x0 -> x1, local copies, waits for them, and re-layouts: none -> 1.78 us  [body(): return result.reshape(2, -1, low_width).transpose(1, 0, 2)]
    dot_general x2 -> x1, matrix products: 5.53 us -> 3.79 us  [body(): lax.dot_general(spread.reshape(-1, high_width), interp, contract, preferr...]
where the time goes in v7:
time: 58.2 us; the launch traced here: 57.9 us
  starting transfers between devices  23.4 us (40%)
  other arithmetic  16.2 us (28%)
  Pallas kernels  7.74 us (13%)
  matrix products  6.08 us (10%)
  local copies, waits for them, and re-layouts  4.23 us (7%)
    ppermute x1, starting transfers between devices, body(): after = lax.ppermute(parent[:, :REACH], axes, down)  21.3 us
    pallas_call x1, Pallas kernels, translate(): pl.pallas_call(translate_kernel, out_shape=jax.ShapeDtypeStruct((2, rows...  7.74 us
    convert_element_type x1, other arithmetic, split_parts(): high.astype(jnp.bfloat16)  5.4 us
    convert_element_type x1, other arithmetic, build_interp(): return dense.astype(jnp.bfloat16)  4.67 us
    dot_general x1, matrix products, body(): lax.dot_general(spread.reshape(-1, high_width), interp, contract, preferr...  3.79 us
    transpose x1, other arithmetic, translate(): ops = split_parts(translation).transpose(1, 0, 2)  3.23 us
    ppermute x1, starting transfers between devices, body(): before = lax.ppermute(parent[:, parents_here - REACH:], axes, up)  2.1 us
    transpose x1, local copies, waits for them, and re-layouts, body(): return result.reshape(2, -1, low_width).transpose(1, 0, 2)  1.78 us
  transfers between devices with their start and end apart: 2, of which 0 were waited for; matrix products, arithmetic and copies ran while one was open for 19% of the time, Pallas kernels for 0%

profile of v7, /device:TPU:14, one launch (start us, length us, event | category | flops | bytes accessed | tf_op | source)
XLA Modules:
  0.0 57.9 jit_solution(6774992487931599149)
XLA Ops:
  0.0 1.1 %fusion.16 = (f32[1,2048]{1,0:T(1,128)S(1)}, f32[1,2048]{1,0:T(1,128)S(1)}, f32[1,2048]{1,0:T(1,128)S(1)}, f32[1,2048]{1,0:T(1,128)S(1)}, f32[1,2048]{1,0:T(1,128)S(1)}, /*index=5*/f32[1,2048]{1,0:T(1,128)S(1)}) fusion(f32[6,2048]{1,0:T(8,128)} %bitcast.49), kind=kLoop, calls=%fused_computation.35 | loop fusion | bytes 98304 | tf_op jit(solution)/shard_map/slice | solution.py:19
  1.1 4.7 %select_convert_fusion = bf16[1024,2048]{1,0:T(8,128)(2,1)S(1)} fusion(f32[2048]{0:T(1024)S(1)} %bitcast.51, f32[2048]{0:T(1024)S(1)} %bitcast.52, f32[2048]{0:T(1024)S(1)} %bitcast.53, f32[2048]{0:T(1024)S(1)} %bitcast.54, f32[2048]{0:T(1024)S(1)} %bitcast.55, f32[2048]{0:T(1024)S(1)} %bitcast.50, s32[2048]{0:T(1024)} %param.10), kind=kLoop, calls=%fused_computation | loop fusion | flops 27262976 | bytes 4251648 | tf_op jit(solution)/shard_map/convert_element_type | solution.py:20
  5.8 0.7 %fusion.14 = (bf16[128,1,1024]{2,1,0:T(2,128)(2,1)S(1)}, bf16[128,1,1024]{2,1,0:T(2,128)(2,1)S(1)}) fusion(bf16[128,2,1024]{2,1,0:T(2,128)(2,1)S(1)} %copy-done.1), kind=kLoop, calls=%fused_computation.33 | loop fusion | bytes 1048576 | tf_op jit(solution)/shard_map/slice | solution.py:101
  6.6 0.2 fusion.15
  6.8 0.7 %convolution_bitcast_fusion.1 = f32[16,8,2048]{2,1,0:T(8,128)S(1)} fusion(bf16[1024,2048]{1,0:T(8,128)(2,1)S(1)} %select_convert_fusion, bf16[128,1,1024]{2,1,0:T(2,128)(2,1)S(1)} %get-tuple-element.9), kind=kOutput, calls=%fused_computation.15 | convolution fusion | flops 536870912 | bytes 5505024 | tf_op jit(solution)/shard_map/dot_general | solution.py:101
  7.6 0.0 copy-start.5
  7.6 0.0 copy-start.6
  7.6 1.5 %subtract_reduce_fusion = (bf16[16,2048]{1,0:T(8,128)(2,1)S(1)}, bf16[16,2048]{1,0:T(8,128)(2,1)S(1)}) fusion(f32[16,8,2048]{2,1,0:T(8,128)S(1)} %convolution_bitcast_fusion.1, f32[8,2048]{1,0:T(8,128)S(1)} %get-tuple-element.12.sin_ref, f32[8,2048]{1,0:T(8,128)S(1)} %get-tuple-element.11.cos_ref, bf16[1024,2048]{1,0:T(8,128)(2,1)S(1)} %select_convert_fusion, ...), kind=kOutput, calls=%fused_computation.19 | convolution fusion | flops 538902528 | bytes 5767168 | tf_op jit(solution)/shard_map/dot_general | solution.py:102
  9.2 21.3 %collective-permute-start.1 = (bf16[2,16,2048]{2,1,0:T(8,128)(2,1)S(1)}, bf16[2,16,2048]{2,1,0:T(8,128)(2,1)S(1)}, u32[]{:S(2)}, u32[]{:S(2)}) collective-permute-start(bf16[2,16,2048]{2,1,0:T(8,128)(2,1)S(1)} %pad_maximum_fusion.1), channel_id=1, source_target_pairs={{1,0},{2,1},{3,2},{4,3},{5,4},{6,5},{7,6},{8,7},{9,8},{10,9},{11,1... | collective-permute-start | bytes 393224 | tf_op jit(solution)/shard_map/ppermute | solution.py:112
  30.6 2.1 %collective-permute-start = (bf16[2,16,2048]{2,1,0:T(8,128)(2,1)S(1)}, bf16[2,16,2048]{2,1,0:T(8,128)(2,1)S(1)}, u32[]{:S(2)}, u32[]{:S(2)}) collective-permute-start(bf16[2,16,2048]{2,1,0:T(8,128)(2,1)S(1)} %pad_maximum_fusion.1), channel_id=1, source_target_pairs={{0,1},{1,2},{2,3},{3,4},{4,5},{5,6},{6,7},{7,8},{8,9},{9,10},{10,1... | collective-permute-start | bytes 393224 | tf_op jit(solution)/shard_map/ppermute | solution.py:111
  32.7 0.1 subtract_bitcast_fusion
  32.8 0.1 eq.66
  32.9 0.2 iota_compare_fusion
  33.0 0.1 eq.70
  33.1 0.1 dynamic_slice.11
  33.2 0.1 lt.30
  33.3 5.4 %reduce-precision_convert_fusion = (bf16[316,2,2048]{2,0,1:T(8,128)(2,1)S(1)}, bf16[316,2,2048]{2,0,1:T(8,128)(2,1)S(1)}) fusion(f32[316,2,2048]{2,1,0:T(2,128)} %param.15), kind=kLoop, calls=%fused_computation.9 | loop fusion | flops 5177344 | bytes 10354688 | tf_op jit(solution)/shard_map/convert_element_type | solution.py:86
  38.7 3.2 %maximum_bitcast_fusion.ops_ref = bf16[2,632,2048]{2,1,0:T(8,128)(2,1)} fusion(bf16[316,2,2048]{2,0,1:T(8,128)(2,1)S(1)} %get-tuple-element.8, bf16[316,2,2048]{2,0,1:T(8,128)(2,1)S(1)} %get-tuple-element.7), kind=kLoop, calls=%fused_computation.11 | loop fusion | flops 10354688 | bytes 10354688 | tf_op jit(solution)/shard_map/transpose | solution.py:63
  41.9 0.8 %fusion.13.pick_box_ref = bf16[432,48]{1,0:T(8,128)(2,1)} fusion(s32[432]{0:T(512)S(1)} %eq.70, pred[432]{0:T(512)(128)(4,1)S(1)} %lt.30), kind=kLoop, calls=%fused_computation.26 | loop fusion | flops 62208 | bytes 43632 | tf_op jit(solution)/shard_map/convert_element_type | solution.py:60
  42.8 1.0 %add_convert_fusion.pick_cls_ref = bf16[432,632]{1,0:T(8,128)(2,1)} fusion(pred[432,316]{1,0:T(8,128)(4,1)S(1)} %iota_compare_fusion), kind=kLoop, calls=%fused_computation.17 | loop fusion | flops 546048 | bytes 682560 | tf_op jit(solution)/shard_map/concatenate | solution.py:62
  43.8 0.8 %pad_maximum_fusion.win_ref = bf16[2,48,2048]{2,1,0:T(8,128)(2,1)} fusion(bf16[2,16,2048]{2,1,0:T(8,128)(2,1)S(1)} %collective-permute-done.1, bf16[1,16,2048]{2,1,0:T(8,128)(2,1)S(1)} %bitcast.48, bf16[1,16,2048]{2,1,0:T(8,128)(2,1)S(1)} %bitcast.46, bf16[2,16,2048]{2,1,0:T(8,128)(2,1)S(1)} %collective-permute-done), kind=kLoop, calls=%fused_computation.21 | loop fusion | flops 1572864 | bytes 786432 | tf_op jit(solution)/shard_map/concatenate | solution.py:113
  44.6 7.7 %shard_map.82 = bf16[2,128,2048]{2,1,0:T(8,128)(2,1)} custom-call(bf16[432,632]{1,0:T(8,128)(2,1)} %add_convert_fusion.pick_cls_ref, bf16[432,48]{1,0:T(8,128)(2,1)} %fusion.13.pick_box_ref, bf16[2,632,2048]{2,1,0:T(8,128)(2,1)} %maximum_bitcast_fusion.ops_ref, bf16[2,48,2048]{2,1,0:T(8,128)(2,1)} %pad_maximum_fusion.win_ref, f32[8,2048]{1,0:T(8,128)} %copy-done.2, ...), custom_call_target="tpu_custom_call" | custom-call | tf_op jit(solution)/shard_map/pallas_call | solution.py:66
  52.3 3.8 %fusion.9 = f32[128,2,1024]{2,0,1:T(8,128)S(1)} fusion(bf16[2,128,2048]{2,1,0:T(8,128)(2,1)} %shard_map.82, bf16[1024,2048]{1,0:T(8,128)(2,1)} %copy-done), kind=kOutput, calls=%fused_computation.16 | convolution fusion | flops 1073741824 | bytes 6291456 | tf_op jit(solution)/shard_map/dot_general | solution.py:123
  56.1 1.8 %copy.16 = f32[128,2,1024]{2,1,0:T(2,128)} copy(f32[128,2,1024]{2,0,1:T(8,128)S(1)} %fusion.9) | data formatting | bytes 2097152 | tf_op jit(solution)/shard_map/transpose | solution.py:126
  (18 shorter events, 0.1 us)
Async XLA Ops:
  0.0 5.8 %copy-start.1 = (bf16[128,2,1024]{2,1,0:T(2,128)(2,1)S(1)}, bf16[128,2,1024]{2,1,0:T(2,128)(2,1)}, u32[]{:S(2)}) copy-start(bf16[128,2,1024]{2,1,0:T(2,128)(2,1)} %param.8) | copy-start | bytes 1572868
  0.0 6.6 %copy-start.4 = (f32[8,2048]{1,0:T(8,128)S(1)}, f32[8,2048]{1,0:T(8,128)}, u32[]{:S(2)}) copy-start(f32[8,2048]{1,0:T(8,128)} %param.11) | copy-start | bytes 196612
  5.8 3.4 %copy-start = (bf16[1024,2048]{1,0:T(8,128)(2,1)}, bf16[1024,2048]{1,0:T(8,128)(2,1)S(1)}, u32[]{:S(2)}) copy-start(bf16[1024,2048]{1,0:T(8,128)(2,1)S(1)} %select_convert_fusion) | copy-start | bytes 12582916
  6.8 2.4 %copy-start.2 = (f32[8,2048]{1,0:T(8,128)}, f32[8,2048]{1,0:T(8,128)S(1)}, u32[]{:S(2)}) copy-start(f32[8,2048]{1,0:T(8,128)S(1)} %get-tuple-element.11.cos_ref) | copy-start | bytes 196612
  6.8 2.4 %copy-start.3 = (f32[8,2048]{1,0:T(8,128)}, f32[8,2048]{1,0:T(8,128)S(1)}, u32[]{:S(2)}) copy-start(f32[8,2048]{1,0:T(8,128)S(1)} %get-tuple-element.12.sin_ref) | copy-start | bytes 196612
  7.6 25.1 %copy-start.5 = (s32[128,27]{0,1:T(8,128)S(1)}, s32[128,27]{0,1:T(8,128)}, u32[]{:S(2)}) copy-start(s32[128,27]{0,1:T(8,128)} %param.12) | copy-start | bytes 41476
  7.6 25.1 %copy-start.6 = (s32[128,27]{0,1:T(8,128)S(1)}, s32[128,27]{0,1:T(8,128)}, u32[]{:S(2)}) copy-start(s32[128,27]{0,1:T(8,128)} %param.13) | copy-start | bytes 41476
  7.6 25.5 %copy-start.7 = (s32[128]{0:T(128)S(1)}, s32[128]{0:T(128)}, u32[]{:S(2)}) copy-start(s32[128]{0:T(128)} %param.14) | copy-start | bytes 1540
  9.2 34.6 %collective-permute-start.1 = (bf16[2,16,2048]{2,1,0:T(8,128)(2,1)S(1)}, bf16[2,16,2048]{2,1,0:T(8,128)(2,1)S(1)}, u32[]{:S(2)}, u32[]{:S(2)}) collective-permute-start(bf16[2,16,2048]{2,1,0:T(8,128)(2,1)S(1)} %pad_maximum_fusion.1), channel_id=1, source_target_pairs={{1,0},{2,1},{3,2},{4,3},{5,4},{6,5},{7,6},{8,7},{9,8},{10,9},{11,1... | collective-permute-start | bytes 393224 | tf_op jit(solution)/shard_map/ppermute | solution.py:112
  30.6 13.2 %collective-permute-start = (bf16[2,16,2048]{2,1,0:T(8,128)(2,1)S(1)}, bf16[2,16,2048]{2,1,0:T(8,128)(2,1)S(1)}, u32[]{:S(2)}, u32[]{:S(2)}) collective-permute-start(bf16[2,16,2048]{2,1,0:T(8,128)(2,1)S(1)} %pad_maximum_fusion.1), channel_id=1, source_target_pairs={{0,1},{1,2},{2,3},{3,4},{4,5},{5,6},{6,7},{7,8},{8,9},{9,10},{10,1... | collective-permute-start | bytes 393224 | tf_op jit(solution)/shard_map/ppermute | solution.py:111

commit v8 on v7

--- a/solution.py
+++ b/solution.py
@@ -13,11 +13,11 @@
 
 def build_interp(interp_band, band_start):
     offset = jnp.arange(K_LOW, dtype=jnp.int32)[:, None] - band_start[None, :]
-    weights = interp_band.T
-    dense = jnp.zeros((K_LOW, interp_band.shape[0]), jnp.float32)
+    weights = interp_band.T.astype(jnp.bfloat16)
+    dense = jnp.zeros((K_LOW, interp_band.shape[0]), jnp.bfloat16)
     for column in range(interp_band.shape[1]):
         dense = jnp.where(offset == column, weights[column][None, :], dense)
-    return dense.astype(jnp.bfloat16)
+    return dense
 
 
 def translate_kernel(pick_cls_ref, pick_box_ref, ops_ref, win_ref, cos_ref, sin_ref, out_ref):

time: 58.2 us -> 58.1 us (level)
  local copies, waits for them, and re-layouts: 4.23 us -> 3.25 us
  other arithmetic: 16.2 us -> 17.1 us
    select_n x0 -> x1, other arithmetic: none -> 4.66 us  [build_interp(): dense = jnp.where(offset == column, weights[column][None, :], dense)]
    convert_element_type x1, other arithmetic: 4.67 us -> 0.91 us  [build_interp(): weights = interp_band.T.astype(jnp.bfloat16)]
    slice x1, local copies, waits for them, and re-layouts: 1.12 us -> 0.14 us  [build_interp(): dense = jnp.where(offset == column, weights[column][None, :], dense)]
where the time goes in v8:
time: 58.1 us; the launch traced here: 57.8 us
  starting transfers between devices  23.4 us (40%)
  other arithmetic  17.1 us (29%)
  Pallas kernels  7.74 us (13%)
  matrix products  6.07 us (10%)
  local copies, waits for them, and re-layouts  3.25 us (6%)
    ppermute x1, starting transfers between devices, body(): after = lax.ppermute(parent[:, :REACH], axes, down)  21.3 us
    pallas_call x1, Pallas kernels, translate(): pl.pallas_call(translate_kernel, out_shape=jax.ShapeDtypeStruct((2, rows...  7.74 us
    convert_element_type x1, other arithmetic, split_parts(): high.astype(jnp.bfloat16)  5.4 us
    select_n x1, other arithmetic, build_interp(): dense = jnp.where(offset == column, weights[column][None, :], dense)  4.66 us
    dot_general x1, matrix products, body(): lax.dot_general(spread.reshape(-1, high_width), interp, contract, preferr...  3.79 us
    transpose x1, other arithmetic, translate(): ops = split_parts(translation).transpose(1, 0, 2)  3.21 us
    ppermute x1, starting transfers between devices, body(): before = lax.ppermute(parent[:, parents_here - REACH:], axes, up)  2.1 us
    transpose x1, local copies, waits for them, and re-layouts, body(): return result.reshape(2, -1, low_width).transpose(1, 0, 2)  1.78 us
  transfers between devices with their start and end apart: 2, of which 0 were waited for; matrix products, arithmetic and copies ran while one was open for 19% of the time, Pallas kernels for 0%

profile of v8, /device:TPU:14, one launch (start us, length us, event | category | flops | bytes accessed | tf_op | source)
XLA Modules:
  0.0 57.8 jit_solution(16485381576630815830)
XLA Ops:
  0.0 0.9 %convert_bitcast_fusion.2 = bf16[6,2048]{1,0:T(8,128)(2,1)S(1)} fusion(f32[2048,6]{0,1:T(8,128)} %param.9), kind=kLoop, calls=%fused_computation.35 | loop fusion | flops 12288 | bytes 73728 | tf_op jit(solution)/shard_map/convert_element_type | solution.py:16
  0.9 0.1 slice_reduce_fusion.5
  1.1 4.7 %fusion.6 = bf16[1024,2048]{1,0:T(8,128)(2,1)S(1)} fusion(s32[2048]{0:T(1024)} %param.10, bf16[2048]{0:T(1024)(128)(2,1)S(1)} %get-tuple-element.8, bf16[2048]{0:T(1024)(128)(2,1)S(1)} %get-tuple-element.9, bf16[2048]{0:T(1024)(128)(2,1)S(1)} %get-tuple-element.10, bf16[2048]{0:T(1024)(128)(2,1)S(1)} %get-tuple-element.11, ...), kind=kLoop, calls=%fused_computation.7 | loop fusion | flops 27262976 | bytes 4227072 | tf_op jit(solution)/shard_map/jit(_where)/select_n | solution.py:19
  5.7 0.7 %fusion.20 = (bf16[128,1,1024]{2,1,0:T(2,128)(2,1)S(1)}, bf16[128,1,1024]{2,1,0:T(2,128)(2,1)S(1)}) fusion(bf16[128,2,1024]{2,1,0:T(2,128)(2,1)S(1)} %copy-done.1), kind=kLoop, calls=%fused_computation.45 | loop fusion | bytes 1048576 | tf_op jit(solution)/shard_map/slice | solution.py:101
  6.5 0.2 fusion.21
  6.8 0.7 %convolution_bitcast_fusion.1 = f32[16,8,2048]{2,1,0:T(8,128)S(1)} fusion(bf16[1024,2048]{1,0:T(8,128)(2,1)S(1)} %fusion.6, bf16[128,1,1024]{2,1,0:T(2,128)(2,1)S(1)} %get-tuple-element.15), kind=kOutput, calls=%fused_computation.20 | convolution fusion | flops 536870912 | bytes 5505024 | tf_op jit(solution)/shard_map/dot_general | solution.py:101
  7.5 0.0 copy-start.6
  7.5 1.5 %subtract_reduce_fusion = (bf16[16,2048]{1,0:T(8,128)(2,1)S(1)}, bf16[16,2048]{1,0:T(8,128)(2,1)S(1)}) fusion(f32[16,8,2048]{2,1,0:T(8,128)S(1)} %convolution_bitcast_fusion.1, f32[8,2048]{1,0:T(8,128)S(1)} %get-tuple-element.18.sin_ref, f32[8,2048]{1,0:T(8,128)S(1)} %get-tuple-element.17.cos_ref, bf16[1024,2048]{1,0:T(8,128)(2,1)S(1)} %fusion.6, ...), kind=kOutput, calls=%fused_computation.24 | convolution fusion | flops 538902528 | bytes 5767168 | tf_op jit(solution)/shard_map/dot_general | solution.py:102
  9.1 21.3 %collective-permute-start.1 = (bf16[2,16,2048]{2,1,0:T(8,128)(2,1)S(1)}, bf16[2,16,2048]{2,1,0:T(8,128)(2,1)S(1)}, u32[]{:S(2)}, u32[]{:S(2)}) collective-permute-start(bf16[2,16,2048]{2,1,0:T(8,128)(2,1)S(1)} %pad_maximum_fusion.1), channel_id=1, source_target_pairs={{1,0},{2,1},{3,2},{4,3},{5,4},{6,5},{7,6},{8,7},{9,8},{10,9},{11,1... | collective-permute-start | bytes 393224 | tf_op jit(solution)/shard_map/ppermute | solution.py:112
  30.5 2.1 %collective-permute-start = (bf16[2,16,2048]{2,1,0:T(8,128)(2,1)S(1)}, bf16[2,16,2048]{2,1,0:T(8,128)(2,1)S(1)}, u32[]{:S(2)}, u32[]{:S(2)}) collective-permute-start(bf16[2,16,2048]{2,1,0:T(8,128)(2,1)S(1)} %pad_maximum_fusion.1), channel_id=1, source_target_pairs={{0,1},{1,2},{2,3},{3,4},{4,5},{5,6},{6,7},{7,8},{8,9},{9,10},{10,1... | collective-permute-start | bytes 393224 | tf_op jit(solution)/shard_map/ppermute | solution.py:111
  32.6 0.1 subtract_bitcast_fusion
  32.7 0.1 eq.66
  32.8 0.2 iota_compare_fusion
  32.9 0.1 eq.70
  33.0 0.1 dynamic_slice.11
  33.1 0.1 lt.30
  33.2 5.4 %reduce-precision_convert_fusion = (bf16[316,2,2048]{2,0,1:T(8,128)(2,1)S(1)}, bf16[316,2,2048]{2,0,1:T(8,128)(2,1)S(1)}) fusion(f32[316,2,2048]{2,1,0:T(2,128)} %param.15), kind=kLoop, calls=%fused_computation.14 | loop fusion | flops 5177344 | bytes 10354688 | tf_op jit(solution)/shard_map/convert_element_type | solution.py:86
  38.6 3.2 %maximum_bitcast_fusion.ops_ref = bf16[2,632,2048]{2,1,0:T(8,128)(2,1)} fusion(bf16[316,2,2048]{2,0,1:T(8,128)(2,1)S(1)} %get-tuple-element.14, bf16[316,2,2048]{2,0,1:T(8,128)(2,1)S(1)} %get-tuple-element.13), kind=kLoop, calls=%fused_computation.16 | loop fusion | flops 10354688 | bytes 10354688 | tf_op jit(solution)/shard_map/transpose | solution.py:63
  41.8 0.8 %fusion.19.pick_box_ref = bf16[432,48]{1,0:T(8,128)(2,1)} fusion(s32[432]{0:T(512)S(1)} %eq.70, pred[432]{0:T(512)(128)(4,1)S(1)} %lt.30), kind=kLoop, calls=%fused_computation.31 | loop fusion | flops 62208 | bytes 43632 | tf_op jit(solution)/shard_map/convert_element_type | solution.py:60
  42.6 1.0 %add_convert_fusion.pick_cls_ref = bf16[432,632]{1,0:T(8,128)(2,1)} fusion(pred[432,316]{1,0:T(8,128)(4,1)S(1)} %iota_compare_fusion), kind=kLoop, calls=%fused_computation.22 | loop fusion | flops 546048 | bytes 682560 | tf_op jit(solution)/shard_map/concatenate | solution.py:62
  43.7 0.8 %pad_maximum_fusion.win_ref = bf16[2,48,2048]{2,1,0:T(8,128)(2,1)} fusion(bf16[2,16,2048]{2,1,0:T(8,128)(2,1)S(1)} %collective-permute-done.1, bf16[1,16,2048]{2,1,0:T(8,128)(2,1)S(1)} %bitcast.43, bf16[1,16,2048]{2,1,0:T(8,128)(2,1)S(1)} %bitcast.41, bf16[2,16,2048]{2,1,0:T(8,128)(2,1)S(1)} %collective-permute-done), kind=kLoop, calls=%fused_computation.26 | loop fusion | flops 1572864 | bytes 786432 | tf_op jit(solution)/shard_map/concatenate | solution.py:113
  44.5 7.7 %shard_map.82 = bf16[2,128,2048]{2,1,0:T(8,128)(2,1)} custom-call(bf16[432,632]{1,0:T(8,128)(2,1)} %add_convert_fusion.pick_cls_ref, bf16[432,48]{1,0:T(8,128)(2,1)} %fusion.19.pick_box_ref, bf16[2,632,2048]{2,1,0:T(8,128)(2,1)} %maximum_bitcast_fusion.ops_ref, bf16[2,48,2048]{2,1,0:T(8,128)(2,1)} %pad_maximum_fusion.win_ref, f32[8,2048]{1,0:T(8,128)} %copy-done.2, ...), custom_call_target="tpu_custom_call" | custom-call | tf_op jit(solution)/shard_map/pallas_call | solution.py:66
  52.2 3.8 %fusion.15 = f32[128,2,1024]{2,0,1:T(8,128)S(1)} fusion(bf16[2,128,2048]{2,1,0:T(8,128)(2,1)} %shard_map.82, bf16[1024,2048]{1,0:T(8,128)(2,1)} %copy-done), kind=kOutput, calls=%fused_computation.21 | convolution fusion | flops 1073741824 | bytes 6291456 | tf_op jit(solution)/shard_map/dot_general | solution.py:123
  56.0 1.8 %copy.16 = f32[128,2,1024]{2,1,0:T(2,128)} copy(f32[128,2,1024]{2,0,1:T(8,128)S(1)} %fusion.15) | data formatting | bytes 2097152 | tf_op jit(solution)/shard_map/transpose | solution.py:126
  (19 shorter events, 0.1 us)
Async XLA Ops:
  0.0 5.7 %copy-start.1 = (bf16[128,2,1024]{2,1,0:T(2,128)(2,1)S(1)}, bf16[128,2,1024]{2,1,0:T(2,128)(2,1)}, u32[]{:S(2)}) copy-start(bf16[128,2,1024]{2,1,0:T(2,128)(2,1)} %param.8) | copy-start | bytes 1572868
  0.0 6.5 %copy-start.4 = (f32[8,2048]{1,0:T(8,128)S(1)}, f32[8,2048]{1,0:T(8,128)}, u32[]{:S(2)}) copy-start(f32[8,2048]{1,0:T(8,128)} %param.11) | copy-start | bytes 196612
  5.7 3.4 %copy-start = (bf16[1024,2048]{1,0:T(8,128)(2,1)}, bf16[1024,2048]{1,0:T(8,128)(2,1)S(1)}, u32[]{:S(2)}) copy-start(bf16[1024,2048]{1,0:T(8,128)(2,1)S(1)} %fusion.6) | copy-start | bytes 12582916
  6.7 2.4 %copy-start.2 = (f32[8,2048]{1,0:T(8,128)}, f32[8,2048]{1,0:T(8,128)S(1)}, u32[]{:S(2)}) copy-start(f32[8,2048]{1,0:T(8,128)S(1)} %get-tuple-element.17.cos_ref) | copy-start | bytes 196612
  6.7 2.4 %copy-start.3 = (f32[8,2048]{1,0:T(8,128)}, f32[8,2048]{1,0:T(8,128)S(1)}, u32[]{:S(2)}) copy-start(f32[8,2048]{1,0:T(8,128)S(1)} %get-tuple-element.18.sin_ref) | copy-start | bytes 196612
  7.5 25.1 %copy-start.5 = (s32[128,27]{0,1:T(8,128)S(1)}, s32[128,27]{0,1:T(8,128)}, u32[]{:S(2)}) copy-start(s32[128,27]{0,1:T(8,128)} %param.12) | copy-start | bytes 41476
  7.5 25.1 %copy-start.6 = (s32[128,27]{0,1:T(8,128)S(1)}, s32[128,27]{0,1:T(8,128)}, u32[]{:S(2)}) copy-start(s32[128,27]{0,1:T(8,128)} %param.13) | copy-start | bytes 41476
  7.5 25.5 %copy-start.7 = (s32[128]{0:T(128)S(1)}, s32[128]{0:T(128)}, u32[]{:S(2)}) copy-start(s32[128]{0:T(128)} %param.14) | copy-start | bytes 1540
  9.1 34.5 %collective-permute-start.1 = (bf16[2,16,2048]{2,1,0:T(8,128)(2,1)S(1)}, bf16[2,16,2048]{2,1,0:T(8,128)(2,1)S(1)}, u32[]{:S(2)}, u32[]{:S(2)}) collective-permute-start(bf16[2,16,2048]{2,1,0:T(8,128)(2,1)S(1)} %pad_maximum_fusion.1), channel_id=1, source_target_pairs={{1,0},{2,1},{3,2},{4,3},{5,4},{6,5},{7,6},{8,7},{9,8},{10,9},{11,1... | collective-permute-start | bytes 393224 | tf_op jit(solution)/shard_map/ppermute | solution.py:112
  30.5 13.2 %collective-permute-start = (bf16[2,16,2048]{2,1,0:T(8,128)(2,1)S(1)}, bf16[2,16,2048]{2,1,0:T(8,128)(2,1)S(1)}, u32[]{:S(2)}, u32[]{:S(2)}) collective-permute-start(bf16[2,16,2048]{2,1,0:T(8,128)(2,1)S(1)} %pad_maximum_fusion.1), channel_id=1, source_target_pairs={{0,1},{1,2},{2,3},{3,4},{4,5},{5,6},{6,7},{7,8},{8,9},{9,10},{10,1... | collective-permute-start | bytes 393224 | tf_op jit(solution)/shard_map/ppermute | solution.py:111

commit v9 on v7

--- a/solution.py
+++ b/solution.py
@@ -5,7 +5,7 @@
 from jax.experimental import pallas as pl
 
 INTERPRET = False
-CHUNK = 512
+CHUNK = 1024
 
 K_LOW = 1024
 REACH = 16

time: 58.2 us -> 58.3 us (level)
  no operation moved by 1% of the time
where the time goes in v9:
time: 58.3 us; the launch traced here: 58.1 us
  starting transfers between devices  23.4 us (40%)
  other arithmetic  16.2 us (28%)
  Pallas kernels  7.91 us (14%)
  matrix products  6.08 us (10%)
  local copies, waits for them, and re-layouts  4.23 us (7%)
    ppermute x1, starting transfers between devices, body(): after = lax.ppermute(parent[:, :REACH], axes, down)  21.3 us
    pallas_call x1, Pallas kernels, translate(): pl.pallas_call(translate_kernel, out_shape=jax.ShapeDtypeStruct((2, rows...  7.91 us
    convert_element_type x1, other arithmetic, split_parts(): high.astype(jnp.bfloat16)  5.4 us
    convert_element_type x1, other arithmetic, build_interp(): return dense.astype(jnp.bfloat16)  4.67 us
    dot_general x1, matrix products, body(): lax.dot_general(spread.reshape(-1, high_width), interp, contract, preferr...  3.79 us
    transpose x1, other arithmetic, translate(): ops = split_parts(translation).transpose(1, 0, 2)  3.23 us
    ppermute x1, starting transfers between devices, body(): before = lax.ppermute(parent[:, parents_here - REACH:], axes, up)  2.1 us
    transpose x1, local copies, waits for them, and re-layouts, body(): return result.reshape(2, -1, low_width).transpose(1, 0, 2)  1.78 us
  transfers between devices with their start and end apart: 2, of which 0 were waited for; matrix products, arithmetic and copies ran while one was open for 19% of the time, Pallas kernels for 0%

profile of v9, /device:TPU:14, one launch (start us, length us, event | category | flops | bytes accessed | tf_op | source)
XLA Modules:
  0.0 58.1 jit_solution(12516957765007760171)
XLA Ops:
  0.0 1.1 %fusion.16 = (f32[1,2048]{1,0:T(1,128)S(1)}, f32[1,2048]{1,0:T(1,128)S(1)}, f32[1,2048]{1,0:T(1,128)S(1)}, f32[1,2048]{1,0:T(1,128)S(1)}, f32[1,2048]{1,0:T(1,128)S(1)}, /*index=5*/f32[1,2048]{1,0:T(1,128)S(1)}) fusion(f32[6,2048]{1,0:T(8,128)} %bitcast.49), kind=kLoop, calls=%fused_computation.35 | loop fusion | bytes 98304 | tf_op jit(solution)/shard_map/slice | solution.py:19
  1.1 4.7 %select_convert_fusion = bf16[1024,2048]{1,0:T(8,128)(2,1)S(1)} fusion(f32[2048]{0:T(1024)S(1)} %bitcast.51, f32[2048]{0:T(1024)S(1)} %bitcast.52, f32[2048]{0:T(1024)S(1)} %bitcast.53, f32[2048]{0:T(1024)S(1)} %bitcast.54, f32[2048]{0:T(1024)S(1)} %bitcast.55, f32[2048]{0:T(1024)S(1)} %bitcast.50, s32[2048]{0:T(1024)} %param.10), kind=kLoop, calls=%fused_computation | loop fusion | flops 27262976 | bytes 4251648 | tf_op jit(solution)/shard_map/convert_element_type | solution.py:20
  5.8 0.7 %fusion.14 = (bf16[128,1,1024]{2,1,0:T(2,128)(2,1)S(1)}, bf16[128,1,1024]{2,1,0:T(2,128)(2,1)S(1)}) fusion(bf16[128,2,1024]{2,1,0:T(2,128)(2,1)S(1)} %copy-done.1), kind=kLoop, calls=%fused_computation.33 | loop fusion | bytes 1048576 | tf_op jit(solution)/shard_map/slice | solution.py:101
  6.6 0.2 fusion.15
  6.8 0.7 %convolution_bitcast_fusion.1 = f32[16,8,2048]{2,1,0:T(8,128)S(1)} fusion(bf16[1024,2048]{1,0:T(8,128)(2,1)S(1)} %select_convert_fusion, bf16[128,1,1024]{2,1,0:T(2,128)(2,1)S(1)} %get-tuple-element.9), kind=kOutput, calls=%fused_computation.15 | convolution fusion | flops 536870912 | bytes 5505024 | tf_op jit(solution)/shard_map/dot_general | solution.py:101
  7.6 0.0 copy-start.5
  7.6 0.0 copy-start.7
  7.6 1.5 %subtract_reduce_fusion = (bf16[16,2048]{1,0:T(8,128)(2,1)S(1)}, bf16[16,2048]{1,0:T(8,128)(2,1)S(1)}) fusion(f32[16,8,2048]{2,1,0:T(8,128)S(1)} %convolution_bitcast_fusion.1, f32[8,2048]{1,0:T(8,128)S(1)} %get-tuple-element.12.sin_ref, f32[8,2048]{1,0:T(8,128)S(1)} %get-tuple-element.11.cos_ref, bf16[1024,2048]{1,0:T(8,128)(2,1)S(1)} %select_convert_fusion, ...), kind=kOutput, calls=%fused_computation.19 | convolution fusion | flops 538902528 | bytes 5767168 | tf_op jit(solution)/shard_map/dot_general | solution.py:102
  9.2 21.3 %collective-permute-start.1 = (bf16[2,16,2048]{2,1,0:T(8,128)(2,1)S(1)}, bf16[2,16,2048]{2,1,0:T(8,128)(2,1)S(1)}, u32[]{:S(2)}, u32[]{:S(2)}) collective-permute-start(bf16[2,16,2048]{2,1,0:T(8,128)(2,1)S(1)} %pad_maximum_fusion.1), channel_id=1, source_target_pairs={{1,0},{2,1},{3,2},{4,3},{5,4},{6,5},{7,6},{8,7},{9,8},{10,9},{11,1... | collective-permute-start | bytes 393224 | tf_op jit(solution)/shard_map/ppermute | solution.py:112
  30.6 2.1 %collective-permute-start = (bf16[2,16,2048]{2,1,0:T(8,128)(2,1)S(1)}, bf16[2,16,2048]{2,1,0:T(8,128)(2,1)S(1)}, u32[]{:S(2)}, u32[]{:S(2)}) collective-permute-start(bf16[2,16,2048]{2,1,0:T(8,128)(2,1)S(1)} %pad_maximum_fusion.1), channel_id=1, source_target_pairs={{0,1},{1,2},{2,3},{3,4},{4,5},{5,6},{6,7},{7,8},{8,9},{9,10},{10,1... | collective-permute-start | bytes 393224 | tf_op jit(solution)/shard_map/ppermute | solution.py:111
  32.7 0.1 subtract_bitcast_fusion
  32.8 0.1 eq.66
  32.9 0.2 iota_compare_fusion
  33.0 0.1 eq.70
  33.1 0.1 dynamic_slice.11
  33.2 0.1 lt.30
  33.3 5.4 %reduce-precision_convert_fusion = (bf16[316,2,2048]{2,0,1:T(8,128)(2,1)S(1)}, bf16[316,2,2048]{2,0,1:T(8,128)(2,1)S(1)}) fusion(f32[316,2,2048]{2,1,0:T(2,128)} %param.15), kind=kLoop, calls=%fused_computation.9 | loop fusion | flops 5177344 | bytes 10354688 | tf_op jit(solution)/shard_map/convert_element_type | solution.py:86
  38.7 3.2 %maximum_bitcast_fusion.ops_ref = bf16[2,632,2048]{2,1,0:T(8,128)(2,1)} fusion(bf16[316,2,2048]{2,0,1:T(8,128)(2,1)S(1)} %get-tuple-element.8, bf16[316,2,2048]{2,0,1:T(8,128)(2,1)S(1)} %get-tuple-element.7), kind=kLoop, calls=%fused_computation.11 | loop fusion | flops 10354688 | bytes 10354688 | tf_op jit(solution)/shard_map/transpose | solution.py:63
  41.9 0.8 %fusion.13.pick_box_ref = bf16[432,48]{1,0:T(8,128)(2,1)} fusion(s32[432]{0:T(512)S(1)} %eq.70, pred[432]{0:T(512)(128)(4,1)S(1)} %lt.30), kind=kLoop, calls=%fused_computation.26 | loop fusion | flops 62208 | bytes 43632 | tf_op jit(solution)/shard_map/convert_element_type | solution.py:60
  42.8 1.0 %add_convert_fusion.pick_cls_ref = bf16[432,632]{1,0:T(8,128)(2,1)} fusion(pred[432,316]{1,0:T(8,128)(4,1)S(1)} %iota_compare_fusion), kind=kLoop, calls=%fused_computation.17 | loop fusion | flops 546048 | bytes 682560 | tf_op jit(solution)/shard_map/concatenate | solution.py:62
  43.8 0.8 %pad_maximum_fusion.win_ref = bf16[2,48,2048]{2,1,0:T(8,128)(2,1)} fusion(bf16[2,16,2048]{2,1,0:T(8,128)(2,1)S(1)} %collective-permute-done.1, bf16[1,16,2048]{2,1,0:T(8,128)(2,1)S(1)} %bitcast.48, bf16[1,16,2048]{2,1,0:T(8,128)(2,1)S(1)} %bitcast.46, bf16[2,16,2048]{2,1,0:T(8,128)(2,1)S(1)} %collective-permute-done), kind=kLoop, calls=%fused_computation.21 | loop fusion | flops 1572864 | bytes 786432 | tf_op jit(solution)/shard_map/concatenate | solution.py:113
  44.6 7.9 %shard_map.82 = bf16[2,128,2048]{2,1,0:T(8,128)(2,1)} custom-call(bf16[432,632]{1,0:T(8,128)(2,1)} %add_convert_fusion.pick_cls_ref, bf16[432,48]{1,0:T(8,128)(2,1)} %fusion.13.pick_box_ref, bf16[2,632,2048]{2,1,0:T(8,128)(2,1)} %maximum_bitcast_fusion.ops_ref, bf16[2,48,2048]{2,1,0:T(8,128)(2,1)} %pad_maximum_fusion.win_ref, f32[8,2048]{1,0:T(8,128)} %copy-done.2, ...), custom_call_target="tpu_custom_call" | custom-call | tf_op jit(solution)/shard_map/pallas_call | solution.py:66
  52.5 3.8 %fusion.9 = f32[128,2,1024]{2,0,1:T(8,128)S(1)} fusion(bf16[2,128,2048]{2,1,0:T(8,128)(2,1)} %shard_map.82, bf16[1024,2048]{1,0:T(8,128)(2,1)} %copy-done), kind=kOutput, calls=%fused_computation.16 | convolution fusion | flops 1073741824 | bytes 6291456 | tf_op jit(solution)/shard_map/dot_general | solution.py:123
  56.3 1.8 %copy.16 = f32[128,2,1024]{2,1,0:T(2,128)} copy(f32[128,2,1024]{2,0,1:T(8,128)S(1)} %fusion.9) | data formatting | bytes 2097152 | tf_op jit(solution)/shard_map/transpose | solution.py:126
  (18 shorter events, 0.1 us)
Async XLA Ops:
  0.0 5.8 %copy-start.1 = (bf16[128,2,1024]{2,1,0:T(2,128)(2,1)S(1)}, bf16[128,2,1024]{2,1,0:T(2,128)(2,1)}, u32[]{:S(2)}) copy-start(bf16[128,2,1024]{2,1,0:T(2,128)(2,1)} %param.8) | copy-start | bytes 1572868
  0.0 6.6 %copy-start.4 = (f32[8,2048]{1,0:T(8,128)S(1)}, f32[8,2048]{1,0:T(8,128)}, u32[]{:S(2)}) copy-start(f32[8,2048]{1,0:T(8,128)} %param.11) | copy-start | bytes 196612
  5.8 3.4 %copy-start = (bf16[1024,2048]{1,0:T(8,128)(2,1)}, bf16[1024,2048]{1,0:T(8,128)(2,1)S(1)}, u32[]{:S(2)}) copy-start(bf16[1024,2048]{1,0:T(8,128)(2,1)S(1)} %select_convert_fusion) | copy-start | bytes 12582916
  6.8 2.4 %copy-start.2 = (f32[8,2048]{1,0:T(8,128)}, f32[8,2048]{1,0:T(8,128)S(1)}, u32[]{:S(2)}) copy-start(f32[8,2048]{1,0:T(8,128)S(1)} %get-tuple-element.11.cos_ref) | copy-start | bytes 196612
  6.8 2.4 %copy-start.3 = (f32[8,2048]{1,0:T(8,128)}, f32[8,2048]{1,0:T(8,128)S(1)}, u32[]{:S(2)}) copy-start(f32[8,2048]{1,0:T(8,128)S(1)} %get-tuple-element.12.sin_ref) | copy-start | bytes 196612
  7.6 25.1 %copy-start.5 = (s32[128,27]{0,1:T(8,128)S(1)}, s32[128,27]{0,1:T(8,128)}, u32[]{:S(2)}) copy-start(s32[128,27]{0,1:T(8,128)} %param.12) | copy-start | bytes 41476
  7.6 25.1 %copy-start.6 = (s32[128,27]{0,1:T(8,128)S(1)}, s32[128,27]{0,1:T(8,128)}, u32[]{:S(2)}) copy-start(s32[128,27]{0,1:T(8,128)} %param.13) | copy-start | bytes 41476
  7.6 25.5 %copy-start.7 = (s32[128]{0:T(128)S(1)}, s32[128]{0:T(128)}, u32[]{:S(2)}) copy-start(s32[128]{0:T(128)} %param.14) | copy-start | bytes 1540
  9.2 34.6 %collective-permute-start.1 = (bf16[2,16,2048]{2,1,0:T(8,128)(2,1)S(1)}, bf16[2,16,2048]{2,1,0:T(8,128)(2,1)S(1)}, u32[]{:S(2)}, u32[]{:S(2)}) collective-permute-start(bf16[2,16,2048]{2,1,0:T(8,128)(2,1)S(1)} %pad_maximum_fusion.1), channel_id=1, source_target_pairs={{1,0},{2,1},{3,2},{4,3},{5,4},{6,5},{7,6},{8,7},{9,8},{10,9},{11,1... | collective-permute-start | bytes 393224 | tf_op jit(solution)/shard_map/ppermute | solution.py:112
  30.6 13.2 %collective-permute-start = (bf16[2,16,2048]{2,1,0:T(8,128)(2,1)S(1)}, bf16[2,16,2048]{2,1,0:T(8,128)(2,1)S(1)}, u32[]{:S(2)}, u32[]{:S(2)}) collective-permute-start(bf16[2,16,2048]{2,1,0:T(8,128)(2,1)S(1)} %pad_maximum_fusion.1), channel_id=1, source_target_pairs={{0,1},{1,2},{2,3},{3,4},{4,5},{5,6},{6,7},{7,8},{8,9},{9,10},{10,1... | collective-permute-start | bytes 393224 | tf_op jit(solution)/shard_map/ppermute | solution.py:111

commit v10 on v9

--- a/solution.py
+++ b/solution.py
@@ -5,7 +5,7 @@
 from jax.experimental import pallas as pl
 
 INTERPRET = False
-CHUNK = 1024
+CHUNK = 2048
 
 K_LOW = 1024
 REACH = 16

time: 58.3 us -> 59.1 us (1.014)
  Pallas kernels: 7.91 us -> 8.73 us
    pallas_call x1, Pallas kernels: 7.91 us -> 8.73 us  [translate(): pl.pallas_call(translate_kernel, out_shape=jax.ShapeDtypeStruct((2, rows...]
where the time goes in v10:
time: 59.1 us; the launch traced here: 58.9 us
  starting transfers between devices  23.4 us (40%)
  other arithmetic  16.2 us (27%)
  Pallas kernels  8.73 us (15%)
  matrix products  6.08 us (10%)
  local copies, waits for them, and re-layouts  4.23 us (7%)
    ppermute x1, starting transfers between devices, body(): after = lax.ppermute(parent[:, :REACH], axes, down)  21.3 us
    pallas_call x1, Pallas kernels, translate(): pl.pallas_call(translate_kernel, out_shape=jax.ShapeDtypeStruct((2, rows...  8.73 us
    convert_element_type x1, other arithmetic, split_parts(): high.astype(jnp.bfloat16)  5.4 us
    convert_element_type x1, other arithmetic, build_interp(): return dense.astype(jnp.bfloat16)  4.67 us
    dot_general x1, matrix products, body(): lax.dot_general(spread.reshape(-1, high_width), interp, contract, preferr...  3.79 us
    transpose x1, other arithmetic, translate(): ops = split_parts(translation).transpose(1, 0, 2)  3.23 us
    ppermute x1, starting transfers between devices, body(): before = lax.ppermute(parent[:, parents_here - REACH:], axes, up)  2.1 us
    transpose x1, local copies, waits for them, and re-layouts, body(): return result.reshape(2, -1, low_width).transpose(1, 0, 2)  1.78 us
  transfers between devices with their start and end apart: 2, of which 0 were waited for; matrix products, arithmetic and copies ran while one was open for 19% of the time, Pallas kernels for 0%

profile of v10, /device:TPU:14, one launch (start us, length us, event | category | flops | bytes accessed | tf_op | source)
XLA Modules:
  0.0 58.9 jit_solution(9069203717708014871)
XLA Ops:
  0.0 1.1 %fusion.16 = (f32[1,2048]{1,0:T(1,128)S(1)}, f32[1,2048]{1,0:T(1,128)S(1)}, f32[1,2048]{1,0:T(1,128)S(1)}, f32[1,2048]{1,0:T(1,128)S(1)}, f32[1,2048]{1,0:T(1,128)S(1)}, /*index=5*/f32[1,2048]{1,0:T(1,128)S(1)}) fusion(f32[6,2048]{1,0:T(8,128)} %bitcast.49), kind=kLoop, calls=%fused_computation.35 | loop fusion | bytes 98304 | tf_op jit(solution)/shard_map/slice | solution.py:19
  1.1 4.7 %select_convert_fusion = bf16[1024,2048]{1,0:T(8,128)(2,1)S(1)} fusion(f32[2048]{0:T(1024)S(1)} %bitcast.51, f32[2048]{0:T(1024)S(1)} %bitcast.52, f32[2048]{0:T(1024)S(1)} %bitcast.53, f32[2048]{0:T(1024)S(1)} %bitcast.54, f32[2048]{0:T(1024)S(1)} %bitcast.55, f32[2048]{0:T(1024)S(1)} %bitcast.50, s32[2048]{0:T(1024)} %param.10), kind=kLoop, calls=%fused_computation | loop fusion | flops 27262976 | bytes 4251648 | tf_op jit(solution)/shard_map/convert_element_type | solution.py:20
  5.8 0.7 %fusion.14 = (bf16[128,1,1024]{2,1,0:T(2,128)(2,1)S(1)}, bf16[128,1,1024]{2,1,0:T(2,128)(2,1)S(1)}) fusion(bf16[128,2,1024]{2,1,0:T(2,128)(2,1)S(1)} %copy-done.1), kind=kLoop, calls=%fused_computation.33 | loop fusion | bytes 1048576 | tf_op jit(solution)/shard_map/slice | solution.py:101
  6.6 0.2 fusion.15
  6.8 0.7 %convolution_bitcast_fusion.1 = f32[16,8,2048]{2,1,0:T(8,128)S(1)} fusion(bf16[1024,2048]{1,0:T(8,128)(2,1)S(1)} %select_convert_fusion, bf16[128,1,1024]{2,1,0:T(2,128)(2,1)S(1)} %get-tuple-element.9), kind=kOutput, calls=%fused_computation.15 | convolution fusion | flops 536870912 | bytes 5505024 | tf_op jit(solution)/shard_map/dot_general | solution.py:101
  7.6 0.0 copy-start.5
  7.6 0.0 copy-start.6
  7.6 1.5 %subtract_reduce_fusion = (bf16[16,2048]{1,0:T(8,128)(2,1)S(1)}, bf16[16,2048]{1,0:T(8,128)(2,1)S(1)}) fusion(f32[16,8,2048]{2,1,0:T(8,128)S(1)} %convolution_bitcast_fusion.1, f32[8,2048]{1,0:T(8,128)S(1)} %get-tuple-element.12.sin_ref, f32[8,2048]{1,0:T(8,128)S(1)} %get-tuple-element.11.cos_ref, bf16[1024,2048]{1,0:T(8,128)(2,1)S(1)} %select_convert_fusion, ...), kind=kOutput, calls=%fused_computation.19 | convolution fusion | flops 538902528 | bytes 5767168 | tf_op jit(solution)/shard_map/dot_general | solution.py:102
  9.2 21.3 %collective-permute-start.1 = (bf16[2,16,2048]{2,1,0:T(8,128)(2,1)S(1)}, bf16[2,16,2048]{2,1,0:T(8,128)(2,1)S(1)}, u32[]{:S(2)}, u32[]{:S(2)}) collective-permute-start(bf16[2,16,2048]{2,1,0:T(8,128)(2,1)S(1)} %pad_maximum_fusion.1), channel_id=1, source_target_pairs={{1,0},{2,1},{3,2},{4,3},{5,4},{6,5},{7,6},{8,7},{9,8},{10,9},{11,1... | collective-permute-start | bytes 393224 | tf_op jit(solution)/shard_map/ppermute | solution.py:112
  30.6 2.1 %collective-permute-start = (bf16[2,16,2048]{2,1,0:T(8,128)(2,1)S(1)}, bf16[2,16,2048]{2,1,0:T(8,128)(2,1)S(1)}, u32[]{:S(2)}, u32[]{:S(2)}) collective-permute-start(bf16[2,16,2048]{2,1,0:T(8,128)(2,1)S(1)} %pad_maximum_fusion.1), channel_id=1, source_target_pairs={{0,1},{1,2},{2,3},{3,4},{4,5},{5,6},{6,7},{7,8},{8,9},{9,10},{10,1... | collective-permute-start | bytes 393224 | tf_op jit(solution)/shard_map/ppermute | solution.py:111
  32.7 0.1 subtract_bitcast_fusion
  32.8 0.1 eq.66
  32.9 0.2 iota_compare_fusion
  33.0 0.1 eq.70
  33.1 0.1 dynamic_slice.11
  33.2 0.1 lt.30
  33.3 5.4 %reduce-precision_convert_fusion = (bf16[316,2,2048]{2,0,1:T(8,128)(2,1)S(1)}, bf16[316,2,2048]{2,0,1:T(8,128)(2,1)S(1)}) fusion(f32[316,2,2048]{2,1,0:T(2,128)} %param.15), kind=kLoop, calls=%fused_computation.9 | loop fusion | flops 5177344 | bytes 10354688 | tf_op jit(solution)/shard_map/convert_element_type | solution.py:86
  38.7 3.2 %maximum_bitcast_fusion.ops_ref = bf16[2,632,2048]{2,1,0:T(8,128)(2,1)} fusion(bf16[316,2,2048]{2,0,1:T(8,128)(2,1)S(1)} %get-tuple-element.8, bf16[316,2,2048]{2,0,1:T(8,128)(2,1)S(1)} %get-tuple-element.7), kind=kLoop, calls=%fused_computation.11 | loop fusion | flops 10354688 | bytes 10354688 | tf_op jit(solution)/shard_map/transpose | solution.py:63
  41.9 0.8 %fusion.13.pick_box_ref = bf16[432,48]{1,0:T(8,128)(2,1)} fusion(s32[432]{0:T(512)S(1)} %eq.70, pred[432]{0:T(512)(128)(4,1)S(1)} %lt.30), kind=kLoop, calls=%fused_computation.26 | loop fusion | flops 62208 | bytes 43632 | tf_op jit(solution)/shard_map/convert_element_type | solution.py:60
  42.8 1.0 %add_convert_fusion.pick_cls_ref = bf16[432,632]{1,0:T(8,128)(2,1)} fusion(pred[432,316]{1,0:T(8,128)(4,1)S(1)} %iota_compare_fusion), kind=kLoop, calls=%fused_computation.17 | loop fusion | flops 546048 | bytes 682560 | tf_op jit(solution)/shard_map/concatenate | solution.py:62
  43.8 0.8 %pad_maximum_fusion.win_ref = bf16[2,48,2048]{2,1,0:T(8,128)(2,1)} fusion(bf16[2,16,2048]{2,1,0:T(8,128)(2,1)S(1)} %collective-permute-done.1, bf16[1,16,2048]{2,1,0:T(8,128)(2,1)S(1)} %bitcast.48, bf16[1,16,2048]{2,1,0:T(8,128)(2,1)S(1)} %bitcast.46, bf16[2,16,2048]{2,1,0:T(8,128)(2,1)S(1)} %collective-permute-done), kind=kLoop, calls=%fused_computation.21 | loop fusion | flops 1572864 | bytes 786432 | tf_op jit(solution)/shard_map/concatenate | solution.py:113
  44.6 8.7 %shard_map.82 = bf16[2,128,2048]{2,1,0:T(8,128)(2,1)} custom-call(bf16[432,632]{1,0:T(8,128)(2,1)} %add_convert_fusion.pick_cls_ref, bf16[432,48]{1,0:T(8,128)(2,1)} %fusion.13.pick_box_ref, bf16[2,632,2048]{2,1,0:T(8,128)(2,1)} %maximum_bitcast_fusion.ops_ref, bf16[2,48,2048]{2,1,0:T(8,128)(2,1)} %pad_maximum_fusion.win_ref, f32[8,2048]{1,0:T(8,128)} %copy-done.2, ...), custom_call_target="tpu_custom_call" | custom-call | tf_op jit(solution)/shard_map/pallas_call | solution.py:66
  53.3 3.8 %fusion.9 = f32[128,2,1024]{2,0,1:T(8,128)S(1)} fusion(bf16[2,128,2048]{2,1,0:T(8,128)(2,1)} %shard_map.82, bf16[1024,2048]{1,0:T(8,128)(2,1)} %copy-done), kind=kOutput, calls=%fused_computation.16 | convolution fusion | flops 1073741824 | bytes 6291456 | tf_op jit(solution)/shard_map/dot_general | solution.py:123
  57.1 1.8 %copy.16 = f32[128,2,1024]{2,1,0:T(2,128)} copy(f32[128,2,1024]{2,0,1:T(8,128)S(1)} %fusion.9) | data formatting | bytes 2097152 | tf_op jit(solution)/shard_map/transpose | solution.py:126
  (18 shorter events, 0.1 us)
Async XLA Ops:
  0.0 5.8 %copy-start.1 = (bf16[128,2,1024]{2,1,0:T(2,128)(2,1)S(1)}, bf16[128,2,1024]{2,1,0:T(2,128)(2,1)}, u32[]{:S(2)}) copy-start(bf16[128,2,1024]{2,1,0:T(2,128)(2,1)} %param.8) | copy-start | bytes 1572868
  0.0 6.6 %copy-start.4 = (f32[8,2048]{1,0:T(8,128)S(1)}, f32[8,2048]{1,0:T(8,128)}, u32[]{:S(2)}) copy-start(f32[8,2048]{1,0:T(8,128)} %param.11) | copy-start | bytes 196612
  5.8 3.4 %copy-start = (bf16[1024,2048]{1,0:T(8,128)(2,1)}, bf16[1024,2048]{1,0:T(8,128)(2,1)S(1)}, u32[]{:S(2)}) copy-start(bf16[1024,2048]{1,0:T(8,128)(2,1)S(1)} %select_convert_fusion) | copy-start | bytes 12582916
  6.8 2.4 %copy-start.2 = (f32[8,2048]{1,0:T(8,128)}, f32[8,2048]{1,0:T(8,128)S(1)}, u32[]{:S(2)}) copy-start(f32[8,2048]{1,0:T(8,128)S(1)} %get-tuple-element.11.cos_ref) | copy-start | bytes 196612
  6.8 2.4 %copy-start.3 = (f32[8,2048]{1,0:T(8,128)}, f32[8,2048]{1,0:T(8,128)S(1)}, u32[]{:S(2)}) copy-start(f32[8,2048]{1,0:T(8,128)S(1)} %get-tuple-element.12.sin_ref) | copy-start | bytes 196612
  7.6 25.1 %copy-start.5 = (s32[128,27]{0,1:T(8,128)S(1)}, s32[128,27]{0,1:T(8,128)}, u32[]{:S(2)}) copy-start(s32[128,27]{0,1:T(8,128)} %param.12) | copy-start | bytes 41476
  7.6 25.1 %copy-start.6 = (s32[128,27]{0,1:T(8,128)S(1)}, s32[128,27]{0,1:T(8,128)}, u32[]{:S(2)}) copy-start(s32[128,27]{0,1:T(8,128)} %param.13) | copy-start | bytes 41476
  7.6 25.5 %copy-start.7 = (s32[128]{0:T(128)S(1)}, s32[128]{0:T(128)}, u32[]{:S(2)}) copy-start(s32[128]{0:T(128)} %param.14) | copy-start | bytes 1540
  9.2 34.6 %collective-permute-start.1 = (bf16[2,16,2048]{2,1,0:T(8,128)(2,1)S(1)}, bf16[2,16,2048]{2,1,0:T(8,128)(2,1)S(1)}, u32[]{:S(2)}, u32[]{:S(2)}) collective-permute-start(bf16[2,16,2048]{2,1,0:T(8,128)(2,1)S(1)} %pad_maximum_fusion.1), channel_id=1, source_target_pairs={{1,0},{2,1},{3,2},{4,3},{5,4},{6,5},{7,6},{8,7},{9,8},{10,9},{11,1... | collective-permute-start | bytes 393224 | tf_op jit(solution)/shard_map/ppermute | solution.py:112
  30.6 13.2 %collective-permute-start = (bf16[2,16,2048]{2,1,0:T(8,128)(2,1)S(1)}, bf16[2,16,2048]{2,1,0:T(8,128)(2,1)S(1)}, u32[]{:S(2)}, u32[]{:S(2)}) collective-permute-start(bf16[2,16,2048]{2,1,0:T(8,128)(2,1)S(1)} %pad_maximum_fusion.1), channel_id=1, source_target_pairs={{0,1},{1,2},{2,3},{3,4},{4,5},{5,6},{6,7},{7,8},{8,9},{9,10},{10,1... | collective-permute-start | bytes 393224 | tf_op jit(solution)/shard_map/ppermute | solution.py:111
